TPU v7x, 256 devices: a whole 4x4x8 slice. The times are simulated.
256 devices in a mesh: wide: 64 (over y, z, core), col: 4 (over x).
Axes of the slice: x: 4, y: 4, z: 8, core: 2. Of those that a mesh axis runs over, the one named last changes fastest.
Arguments:
- assembled: float32 [9216, 1024], P(('wide', 'col')), as said below
- row_map: int32 [9216], P(('wide', 'col')), may hold values from 0 to 9215, as said below
- fill_pattern: int32 [2, 32], replicated, may hold values from 0 to 1
- trailing_block: float32 [64, 4, 32, 8192], P(None, 'col', None, 'wide'), may hold values from -6 to 6
Outputs:
- schur: float32 [64, 4, 32, 8192], P(None, 'col', None, 'wide')
- panel_rows: float32 [8192, 1024], P(('wide', 'col'))
- diag_factor: float32 [1024, 1024], P(('wide', 'col'))
Inputs may be any that keep to these rules, and one draw needn't show every extreme that they name: row_map is a permutation of the window rows. Each device, with col index c, holds exactly 32 trailing rows 1024 + t whose owner device index t // 32 has col index c, and exactly 4 rows d below 1024 with d // 256 equal to c. At most 2 of one device's trailing rows have the same owner, and every device holds exactly 2 trailing rows of some owner. `assembled`: D is symmetric positive definite.
All inputs are finite; a program needn't handle non-finite values.
Results may differ from a plain program's by a relative error of at most 0.00008.
Values sent between devices are 32-bit elements; how exact they have to be, the bound alone decides.
No kernel may reach another device: no remote copies, remote signals or barrier semaphores. Data moves between devices by JAX's collectives and lax.ppermute only.
A program may use at most 128 MiB of HBM per device.

v0:
```python
import jax
import jax.numpy as jnp
from jax import lax
from jax.sharding import PartitionSpec as P

BLOCK = 256


highest = lax.Precision.HIGHEST
far_index = 1 << 30


def from_root(value, axis, source):
    kept = jnp.where(lax.axis_index(axis) == source, value, 0).astype(value.dtype)
    return lax.psum(kept, axis)


def lower_inverse(lower_factor):
    order_size = lower_factor.shape[0]
    identity = jnp.eye(order_size, dtype=lower_factor.dtype)
    return lax.linalg.triangular_solve(lower_factor, identity, left_side=True, lower=True)


def contract_rows(left_rows, right_rows):
    return lax.dot_general(left_rows, right_rows, (((1,), (1,)), ((), ())), precision=highest)


def regroup(rows_in, target_wide, target_slot, active, capacity, wide_count, place_count):
    onehot = (target_wide[:, None] == jnp.arange(wide_count)[None, :]).astype(jnp.int32) * active[
        :, None
    ]
    before = jnp.cumsum(onehot, axis=0) - onehot
    position = jnp.sum(before * onehot, axis=1)
    overflow = wide_count * capacity
    slot_ids = jnp.where(active > 0, target_wide * capacity + position, overflow)
    buffer = (
        jnp.zeros((overflow, rows_in.shape[1]), rows_in.dtype)
        .at[slot_ids]
        .set(rows_in, mode="drop")
    )
    labels = jnp.full((overflow,), far_index, jnp.int32).at[slot_ids].set(target_slot, mode="drop")
    buffer = buffer.reshape(wide_count, capacity, rows_in.shape[1])
    labels = labels.reshape(wide_count, capacity)
    arrived, arrived_ids = (
        lax.all_to_all(buffer, "wide", split_axis=0, concat_axis=0, tiled=True),
        lax.all_to_all(labels, "wide", split_axis=0, concat_axis=0, tiled=True),
    )
    arrived = arrived.reshape(wide_count * capacity, rows_in.shape[1])
    arrived_ids = arrived_ids.reshape(-1)
    return (
        jnp.zeros((place_count, rows_in.shape[1]), rows_in.dtype)
        .at[arrived_ids]
        .set(arrived, mode="drop")
    )


def schur_update(target, panel_part):
    range_part = lax.all_gather(panel_part, "col", axis=0, tiled=True)
    update = contract_rows(lax.all_gather(panel_part, "wide", axis=0, tiled=True), range_part)
    return target - update.reshape(target.shape)


def local(assembled, row_map, fill_pattern, trailing_block):
    wide_count = lax.axis_size("wide")
    col_count = lax.axis_size("col")
    twice_width = assembled.shape[1]
    half_width = twice_width // 2
    trail_rows = trailing_block.shape[2]
    diag_share = twice_width // (col_count * wide_count)
    slot_limit = max(2, 2 * trail_rows // wide_count)
    wide_index = lax.axis_index("wide")
    col_index = lax.axis_index("col")
    device_index = wide_index * col_count + col_index
    is_diagonal = row_map < twice_width
    trail_id = jnp.maximum(row_map - twice_width, 0)
    owner_device = trail_id // trail_rows
    owner_wide = owner_device // col_count
    local_trail = trail_id % trail_rows
    block_ids = (device_index * trail_rows + jnp.arange(trail_rows)) // BLOCK
    block_hits = (block_ids[:, None] == jnp.arange(fill_pattern.shape[1])[None, :]).astype(
        jnp.int32
    )
    first_flags = jnp.sum(block_hits * fill_pattern[0][None, :], axis=1)
    second_flags = jnp.sum(block_hits * fill_pattern[1][None, :], axis=1)
    column_first = jnp.arange(twice_width) < half_width
    keep = jnp.where(column_first[None, :], first_flags[:, None], second_flags[:, None]).astype(
        jnp.float32
    )
    active = jnp.where(is_diagonal, 0, 1)
    trail_local = (
        regroup(assembled, owner_wide, local_trail, active, slot_limit, wide_count, trail_rows)
        * keep
    )
    order_ids = jnp.argsort(jnp.where(is_diagonal, 0, 1), stable=True)[:diag_share]
    diag_local = assembled[order_ids]
    diag_ids = row_map[order_ids]
    all_rows, all_ids = (
        lax.all_gather(diag_local, ("wide", "col"), axis=0, tiled=True),
        lax.all_gather(diag_ids, ("wide", "col"), axis=0, tiled=True),
    )
    gathered = jnp.zeros((twice_width, twice_width), jnp.float32).at[all_ids].set(all_rows)
    symmetric_all = (gathered + gathered.T) * 0.5
    identity = jnp.eye(twice_width, dtype=jnp.float32)
    symmetric = jnp.where(wide_index == 0, symmetric_all, identity)
    factor = jnp.linalg.cholesky(symmetric)
    factor = from_root(factor, "wide", 0)
    inverse = lower_inverse(factor)
    panel = contract_rows(trail_local, inverse)
    schur = schur_update(trailing_block, panel)
    factor_rows = lax.dynamic_slice_in_dim(factor, device_index * diag_share, diag_share, 0)
    return (schur, panel, factor_rows)


def solution(mesh):
    in_specs = (P(("wide", "col"), None), P(("wide", "col")), P(), P(None, "col", None, "wide"))
    out_specs = (P(None, "col", None, "wide"), P(("wide", "col"), None), P(("wide", "col"), None))
    return jax.shard_map(local, mesh=mesh, in_specs=in_specs, out_specs=out_specs, check_vma=False)
```

profile of v0, /device:TPU:1, one launch (start us, length us, event | category | flops | bytes accessed | tf_op | source)
XLA Modules:
  0.0 809.7 jit_solution(847354889389539363)
XLA Ops:
  7.9 2.0 sort.17
  9.9 2.1 gather_fusion.1
  13.6 81.9 %all-reduce.1 = s32[1024]{0:T(1024)S(1)} all-reduce(s32[1024]{0:T(1024)S(1)} %dynamic-update-slice.47), channel_id=2, replica_groups=mesh['wide'=64,'col'=4] {'wide','col'}, use_global_device_ids=true, to_apply=%add.1 | all-reduce | flops 1024 | bytes 8192
  95.5 36.7 %all-gather.8.cloned.1.call-done = f32[256,4,1024]{2,1,0:T(4,128)} async-done(((f32[1,4,1024]{2,1,0:T(4,128)}), f32[256,4,1024]{2,1,0:T(4,128)}) %all-gather.8.cloned.1.call-update) | async-done | bytes 4194320 | tf_op jit(solution)/shard_map/all_gather | solution.py:98
  132.2 5.3 reshape.230
  137.5 8.0 scatter_custom_fusion.3
  145.5 5.3 copy.18
  150.9 6.9 fusion.2
  157.8 5.5 copy.19
  163.3 4.4 fusion
  167.8 1.9 copy-done.2
  169.7 11.7 %cholesky.222 = f32[128,128]{1,0:T(8,128)S(1)} custom-call(f32[128,128]{1,0:T(8,128)S(1)} %cholesky.577), custom_call_target="Cholesky" | custom-call | tf_op jit(solution)/shard_map/jit(cholesky)/cholesky | solution.py:105
  181.5 2.5 cholesky.254
  184.0 9.8 %custom-call.62 = f32[1,128,128]{1,2,0:T(8,128)S(1)} custom-call(f32[1,128,128]{2,1,0:T(8,128)S(1)} %get-tuple-element.71), custom_call_target="InvertDiagBlocksLowerTriangular" | custom-call | tf_op jit(solution)/shard_map/jit(cholesky)/cholesky | solution.py:105
  193.8 2.4 constant_dynamic-update-slice_fusion.32
  196.2 1.5 convolution_subtract_fusion.5
  197.7 12.1 %cholesky.243 = f32[128,128]{1,0:T(8,128)S(1)} custom-call(f32[128,128]{1,0:T(8,128)S(1)} %cholesky.581), custom_call_target="Cholesky" | custom-call | tf_op jit(solution)/shard_map/jit(cholesky)/cholesky | solution.py:105
  210.5 9.8 %custom-call.63 = f32[1,128,128]{1,2,0:T(8,128)S(1)} custom-call(f32[1,128,128]{2,1,0:T(8,128)S(1)} %get-tuple-element.68), custom_call_target="InvertDiagBlocksLowerTriangular" | custom-call | tf_op jit(solution)/shard_map/jit(cholesky)/cholesky | solution.py:105
  221.5 2.1 convolution_subtract_fusion.6
  223.6 11.7 %cholesky.466 = f32[128,128]{1,0:T(8,128)S(1)} custom-call(f32[128,128]{1,0:T(8,128)S(1)} %cholesky.586), custom_call_target="Cholesky" | custom-call | tf_op jit(solution)/shard_map/jit(cholesky)/cholesky | solution.py:105
  236.6 9.8 %custom-call.64 = f32[1,128,128]{1,2,0:T(8,128)S(1)} custom-call(f32[1,128,128]{2,1,0:T(8,128)S(1)} %get-tuple-element.65), custom_call_target="InvertDiagBlocksLowerTriangular" | custom-call | tf_op jit(solution)/shard_map/jit(cholesky)/cholesky | solution.py:105
  247.6 2.3 convolution_subtract_fusion.7
  249.9 11.9 %cholesky.485 = f32[128,128]{1,0:T(8,128)S(1)} custom-call(f32[128,128]{1,0:T(8,128)S(1)} %cholesky.591), custom_call_target="Cholesky" | custom-call | tf_op jit(solution)/shard_map/jit(cholesky)/cholesky | solution.py:105
  263.1 9.8 %custom-call.65 = f32[1,128,128]{1,2,0:T(8,128)S(1)} custom-call(f32[1,128,128]{2,1,0:T(8,128)S(1)} %get-tuple-element.62), custom_call_target="InvertDiagBlocksLowerTriangular" | custom-call | tf_op jit(solution)/shard_map/jit(cholesky)/cholesky | solution.py:105
  274.0 2.3 convolution_subtract_fusion.8
  276.3 11.7 %cholesky.504 = f32[128,128]{1,0:T(8,128)S(1)} custom-call(f32[128,128]{1,0:T(8,128)S(1)} %cholesky.596), custom_call_target="Cholesky" | custom-call | tf_op jit(solution)/shard_map/jit(cholesky)/cholesky | solution.py:105
  289.3 10.2 %custom-call.66 = f32[1,128,128]{1,2,0:T(8,128)S(1)} custom-call(f32[1,128,128]{2,1,0:T(8,128)S(1)} %get-tuple-element.59), custom_call_target="InvertDiagBlocksLowerTriangular" | custom-call | tf_op jit(solution)/shard_map/jit(cholesky)/cholesky | solution.py:105
  300.5 2.3 convolution_subtract_fusion.9
  302.8 11.7 %cholesky.524 = f32[128,128]{1,0:T(8,128)S(1)} custom-call(f32[128,128]{1,0:T(8,128)S(1)} %cholesky.601), custom_call_target="Cholesky" | custom-call | tf_op jit(solution)/shard_map/jit(cholesky)/cholesky | solution.py:105
  315.8 9.8 %custom-call.67 = f32[1,128,128]{1,2,0:T(8,128)S(1)} custom-call(f32[1,128,128]{2,1,0:T(8,128)S(1)} %get-tuple-element.56), custom_call_target="InvertDiagBlocksLowerTriangular" | custom-call | tf_op jit(solution)/shard_map/jit(cholesky)/cholesky | solution.py:105
  326.6 2.0 convolution_subtract_fusion.10
  328.6 11.9 %cholesky.544 = f32[128,128]{1,0:T(8,128)S(1)} custom-call(f32[128,128]{1,0:T(8,128)S(1)} %cholesky.606), custom_call_target="Cholesky" | custom-call | tf_op jit(solution)/shard_map/jit(cholesky)/cholesky | solution.py:105
  341.8 9.8 %custom-call.68 = f32[1,128,128]{1,2,0:T(8,128)S(1)} custom-call(f32[1,128,128]{2,1,0:T(8,128)S(1)} %get-tuple-element.53), custom_call_target="InvertDiagBlocksLowerTriangular" | custom-call | tf_op jit(solution)/shard_map/jit(cholesky)/cholesky | solution.py:105
  352.4 1.8 convolution_subtract_fusion.11
  354.2 11.7 %cholesky.562 = f32[128,128]{1,0:T(8,128)S(1)} custom-call(f32[128,128]{1,0:T(8,128)S(1)} %convolution_subtract_fusion.11), custom_call_target="Cholesky" | custom-call | tf_op jit(solution)/shard_map/jit(cholesky)/cholesky | solution.py:105
  372.9 4.8 select_select_fusion
  379.9 7.8 all-to-all-start
  390.1 6.9 all-to-all-done
  396.9 4.7 all-to-all-start.1
  402.3 2.5 fusion.20
  406.2 14.5 %all-to-all-done.1 = f32[64,2,1024]{2,1,0:T(2,128)S(1)} async-done(((f32[64,2,1024]{2,1,0:T(2,128)}), f32[64,2,1024]{2,1,0:T(2,128)S(1)}, u32[]{:S(2)}, u32[]{:S(2)}) %all-to-all-start.1) | async-done | bytes 524320 | tf_op jit(solution)/shard_map/all_to_all | solution.py:45
  422.1 152.6 %all-reduce.4.cloned.1.call-done = f32[1024,1024]{1,0:T(8,128)} async-done(((f32[1024,1024]{1,0:T(8,128)}), f32[1024,1024]{1,0:T(8,128)}) %all-reduce.4.cloned.1.call-update) | async-done | bytes 4194320 | tf_op jit(solution)/shard_map/psum | solution.py:15
  574.7 4.7 fusion.3
  579.4 23.2 %while.1 = (s32[]{:T(128)}, f32[1024,1024]{1,0:T(8,128)}, s32[8,2]{0,1:T(2,128)S(1)}, f32[8,128,128]{2,1,0:T(8,128)S(1)}, s32[]{:T(128)}) while((s32[]{:T(128)}, f32[1024,1024]{1,0:T(8,128)}, s32[8,2]{0,1:T(2,128)S(1)}, f32[8,128,128]{2,1,0:T(8,128)S(1)}, s32[]{:T(128)}) %tuple.65), condition=%wide.while_cond, body=%wide.while_body.sunk | while | flops 2 | bytes 131189 | solution.py:21
  580.0 2.3 bitcast_dynamic-update-slice_fusion.2
  582.9 2.3 bitcast_dynamic-update-slice_fusion.2
  585.8 2.3 bitcast_dynamic-update-slice_fusion.2
  588.7 2.3 bitcast_dynamic-update-slice_fusion.2
  591.6 2.3 bitcast_dynamic-update-slice_fusion.2
  594.5 2.3 bitcast_dynamic-update-slice_fusion.2
  597.4 2.3 bitcast_dynamic-update-slice_fusion.2
  600.3 2.2 bitcast_dynamic-update-slice_fusion.2
  602.6 78.8 %custom-call.69 = f32[8,128,128]{1,2,0:T(8,128)S(1)} custom-call(f32[8,128,128]{2,1,0:T(8,128)S(1)} %get-tuple-element.12), custom_call_target="InvertDiagBlocksLowerTriangular" | custom-call | tf_op jit(solution)/shard_map/triangular_solve | solution.py:21
  681.9 1.9 convolution_subtract_fusion.4
  684.6 1.6 convolution_subtract_fusion
  687.0 2.0 fusion.21
  689.8 2.3 fusion.24
  692.8 2.6 convolution_subtract_fusion.2
  696.1 2.8 convolution_subtract_fusion.1
  699.6 3.5 convolution_subtract_fusion.3
  703.7 4.7 fusion.58
  709.8 10.5 %all_gather.15 = f32[128,1024]{1,0:T(8,128)S(1)} all-gather(f32[32,1024]{1,0:T(8,128)} %fusion.58), channel_id=1, replica_groups=mesh['wide'=64,'col'=4] {'col'}, dimensions={0}, use_global_device_ids=true | all-gather | bytes 655360 | tf_op jit(solution)/shard_map/all_gather | solution.py:58
  720.3 72.2 %all-gather.6.cloned.1.call-done = f32[2048,1024]{1,0:T(8,128)} async-done(((f32[32,1024]{1,0:T(8,128)}), f32[2048,1024]{1,0:T(8,128)}) %all-gather.6.cloned.1.call-update) | async-done | bytes 8388624 | tf_op jit(solution)/shard_map/all_gather | solution.py:59
  792.5 9.0 %fusion.92 = f32[2048,128]{1,0:T(8,128)S(1)} fusion(f32[2048,1024]{1,0:T(8,128)} %all-gather.6.cloned.1.call-done, f32[128,1024]{1,0:T(8,128)S(1)} %all_gather.15), kind=kOutput, calls=%fused_computation.214 | convolution fusion | flops 3221225472 | bytes 9961472 | tf_op jit(solution)/shard_map/dot_general | solution.py:25
  (99 shorter events, 38.2 us)
Async XLA Ops:
  7.2 125.1 %all-gather.8.cloned.1.call-start = ((), (), s32[]{:S(2)}) async-start(), calls=%async_computation.4 | async-start | bytes 4210688 | tf_op jit(solution)/shard_map/all_gather | solution.py:98
  12.1 562.6 %all-reduce.4.cloned.1.call-start = ((), (), s32[]{:S(2)}) async-start(), calls=%async_computation.2 | async-start | bytes 8388608 | tf_op jit(solution)/shard_map/psum | solution.py:15
  167.8 1.9 copy-start.2
  377.8 0.7 copy-start
  377.8 24.0 %copy-start.4 = (s32[2,32]{1,0:T(2,128)S(1)}, s32[2,32]{1,0:T(2,128)}, u32[]{:S(2)}) copy-start(s32[2,32]{1,0:T(2,128)} %param.6) | copy-start | bytes 772
  379.9 17.1 %all-to-all-start = ((s32[64,1,2]{2,1,0:T(1,128)}), s32[64,1,2]{2,1,0:T(1,128)S(1)}, u32[]{:S(2)}, u32[]{:S(2)}) async-start(s32[64,1,2]{2,1,0:T(1,128)} %bitcast), calls=%async_computation | async-start | bytes 65536 | tf_op jit(solution)/shard_map/all_to_all | solution.py:46
  396.9 23.7 %all-to-all-start.1 = ((f32[64,2,1024]{2,1,0:T(2,128)}), f32[64,2,1024]{2,1,0:T(2,128)S(1)}, u32[]{:S(2)}, u32[]{:S(2)}) async-start(f32[64,2,1024]{2,1,0:T(2,128)} %reshape.146), calls=%async_computation.1 | async-start | bytes 1048576 | tf_op jit(solution)/shard_map/all_to_all | solution.py:45
  401.7 390.8 %all-gather.6.cloned.1.call-start = ((), (), s32[]{:S(2)}) async-start(), calls=%async_computation.3 | async-start | bytes 8519680 | tf_op jit(solution)/shard_map/all_gather | solution.py:59
  681.4 3.2 copy-start.1
  720.3 81.3 %copy-start.3 = (f32[64,1,32,128]{3,2,1,0:T(8,128)S(1)}, f32[64,1,32,128]{3,2,1,0:T(8,128)}, u32[]{:S(2)}) copy-start(f32[64,1,32,128]{3,2,1,0:T(8,128)} %param.7) | copy-start | bytes 3145732
Sparse Core Ops, SparseCore 0:
  12.2 119.9 all-gather.7
  377.9 196.7 all-reduce.3
  708.5 83.9 all-gather.5
where the time goes:
time: 816 us; the launch traced here: 810 us
  waiting for transfers between devices  283 us (35%)
  other arithmetic  280 us (34%)
  blocking collectives  92.4 us (11%)
  local copies, waits for them, and re-layouts  62.8 us (8%)
  matrix products  59 us (7%)
  between operations  19.7 us (2%)
  starting transfers between devices  12.7 us (2%)
    another operation x30, other arithmetic, local(): factor = jnp.linalg.cholesky(symmetric)  172 us
    psum x1, waiting for transfers between devices, from_root(): return lax.psum(kept, axis)  153 us
    another operation x3, other arithmetic, lower_inverse(): lax.linalg.triangular_solve(lower_factor, identity, left_side=True, lower...  83.5 us
    unnamed x1, blocking collectives  81.9 us
    all_gather x1, waiting for transfers between devices, schur_update(): lax.all_gather(panel_part, 'wide', axis=0, tiled=True)  72.2 us
    all_gather x1, waiting for transfers between devices, local(): lax.all_gather(diag_local, ('wide', 'col'), axis=0, tiled=True)  36.7 us
    another operation x14, matrix products, local(): factor = jnp.linalg.cholesky(symmetric)  23.1 us
    another operation x24, local copies, waits for them, and re-layouts  23 us
  transfers between devices with their start and end apart: 5, of which 5 were waited for; matrix products, arithmetic and copies ran while one was open for 1% of the time, Pallas kernels for 0%

commit v1 on v0

v1 whole, which is shorter than its diff:
```python
import jax
import jax.numpy as jnp
from jax import lax
from jax.sharding import PartitionSpec as P

BLOCK = 256

highest = lax.Precision.HIGHEST


def lower_inverse(lower_factor):
    order_size = lower_factor.shape[0]
    identity = jnp.eye(order_size, dtype=lower_factor.dtype)
    return lax.linalg.triangular_solve(lower_factor, identity, left_side=True, lower=True)


def contract_rows(left_rows, right_rows):
    return lax.dot_general(left_rows, right_rows, (((1,), (1,)), ((), ())), precision=highest)


def local(assembled, row_map, fill_pattern, trailing_block):
    wide_count = lax.axis_size("wide")
    col_count = lax.axis_size("col")
    asm_rows, twice_width = assembled.shape
    half_width = twice_width // 2
    trail_rows = trailing_block.shape[2]
    diag_share = twice_width // (col_count * wide_count)
    diag_col = twice_width // col_count
    wide_index = lax.axis_index("wide")
    col_index = lax.axis_index("col")
    device_index = wide_index * col_count + col_index

    packed_rows = ((asm_rows + 1 + 7) // 8) * 8
    id_row = jnp.zeros((twice_width,), jnp.float32).at[:asm_rows].set(row_map.astype(jnp.float32))
    packed = jnp.concatenate(
        [assembled, id_row[None, :], jnp.zeros((packed_rows - asm_rows - 1, twice_width), jnp.float32)],
        axis=0,
    )
    gathered = lax.all_gather(packed, "wide", axis=0, tiled=True)
    gathered3 = gathered.reshape(wide_count, packed_rows, twice_width)
    ids = gathered3[:, asm_rows, :asm_rows].astype(jnp.int32).reshape(-1)
    source = (
        jnp.arange(wide_count)[:, None] * packed_rows + jnp.arange(asm_rows)[None, :]
    ).reshape(-1)

    is_diagonal = ids < twice_width
    diag_slot = jnp.where(is_diagonal, ids - diag_col * col_index, diag_col)
    diag_src = jnp.zeros((diag_col,), jnp.int32).at[diag_slot].set(source, mode="drop")
    diag_block = gathered[diag_src]
    full = lax.all_gather(diag_block, "col", axis=0, tiled=True)

    trail_id = ids - twice_width
    owner_wide = trail_id // (trail_rows * col_count)
    trail_slot = jnp.where(is_diagonal, wide_count * trail_rows, owner_wide * trail_rows + trail_id % trail_rows)
    trail_src = jnp.zeros((wide_count * trail_rows,), jnp.int32).at[trail_slot].set(source, mode="drop")
    trail_all = gathered[trail_src]
    row_global = (
        (jnp.arange(wide_count)[:, None] * col_count + col_index) * trail_rows
        + jnp.arange(trail_rows)[None, :]
    ).reshape(-1)
    block_ids = row_global // BLOCK
    first_flags = fill_pattern[0][block_ids]
    second_flags = fill_pattern[1][block_ids]
    column_first = jnp.arange(twice_width) < half_width
    keep = jnp.where(column_first[None, :], first_flags[:, None], second_flags[:, None]).astype(jnp.float32)
    masked_all = trail_all * keep
    masked_own = lax.dynamic_slice_in_dim(masked_all, wide_index * trail_rows, trail_rows, 0)
    masked_range = lax.all_gather(masked_own, "col", axis=0, tiled=True)

    symmetric = (full + full.T) * 0.5
    factor = jnp.linalg.cholesky(symmetric)
    inverse = lower_inverse(factor)
    panel = contract_rows(masked_own, inverse)
    range_panel = contract_rows(masked_range, inverse)
    range_back = lax.dot_general(range_panel, inverse, (((1,), (0,)), ((), ())), precision=highest)
    update = contract_rows(masked_all, range_back)
    schur = trailing_block - update.reshape(trailing_block.shape)
    factor_rows = lax.dynamic_slice_in_dim(factor, device_index * diag_share, diag_share, 0)
    return (schur, panel, factor_rows)


def solution(mesh):
    in_specs = (P(("wide", "col"), None), P(("wide", "col")), P(), P(None, "col", None, "wide"))
    out_specs = (P(None, "col", None, "wide"), P(("wide", "col"), None), P(("wide", "col"), None))
    return jax.shard_map(local, mesh=mesh, in_specs=in_specs, out_specs=out_specs, check_vma=False)
```

time: 816 us -> 607 us (0.74)
  waiting for transfers between devices: 283 us -> 91.7 us
  blocking collectives: 92.4 us -> 11 us
  other arithmetic: 280 us -> 322 us
  local copies, waits for them, and re-layouts: 62.8 us -> 88 us
  starting transfers between devices: 12.7 us -> 0.08 us
    psum x1 -> x0, waiting for transfers between devices: 153 us -> none  [from_root(): return lax.psum(kept, axis)]
    unnamed x1 -> x0, blocking collectives: 81.9 us -> none
    gather x1 -> x7, other arithmetic: 0.01 us -> 40.5 us  [the longest x3 20.6 us: local(): first_flags = fill_pattern[0][block_ids]]
    gather x2 -> x7, local copies, waits for them, and re-layouts: 3.38 us -> 25.4 us  [the longest x1 15.7 us: local(): trail_all = gathered[trail_src]]
    all_to_all x2 -> x0, waiting for transfers between devices: 21.4 us -> none  [the longest x1 14.5 us: regroup(): lax.all_to_all(buffer, 'wide', split_axis=0, concat_axis=0, tiled=True)]
    all_gather x2, waiting for transfers between devices: 109 us -> 91.7 us  [the longest x1 91.7 us: local(): gathered = lax.all_gather(packed, 'wide', axis=0, tiled=True)]
    all_to_all x2 -> x0, starting transfers between devices: 12.5 us -> none  [the longest x1 7.81 us: regroup(): lax.all_to_all(labels, 'wide', split_axis=0, concat_axis=0, tiled=True)]
    select_n x8 -> x2, other arithmetic: 12.5 us -> 0.14 us  [the longest x1 0.13 us: local(): jnp.zeros((diag_col,), jnp.int32).at[diag_slot].set(source, mode='drop')]
  transfers between devices with their start and end apart: 5 -> 2, of which waited for: 5 -> 1; matrix products, arithmetic and copies ran while one was open for 1% -> 13% of each run, Pallas kernels for 0% -> 0%
where the time goes in v1:
time: 607 us; the launch traced here: 597 us
  other arithmetic  322 us (53%)
  waiting for transfers between devices  91.7 us (15%)
  local copies, waits for them, and re-layouts  88 us (14%)
  matrix products  64 us (11%)
  between operations  20.1 us (3%)
  blocking collectives  11 us (2%)
    another operation x30, other arithmetic, local(): factor = jnp.linalg.cholesky(symmetric)  173 us
    all_gather x1, waiting for transfers between devices, local(): gathered = lax.all_gather(packed, 'wide', axis=0, tiled=True)  91.7 us
    another operation x3, other arithmetic, lower_inverse(): lax.linalg.triangular_solve(lower_factor, identity, left_side=True, lower...  85.4 us
    another operation x14, matrix products, local(): factor = jnp.linalg.cholesky(symmetric)  23.1 us
    another operation x24, local copies, waits for them, and re-layouts  23 us
    another operation x15, matrix products, lower_inverse(): lax.linalg.triangular_solve(lower_factor, identity, left_side=True, lower...  22.2 us
    gather x3, other arithmetic, local(): first_flags = fill_pattern[0][block_ids]  20.6 us
    gather x2, other arithmetic, local(): second_flags = fill_pattern[1][block_ids]  19.9 us
  transfers between devices with their start and end apart: 2, of which 1 were waited for; matrix products, arithmetic and copies ran while one was open for 13% of the time, Pallas kernels for 0%

profile of v1, /device:TPU:1, one launch (start us, length us, event | category | flops | bytes accessed | tf_op | source)
XLA Modules:
  0.0 596.8 jit_solution(17203450287779156365)
XLA Ops:
  7.9 1.7 fusion.50
  9.9 91.7 %all-gather.4.cloned.1.call-done = f32[2560,1024]{1,0:T(8,128)} async-done(((f32[40,1024]{1,0:T(8,128)}), f32[2560,1024]{1,0:T(8,128)}) %all-gather.4.cloned.1.call-update) | async-done | bytes 10485776 | tf_op jit(solution)/shard_map/all_gather | solution.py:39
  103.0 9.0 %scatter_custom_fusion.1 = s32[256]{0:T(256)S(1)} fusion(s32[2304]{0:T(1024)S(1)} %get-tuple-element.23, s32[2304]{0:T(1024)S(1)} %reshape.468, s32[]{:T(128)} %copy.61), kind=kCustom, calls=%fused_computation.238 | custom fusion | bytes 1028 | tf_op jit(solution)/shard_map/scatter | solution.py:48
  112.1 5.6 gather_fusion.1
  122.0 4.6 compare_select_fusion.7
  127.6 2.5 fusion.23
  130.1 4.2 compare_select_fusion.8
  134.3 15.6 %select_select_fusion.1 = s32[2048]{0:T(1024)S(1)} fusion(pred[2048]{0:T(1024)(128)(4,1)S(1)} %get-tuple-element.49, pred[2048]{0:T(1024)(128)(4,1)S(1)} %get-tuple-element.48, pred[2048]{0:T(1024)(128)(4,1)S(1)} %get-tuple-element.47, pred[2048]{0:T(1024)(128)(4,1)S(1)} %get-tuple-element.46, pred[2048]{0:T(1024)(128)(4,1)S(1)} %get-tuple-element.45, ...), kind=kLoop, calls=%fused_computation.212 | loop fusion | flops 51200 | bytes 67684 | tf_op jit(solution)/shard_map/gather | solution.py:63
  150.0 15.5 %select_select_fusion.2 = s32[2048]{0:T(1024)S(1)} fusion(pred[2048]{0:T(1024)(128)(4,1)S(1)} %get-tuple-element.49, pred[2048]{0:T(1024)(128)(4,1)S(1)} %get-tuple-element.48, pred[2048]{0:T(1024)(128)(4,1)S(1)} %get-tuple-element.47, pred[2048]{0:T(1024)(128)(4,1)S(1)} %get-tuple-element.46, pred[2048]{0:T(1024)(128)(4,1)S(1)} %get-tuple-element.45, ...), kind=kLoop, calls=%fused_computation.213 | loop fusion | flops 51200 | bytes 67684 | tf_op jit(solution)/shard_map/gather | solution.py:62
  165.4 9.0 %scatter_custom_fusion = s32[2048]{0:T(1024)S(1)} fusion(s32[2304]{0:T(1024)S(1)} %get-tuple-element.24, s32[2304]{0:T(1024)S(1)} %reshape.468, s32[]{:T(128)} %copy.61), kind=kCustom, calls=%fused_computation.216 | custom fusion | bytes 8196 | tf_op jit(solution)/shard_map/scatter | solution.py:55
  174.4 15.7 %gather_fusion = f32[2048,1024]{1,0:T(8,128)} fusion(f32[2560,1024]{1,0:T(8,128)} %all-gather.4.cloned.1.call-done, s32[2048]{0:T(1024)S(1)} %fusion.75), kind=kCustom, calls=%fused_computation | custom fusion | bytes 16785408 | tf_op jit(solution)/shard_map/gather | solution.py:56
  190.2 5.4 convert_multiply_fusion
  195.6 3.2 copy-done
  198.8 11.0 %all_gather.10 = f32[128,1024]{1,0:T(8,128)S(1)} all-gather(f32[32,1024]{1,0:T(8,128)S(1)} %constant_dynamic-slice_fusion.2), channel_id=1, replica_groups=mesh['wide'=64,'col'=4] {'col'}, dimensions={0}, use_global_device_ids=true | all-gather | bytes 655360 | tf_op jit(solution)/shard_map/all_gather | solution.py:68
  209.8 5.4 copy.13
  215.2 6.8 %fusion.1 = f32[1024,1024]{1,0:T(8,128)} fusion(f32[1024,1024]{1,0:T(8,128)} %copy.13, f32[1024,1024]{0,1:T(8,128)} %all-gather.6.cloned.1.call-done), kind=kLoop, calls=%fused_computation.10 | loop fusion | flops 2097152 | bytes 12582912 | tf_op jit(solution)/shard_map/mul | solution.py:70
  222.0 5.5 copy.14
  227.5 4.4 fusion
  232.0 2.0 copy-done.2
  234.0 11.7 %cholesky.223 = f32[128,128]{1,0:T(8,128)S(1)} custom-call(f32[128,128]{1,0:T(8,128)S(1)} %cholesky.580), custom_call_target="Cholesky" | custom-call | tf_op jit(solution)/shard_map/jit(cholesky)/cholesky | solution.py:71
  245.7 2.5 cholesky.255
  248.2 9.8 %custom-call.62 = f32[1,128,128]{1,2,0:T(8,128)S(1)} custom-call(f32[1,128,128]{2,1,0:T(8,128)S(1)} %get-tuple-element.110), custom_call_target="InvertDiagBlocksLowerTriangular" | custom-call | tf_op jit(solution)/shard_map/jit(cholesky)/cholesky | solution.py:71
  258.0 2.3 constant_dynamic-update-slice_fusion.30
  261.9 12.1 %cholesky.244 = f32[128,128]{1,0:T(8,128)S(1)} custom-call(f32[128,128]{1,0:T(8,128)S(1)} %cholesky.584), custom_call_target="Cholesky" | custom-call | tf_op jit(solution)/shard_map/jit(cholesky)/cholesky | solution.py:71
  274.6 9.8 %custom-call.63 = f32[1,128,128]{1,2,0:T(8,128)S(1)} custom-call(f32[1,128,128]{2,1,0:T(8,128)S(1)} %get-tuple-element.107), custom_call_target="InvertDiagBlocksLowerTriangular" | custom-call | tf_op jit(solution)/shard_map/jit(cholesky)/cholesky | solution.py:71
  285.7 2.1 convolution_subtract_fusion.6
  287.8 11.7 %cholesky.468 = f32[128,128]{1,0:T(8,128)S(1)} custom-call(f32[128,128]{1,0:T(8,128)S(1)} %cholesky.589), custom_call_target="Cholesky" | custom-call | tf_op jit(solution)/shard_map/jit(cholesky)/cholesky | solution.py:71
  300.9 9.8 %custom-call.64 = f32[1,128,128]{1,2,0:T(8,128)S(1)} custom-call(f32[1,128,128]{2,1,0:T(8,128)S(1)} %get-tuple-element.104), custom_call_target="InvertDiagBlocksLowerTriangular" | custom-call | tf_op jit(solution)/shard_map/jit(cholesky)/cholesky | solution.py:71
  311.9 2.3 convolution_subtract_fusion.7
  314.2 11.8 %cholesky.487 = f32[128,128]{1,0:T(8,128)S(1)} custom-call(f32[128,128]{1,0:T(8,128)S(1)} %cholesky.594), custom_call_target="Cholesky" | custom-call | tf_op jit(solution)/shard_map/jit(cholesky)/cholesky | solution.py:71
  327.4 9.8 %custom-call.65 = f32[1,128,128]{1,2,0:T(8,128)S(1)} custom-call(f32[1,128,128]{2,1,0:T(8,128)S(1)} %get-tuple-element.101), custom_call_target="InvertDiagBlocksLowerTriangular" | custom-call | tf_op jit(solution)/shard_map/jit(cholesky)/cholesky | solution.py:71
  338.3 2.3 convolution_subtract_fusion.8
  340.6 11.7 %cholesky.506 = f32[128,128]{1,0:T(8,128)S(1)} custom-call(f32[128,128]{1,0:T(8,128)S(1)} %cholesky.599), custom_call_target="Cholesky" | custom-call | tf_op jit(solution)/shard_map/jit(cholesky)/cholesky | solution.py:71
  353.6 10.0 %custom-call.66 = f32[1,128,128]{1,2,0:T(8,128)S(1)} custom-call(f32[1,128,128]{2,1,0:T(8,128)S(1)} %get-tuple-element.98), custom_call_target="InvertDiagBlocksLowerTriangular" | custom-call | tf_op jit(solution)/shard_map/jit(cholesky)/cholesky | solution.py:71
  364.6 2.3 convolution_subtract_fusion.9
  366.9 11.7 %cholesky.526 = f32[128,128]{1,0:T(8,128)S(1)} custom-call(f32[128,128]{1,0:T(8,128)S(1)} %cholesky.604), custom_call_target="Cholesky" | custom-call | tf_op jit(solution)/shard_map/jit(cholesky)/cholesky | solution.py:71
  380.0 9.8 %custom-call.67 = f32[1,128,128]{1,2,0:T(8,128)S(1)} custom-call(f32[1,128,128]{2,1,0:T(8,128)S(1)} %get-tuple-element.95), custom_call_target="InvertDiagBlocksLowerTriangular" | custom-call | tf_op jit(solution)/shard_map/jit(cholesky)/cholesky | solution.py:71
  390.7 2.1 convolution_subtract_fusion.10
  392.8 12.1 %cholesky.546 = f32[128,128]{1,0:T(8,128)S(1)} custom-call(f32[128,128]{1,0:T(8,128)S(1)} %cholesky.609), custom_call_target="Cholesky" | custom-call | tf_op jit(solution)/shard_map/jit(cholesky)/cholesky | solution.py:71
  406.2 9.8 %custom-call.68 = f32[1,128,128]{1,2,0:T(8,128)S(1)} custom-call(f32[1,128,128]{2,1,0:T(8,128)S(1)} %get-tuple-element.92), custom_call_target="InvertDiagBlocksLowerTriangular" | custom-call | tf_op jit(solution)/shard_map/jit(cholesky)/cholesky | solution.py:71
  416.9 1.8 convolution_subtract_fusion.11
  418.7 11.7 %cholesky.564 = f32[128,128]{1,0:T(8,128)S(1)} custom-call(f32[128,128]{1,0:T(8,128)S(1)} %convolution_subtract_fusion.11), custom_call_target="Cholesky" | custom-call | tf_op jit(solution)/shard_map/jit(cholesky)/cholesky | solution.py:71
  437.3 6.6 %fusion.2 = (f32[1024,1024]{1,0:T(8,128)}, f32[1024,1024]{1,0:T(8,128)}) fusion(f32[1024,1024]{1,0:T(8,128)} %get-tuple-element.90, pred[]{:T(512)S(6)} %cholesky.579), kind=kLoop, calls=%fused_computation.14 | loop fusion | flops 4194304 | bytes 12582913 | tf_op jit(solution)/shard_map/triangular_solve | solution.py:14
  443.9 23.2 %while.2 = (s32[]{:T(128)}, f32[1024,1024]{1,0:T(8,128)}, s32[8,2]{0,1:T(2,128)S(1)}, f32[8,128,128]{2,1,0:T(8,128)S(1)}, s32[]{:T(128)}) while((s32[]{:T(128)}, f32[1024,1024]{1,0:T(8,128)}, s32[8,2]{0,1:T(2,128)S(1)}, f32[8,128,128]{2,1,0:T(8,128)S(1)}, s32[]{:T(128)}) %tuple.153), condition=%wide.while_cond.1, body=%wide.while_body.1.sunk | while | flops 2 | bytes 131189 | solution.py:14
  444.5 2.3 bitcast_dynamic-update-slice_fusion.2
  447.4 2.3 bitcast_dynamic-update-slice_fusion.2
  450.3 2.3 bitcast_dynamic-update-slice_fusion.2
  453.2 2.3 bitcast_dynamic-update-slice_fusion.2
  456.1 2.3 bitcast_dynamic-update-slice_fusion.2
  459.1 2.3 bitcast_dynamic-update-slice_fusion.2
  462.0 2.3 bitcast_dynamic-update-slice_fusion.2
  464.9 2.2 bitcast_dynamic-update-slice_fusion.2
  467.1 78.8 %custom-call.69 = f32[8,128,128]{1,2,0:T(8,128)S(1)} custom-call(f32[8,128,128]{2,1,0:T(8,128)S(1)} %get-tuple-element.22), custom_call_target="InvertDiagBlocksLowerTriangular" | custom-call | tf_op jit(solution)/shard_map/triangular_solve | solution.py:14
  546.4 1.9 convolution_subtract_fusion.4
  549.1 1.6 convolution_subtract_fusion
  551.5 2.0 fusion.17
  554.3 2.2 fusion.20
  557.3 2.6 convolution_subtract_fusion.2
  560.6 2.8 convolution_subtract_fusion.1
  564.1 3.5 convolution_subtract_fusion.3
  568.2 4.6 fusion.91
  572.8 4.5 fusion.88
  577.3 2.4 fusion.89
  579.7 7.3 %fusion.90 = f32[2048,128]{1,0:T(8,128)S(1)} fusion(f32[2048,1024]{1,0:T(8,128)S(1)} %bitcast.196, f32[128,1024]{1,0:T(8,128)S(1)} %fusion.89), kind=kOutput, calls=%fused_computation.253 | convolution fusion | flops 3221225472 | bytes 9961472 | tf_op jit(solution)/shard_map/dot_general | solution.py:18
  (104 shorter events, 37.6 us)
Async XLA Ops:
  7.2 94.4 %all-gather.4.cloned.1.call-start = ((), (), s32[]{:S(2)}) async-start(), calls=%async_computation | async-start | bytes 10649600 | tf_op jit(solution)/shard_map/all_gather | solution.py:39
  9.6 200.2 %all-gather.6.cloned.1.call-start = ((), (), s32[]{:S(2)}) async-start(), calls=%async_computation.1 | async-start | bytes 5242880 | tf_op jit(solution)/shard_map/all_gather | solution.py:50
  112.0 7.1 %copy-start.4 = (s32[2,32]{1,0:T(2,128)S(1)}, s32[2,32]{1,0:T(2,128)}, u32[]{:S(2)}) copy-start(s32[2,32]{1,0:T(2,128)} %param.8) | copy-start | bytes 772
  195.6 3.2 copy-start
  232.0 2.0 copy-start.2
  545.9 3.2 copy-start.1
  567.6 12.1 %slice-start = ((s8[8388608]{0:T(1024)(128)(4,1)}), s8[4194304]{0:T(1024)(128)(4,1)S(1)}, s32[]{:S(2)}) async-start(s8[8388608]{0:T(1024)(128)(4,1)} %bitcast.195), calls=%async_computation.2 | async-start | bytes 8388608
  572.8 6.9 %slice-start.1 = ((s8[8388608]{0:T(1024)(128)(4,1)}), s8[4194304]{0:T(1024)(128)(4,1)S(1)}, s32[]{:S(2)}) async-start(s8[8388608]{0:T(1024)(128)(4,1)} %bitcast.195), calls=%async_computation.3 | async-start | bytes 8388608
  579.7 8.7 %copy-start.3 = (f32[64,1,32,128]{3,2,1,0:T(8,128)S(1)}, f32[64,1,32,128]{3,2,1,0:T(8,128)}, u32[]{:S(2)}) copy-start(f32[64,1,32,128]{3,2,1,0:T(8,128)} %param.9) | copy-start | bytes 3145732
Sparse Core Ops, SparseCore 0:
  11.3 90.2 all-gather.3
  119.1 47.2 all-gather.5

commit v2 on v1

v2 whole, which is shorter than its diff:
```python
import jax
import jax.numpy as jnp
from jax import lax
from jax.sharding import PartitionSpec as P

BLOCK = 256
FACTOR_BLOCK = 128

highest = lax.Precision.HIGHEST


def lower_inverse(lower_factor):
    order_size = lower_factor.shape[0]
    identity = jnp.eye(order_size, dtype=lower_factor.dtype)
    return lax.linalg.triangular_solve(lower_factor, identity, left_side=True, lower=True)


def contract_rows(left_rows, right_rows):
    return lax.dot_general(left_rows, right_rows, (((1,), (1,)), ((), ())), precision=highest)


def matmul(left, right):
    return lax.dot_general(left, right, (((1,), (0,)), ((), ())), precision=highest)


def factor_and_inverse(gathered):
    order_size = gathered.shape[0]
    size = FACTOR_BLOCK
    count = order_size // size
    factor = jnp.zeros((order_size, order_size), jnp.float32)
    diag_inverses = []
    for k in range(count):
        start = k * size
        column = (gathered[start:, start:start + size] + gathered[start:start + size, start:].T) * 0.5
        if k > 0:
            column = column - contract_rows(factor[start:, :start], factor[start:start + size, :start])
        block = jnp.tril(lax.linalg.cholesky(column[:size], symmetrize_input=False))
        block_inverse = jnp.tril(lower_inverse(block))
        factor = factor.at[start:start + size, start:start + size].set(block)
        if k < count - 1:
            factor = factor.at[start + size:, start:start + size].set(contract_rows(column[size:], block_inverse))
        diag_inverses.append(block_inverse)
    inverse = jnp.zeros((order_size, order_size), jnp.float32)
    inverse = inverse.at[:size, :size].set(diag_inverses[0])
    for k in range(1, count):
        start = k * size
        partial = matmul(factor[start:start + size, :start], inverse[:start, :start])
        inverse = inverse.at[start:start + size, :start].set(-matmul(diag_inverses[k], partial))
        inverse = inverse.at[start:start + size, start:start + size].set(diag_inverses[k])
    return factor, inverse


def local(assembled, row_map, fill_pattern, trailing_block):
    wide_count = lax.axis_size("wide")
    col_count = lax.axis_size("col")
    asm_rows, twice_width = assembled.shape
    half_width = twice_width // 2
    trail_rows = trailing_block.shape[2]
    blocks = fill_pattern.shape[1]
    diag_share = twice_width // (col_count * wide_count)
    diag_col = twice_width // col_count
    trail_col = wide_count * trail_rows
    wide_index = lax.axis_index("wide")
    col_index = lax.axis_index("col")
    device_index = wide_index * col_count + col_index
    is_diagonal = row_map < twice_width

    order_ids = jnp.argsort(jnp.where(is_diagonal, 0, 1), stable=True)[:diag_share]
    diag_pack_rows = ((diag_share + 1 + 7) // 8) * 8
    diag_id_row = jnp.zeros((twice_width,), jnp.float32).at[:diag_share].set(row_map[order_ids].astype(jnp.float32))
    diag_pack = jnp.concatenate(
        [assembled[order_ids], diag_id_row[None, :],
         jnp.zeros((diag_pack_rows - diag_share - 1, twice_width), jnp.float32)], axis=0)
    diag_wide = lax.all_gather(diag_pack, "wide", axis=0, tiled=True).reshape(wide_count, diag_pack_rows, twice_width)
    diag_rows = diag_wide[:, :diag_share, :].reshape(wide_count * diag_share, twice_width)
    diag_slot = diag_wide[:, diag_share, :diag_share].astype(jnp.int32).reshape(-1) - diag_col * col_index
    diag_block = jnp.zeros((diag_col, twice_width), jnp.float32).at[diag_slot].set(diag_rows, mode="drop")
    full = lax.all_gather(diag_block, "col", axis=0, tiled=True)

    packed_rows = ((asm_rows + 1 + 7) // 8) * 8
    id_row = jnp.zeros((twice_width,), jnp.float32).at[:asm_rows].set(row_map.astype(jnp.float32))
    packed = jnp.concatenate(
        [assembled, id_row[None, :], jnp.zeros((packed_rows - asm_rows - 1, twice_width), jnp.float32)], axis=0)
    packed, full = lax.optimization_barrier((packed, full))
    gathered = lax.all_gather(packed, "wide", axis=0, tiled=True)
    gathered3 = gathered.reshape(wide_count, packed_rows, twice_width)
    ids = gathered3[:, asm_rows, :asm_rows].astype(jnp.int32)
    trail_id = ids - twice_width
    trail_slot = (trail_id // (trail_rows * col_count)) * trail_rows + trail_id % trail_rows
    key = jnp.where(ids >= twice_width, trail_slot, trail_col)
    key = jnp.concatenate([key, jnp.full((wide_count, packed_rows - asm_rows), trail_col, jnp.int32)], axis=1)
    key = key.reshape(-1)
    _, order = lax.sort((key, jnp.arange(key.shape[0], dtype=jnp.int32)), num_keys=1)
    trail_src = order[:trail_col]

    block_of = jnp.concatenate(
        [trail_id // BLOCK, jnp.full((wide_count, packed_rows - asm_rows), -1, jnp.int32)], axis=1).reshape(-1)
    block_hits = (block_of[:, None] == jnp.arange(blocks)[None, :]).astype(jnp.int32)
    first_keep = jnp.sum(block_hits * fill_pattern[0][None, :], axis=1).astype(jnp.float32)
    second_keep = jnp.sum(block_hits * fill_pattern[1][None, :], axis=1).astype(jnp.float32)

    own_src = lax.dynamic_slice_in_dim(trail_src, wide_index * trail_rows, trail_rows, 0)
    column_first = jnp.arange(twice_width) < half_width
    own_keep = jnp.where(column_first[None, :], first_keep[own_src][:, None], second_keep[own_src][:, None])
    masked_own = gathered[own_src] * own_keep
    masked_range = lax.all_gather(masked_own, "col", axis=0, tiled=True)

    factor, inverse = factor_and_inverse(full)
    range_panel = contract_rows(masked_range, inverse)
    panel = lax.dynamic_slice_in_dim(range_panel, col_index * trail_rows, trail_rows, 0)
    range_back = matmul(range_panel, inverse)
    first_part = contract_rows(gathered[:, :half_width], range_back[:, :half_width])
    second_part = contract_rows(gathered[:, half_width:], range_back[:, half_width:])
    update_all = first_keep[:, None] * first_part + second_keep[:, None] * second_part
    update = update_all[trail_src]
    schur = trailing_block - update.reshape(trailing_block.shape)
    factor_rows = lax.dynamic_slice_in_dim(factor, device_index * diag_share, diag_share, 0)
    return (schur, panel, factor_rows)


def solution(mesh):
    in_specs = (P(("wide", "col"), None), P(("wide", "col")), P(), P(None, "col", None, "wide"))
    out_specs = (P(None, "col", None, "wide"), P(("wide", "col"), None), P(("wide", "col"), None))
    return jax.shard_map(local, mesh=mesh, in_specs=in_specs, out_specs=out_specs, check_vma=False)
```

time: 607 us -> 471 us (0.78)
  other arithmetic: 322 us -> 202 us
  local copies, waits for them, and re-layouts: 88 us -> 39.4 us
  waiting for transfers between devices: 91.7 us -> 129 us
    all_gather x1, waiting for transfers between devices: 91.7 us -> 0.01 us  [local(): gathered = lax.all_gather(packed, 'wide', axis=0, tiled=True)]
    all_gather x0 -> x1, waiting for transfers between devices: none -> 81.9 us  [local(): lax.all_gather(diag_pack, 'wide', axis=0, tiled=True)]
    another operation x30 -> x24, other arithmetic: 173 us -> 99.4 us  [factor_and_inverse(): block = jnp.tril(lax.linalg.cholesky(column[:size], symmetrize_input=False))]
    all_gather x1, waiting for transfers between devices: 0.01 us -> 47 us  [local(): full = lax.all_gather(diag_block, 'col', axis=0, tiled=True)]
    gather x7 -> x3, other arithmetic: 40.5 us -> 0.02 us  [the longest x1 0.01 us: local(): assembled[order_ids]]
    dot_general x1 -> x15, matrix products: 2.41 us -> 28.7 us  [matmul(): lax.dot_general(left, right, (((1,), (0,)), ((), ())), precision=highest)]
    another operation x33 -> x1, local copies, waits for them, and re-layouts: 25.6 us -> 0.01 us
    another operation x14 -> x0, matrix products: 23.1 us -> none  [local(): factor = jnp.linalg.cholesky(symmetric)]
  transfers between devices with their start and end apart: 2 -> 3, of which waited for: 1 -> 2; matrix products, arithmetic and copies ran while one was open for 13% -> 55% of each run, Pallas kernels for 0% -> 0%
where the time goes in v2:
time: 471 us; the launch traced here: 465 us
  other arithmetic  202 us (43%)
  waiting for transfers between devices  129 us (27%)
  matrix products  69.7 us (15%)
  local copies, waits for them, and re-layouts  39.4 us (8%)
  between operations  14.5 us (3%)
  blocking collectives  10.3 us (2%)
    another operation x24, other arithmetic, factor_and_inverse(): block = jnp.tril(lax.linalg.cholesky(column[:size], symmetrize_input=False))  99.4 us
    another operation x15, other arithmetic, lower_inverse(): lax.linalg.triangular_solve(lower_factor, identity, left_side=True, lower...  87.4 us
    all_gather x1, waiting for transfers between devices, local(): lax.all_gather(diag_pack, 'wide', axis=0, tiled=True)  81.9 us
    all_gather x1, waiting for transfers between devices, local(): full = lax.all_gather(diag_block, 'col', axis=0, tiled=True)  47 us
    dot_general x17, matrix products, contract_rows(): lax.dot_general(left_rows, right_rows, (((1,), (1,)), ((), ())), precisio...  38.7 us
    dot_general x15, matrix products, matmul(): lax.dot_general(left, right, (((1,), (0,)), ((), ())), precision=highest)  28.7 us
    all_gather x1, blocking collectives, local(): masked_range = lax.all_gather(masked_own, 'col', axis=0, tiled=True)  10.3 us
  transfers between devices with their start and end apart: 3, of which 2 were waited for; matrix products, arithmetic and copies ran while one was open for 55% of the time, Pallas kernels for 0%

profile of v2, /device:TPU:1, one launch (start us, length us, event | category | flops | bytes accessed | tf_op | source)
XLA Modules:
  0.0 464.8 jit_solution(15050510319490298946)
XLA Ops:
  7.9 2.0 sort.32
  10.0 1.3 gather_fusion.1
  11.3 1.5 gather_fusion
  13.5 81.9 %all-gather.4.cloned.1.call-done = f32[512,1024]{1,0:T(8,128)} async-done(((f32[8,1024]{1,0:T(8,128)}), f32[512,1024]{1,0:T(8,128)}) %all-gather.4.cloned.1.call-update) | async-done | bytes 2097168 | tf_op jit(solution)/shard_map/all_gather | solution.py:74
  95.4 1.8 slice.958
  98.8 1.7 scatter_custom_fusion
  100.4 1.3 copy.31
  102.5 47.0 %all-gather.6.cloned.1.call-done = f32[1024,1024]{0,1:T(8,128)} async-done(((f32[256,1024]{0,1:T(8,128)}), f32[1024,1024]{0,1:T(8,128)}) %all-gather.6.cloned.1.call-update) | async-done | bytes 4194320 | tf_op jit(solution)/shard_map/all_gather | solution.py:78
  149.6 5.9 %copy.35 = f32[1024,1024]{1,0:T(8,128)} copy(f32[1024,1024]{0,1:T(8,128)} %all-gather.6.cloned.1.call-done) | data formatting | bytes 8388608 | tf_op jit(solution)/shard_map/optimization_barrier | solution.py:84
  156.3 1.3 fusion.35
  157.6 11.7 %custom-call.20 = f32[128,128]{1,0:T(8,128)S(1)} custom-call(f32[128,128]{1,0:T(8,128)S(1)} %slice.962), custom_call_target="Cholesky" | custom-call | tf_op jit(solution)/shard_map/cholesky/custom-call.1 | solution.py:37
  170.7 9.8 %custom-call.21 = f32[1,128,128]{1,2,0:T(8,128)S(1)} custom-call(f32[1,128,128]{2,1,0:T(8,128)S(1)} %get-tuple-element.399), custom_call_target="InvertDiagBlocksLowerTriangular" | custom-call | tf_op jit(solution)/shard_map/triangular_solve/custom-call.0 | solution.py:15
  180.5 2.6 scatter.120
  183.3 2.5 scatter.119
  185.8 1.3 constant_dynamic-update-slice_fusion
  187.2 1.7 convolution_subtract_fusion
  188.9 11.7 %custom-call.22 = f32[128,128]{1,0:T(8,128)S(1)} custom-call(f32[128,128]{1,0:T(8,128)S(1)} %slice.966), custom_call_target="Cholesky" | custom-call | tf_op jit(solution)/shard_map/cholesky/custom-call.1 | solution.py:37
  201.3 1.3 fusion.90
  202.6 9.9 %custom-call.23 = f32[1,128,128]{1,2,0:T(8,128)S(1)} custom-call(f32[1,128,128]{2,1,0:T(8,128)S(1)} %get-tuple-element.414), custom_call_target="InvertDiagBlocksLowerTriangular" | custom-call | tf_op jit(solution)/shard_map/triangular_solve/custom-call.0 | solution.py:15
  212.8 1.3 convolution_dynamic-update-slice_fusion
  214.1 2.2 convolution_subtract_fusion.1
  216.3 11.7 %custom-call.24 = f32[128,128]{1,0:T(8,128)S(1)} custom-call(f32[128,128]{1,0:T(8,128)S(1)} %slice.971), custom_call_target="Cholesky" | custom-call | tf_op jit(solution)/shard_map/cholesky/custom-call.1 | solution.py:37
  228.7 1.3 select_bitcast_fusion.5
  230.0 9.8 %custom-call.25 = f32[1,128,128]{1,2,0:T(8,128)S(1)} custom-call(f32[1,128,128]{2,1,0:T(8,128)S(1)} %get-tuple-element.411), custom_call_target="InvertDiagBlocksLowerTriangular" | custom-call | tf_op jit(solution)/shard_map/triangular_solve/custom-call.0 | solution.py:15
  240.1 1.2 convolution_dynamic-update-slice_fusion.1
  241.4 2.4 convolution_subtract_fusion.2
  243.9 11.9 %custom-call.26 = f32[128,128]{1,0:T(8,128)S(1)} custom-call(f32[128,128]{1,0:T(8,128)S(1)} %slice.976), custom_call_target="Cholesky" | custom-call | tf_op jit(solution)/shard_map/cholesky/custom-call.1 | solution.py:37
  256.4 1.3 select_bitcast_fusion.4
  257.7 9.8 %custom-call.27 = f32[1,128,128]{1,2,0:T(8,128)S(1)} custom-call(f32[1,128,128]{2,1,0:T(8,128)S(1)} %get-tuple-element.409), custom_call_target="InvertDiagBlocksLowerTriangular" | custom-call | tf_op jit(solution)/shard_map/triangular_solve/custom-call.0 | solution.py:15
  268.9 2.4 convolution_subtract_fusion.3
  271.4 11.7 %custom-call.28 = f32[128,128]{1,0:T(8,128)S(1)} custom-call(f32[128,128]{1,0:T(8,128)S(1)} %slice.981), custom_call_target="Cholesky" | custom-call | tf_op jit(solution)/shard_map/cholesky/custom-call.1 | solution.py:37
  283.8 1.3 select_bitcast_fusion.3
  285.1 10.2 %custom-call.29 = f32[1,128,128]{1,2,0:T(8,128)S(1)} custom-call(f32[1,128,128]{2,1,0:T(8,128)S(1)} %get-tuple-element.407), custom_call_target="InvertDiagBlocksLowerTriangular" | custom-call | tf_op jit(solution)/shard_map/triangular_solve/custom-call.0 | solution.py:15
  296.6 2.3 convolution_subtract_fusion.4
  298.9 11.7 %custom-call.30 = f32[128,128]{1,0:T(8,128)S(1)} custom-call(f32[128,128]{1,0:T(8,128)S(1)} %slice.986), custom_call_target="Cholesky" | custom-call | tf_op jit(solution)/shard_map/cholesky/custom-call.1 | solution.py:37
  311.3 1.3 select_bitcast_fusion.2
  312.6 9.8 %custom-call.31 = f32[1,128,128]{1,2,0:T(8,128)S(1)} custom-call(f32[1,128,128]{2,1,0:T(8,128)S(1)} %get-tuple-element.405), custom_call_target="InvertDiagBlocksLowerTriangular" | custom-call | tf_op jit(solution)/shard_map/triangular_solve/custom-call.0 | solution.py:15
  323.7 2.1 convolution_subtract_fusion.5
  325.8 11.8 %custom-call.32 = f32[128,128]{1,0:T(8,128)S(1)} custom-call(f32[128,128]{1,0:T(8,128)S(1)} %slice.991), custom_call_target="Cholesky" | custom-call | tf_op jit(solution)/shard_map/cholesky/custom-call.1 | solution.py:37
  338.3 1.3 select_bitcast_fusion.1
  339.6 9.8 %custom-call.33 = f32[1,128,128]{1,2,0:T(8,128)S(1)} custom-call(f32[1,128,128]{2,1,0:T(8,128)S(1)} %get-tuple-element.403), custom_call_target="InvertDiagBlocksLowerTriangular" | custom-call | tf_op jit(solution)/shard_map/triangular_solve/custom-call.0 | solution.py:15
  350.7 1.8 convolution_subtract_fusion.6
  352.5 11.7 %custom-call.34 = f32[128,128]{1,0:T(8,128)S(1)} custom-call(f32[128,128]{1,0:T(8,128)S(1)} %convolution_subtract_fusion.6), custom_call_target="Cholesky" | custom-call | tf_op jit(solution)/shard_map/cholesky/custom-call.1 | solution.py:37
  364.9 1.3 select_bitcast_fusion
  366.2 9.8 %custom-call.35 = f32[1,128,128]{1,2,0:T(8,128)S(1)} custom-call(f32[1,128,128]{2,1,0:T(8,128)S(1)} %get-tuple-element.401), custom_call_target="InvertDiagBlocksLowerTriangular" | custom-call | tf_op jit(solution)/shard_map/triangular_solve/custom-call.0 | solution.py:15
  376.0 1.4 constant_dynamic-slice_fusion
  379.9 1.3 fusion.54
  382.8 1.7 fusion.33
  386.2 2.3 fusion.26
  390.2 2.8 fusion.17
  393.0 1.2 fusion.21
  394.7 3.2 fusion.15
  398.0 1.3 fusion.20
  400.1 4.2 fusion.13
  404.4 1.3 fusion.19
  407.6 5.7 %sort.33 = (s32[2560]{0:T(1024)}, s32[2560]{0:T(1024)S(1)}) sort(s32[2560]{0:T(1024)S(1)} %reshape.981, s32[2560]{0:T(1024)S(1)} %iota.299), dimensions={0}, to_apply=%region_3.4 | sort | flops 30720 | bytes 40960 | tf_op jit(solution)/shard_map/sort | solution.py:93
  415.3 4.6 %gather_fusion.2 = f32[32,1024]{1,0:T(8,128)S(1)} fusion(f32[2560,1024]{1,0:T(8,128)} %all-gather.8.cloned.1.call-done, s32[1024]{0:T(1024)S(1)} %pad_clamp_fusion), kind=kCustom, calls=%fused_computation.2 | custom fusion | bytes 262272 | tf_op jit(solution)/shard_map/gather | solution.py:105
  420.0 10.3 %all_gather.15 = f32[128,1024]{1,0:T(8,128)S(1)} all-gather(f32[32,1024]{1,0:T(8,128)S(1)} %select_multiply_fusion), channel_id=1, replica_groups=mesh['wide'=64,'col'=4] {'col'}, dimensions={0}, use_global_device_ids=true | all-gather | bytes 655360 | tf_op jit(solution)/shard_map/all_gather | solution.py:106
  430.3 6.7 %fusion.112 = f32[128,1024]{1,0:T(8,128)S(1)} fusion(f32[128,1024]{1,0:T(8,128)S(1)} %all_gather.15, f32[1024,1024]{1,0:T(8,128)} %constant_dynamic-update-slice_fusion.4), kind=kOutput, calls=%fused_computation.229 | convolution fusion | flops 1610612736 | bytes 5242880 | tf_op jit(solution)/shard_map/dot_general | solution.py:19
  437.0 4.6 fusion.113
  442.3 4.4 fusion.4
  446.7 4.7 %fusion.10 = f32[2560,128]{1,0:T(8,128)S(1)} fusion(f32[2560,128]{1,0:T(8,128)S(1)} %fusion.4, f32[2560,1024]{1,0:T(8,128)S(1)} %copy-done, f32[2560]{0:T(1024)S(1)} %convert_element_type.75, f32[128,1024]{1,0:T(8,128)S(1)} %fusion.113), kind=kOutput, calls=%fused_computation.13 | convolution fusion | flops 2013921280 | bytes 8138752 | tf_op jit(solution)/shard_map/dot_general | solution.py:19
  451.5 5.5 %gather_fusion.5 = f32[2048,128]{1,0:T(8,128)S(1)} fusion(f32[2560,128]{1,0:T(8,128)S(1)} %fusion.10, s32[2048]{0:T(1024)S(1)} %get-tuple-element.417), kind=kCustom, calls=%fused_computation.5 | custom fusion | bytes 2105344 | tf_op jit(solution)/shard_map/gather | solution.py:115
  456.9 1.2 sub.69
  (99 shorter events, 30.4 us)
Async XLA Ops:
  7.2 88.2 %all-gather.4.cloned.1.call-start = ((), (), s32[]{:S(2)}) async-start(), calls=%async_computation | async-start | bytes 2129920 | tf_op jit(solution)/shard_map/all_gather | solution.py:74
  13.5 136.1 %all-gather.6.cloned.1.call-start = ((), (), s32[]{:S(2)}) async-start(), calls=%async_computation.1 | async-start | bytes 5242880 | tf_op jit(solution)/shard_map/all_gather | solution.py:78
  95.4 6.4 %copy-start.2 = (f32[36,1024]{1,0:T(8,128)S(1)}, f32[36,1024]{1,0:T(8,128)}, u32[]{:S(2)}) copy-start(f32[36,1024]{1,0:T(8,128)} %param.71) | copy-start | bytes 442372
  95.4 54.2 %copy-start.3 = (s32[2,32]{1,0:T(2,128)S(1)}, s32[2,32]{1,0:T(2,128)}, u32[]{:S(2)}) copy-start(s32[2,32]{1,0:T(2,128)} %param.73) | copy-start | bytes 772
  101.8 304.5 %all-gather.8.cloned.1.call-start = ((), (), s32[]{:S(2)}) async-start(), calls=%async_computation.2 | async-start | bytes 10649600 | tf_op jit(solution)/shard_map/all_gather | solution.py:85
  430.3 12.0 %copy-start = (f32[2560,1024]{1,0:T(8,128)S(1)}, f32[2560,1024]{1,0:T(8,128)}, u32[]{:S(2)}) copy-start(f32[2560,1024]{1,0:T(8,128)} %all-gather.8.cloned.1.call-done) | copy-start | bytes 31457284
  451.4 5.5 %copy-start.1 = (f32[64,1,32,128]{3,2,1,0:T(8,128)S(1)}, f32[64,1,32,128]{3,2,1,0:T(8,128)}, u32[]{:S(2)}) copy-start(f32[64,1,32,128]{3,2,1,0:T(8,128)} %param.74) | copy-start | bytes 3145732
Sparse Core Ops, SparseCore 0:
  13.6 81.7 all-gather.3
  101.9 47.5 all-gather.5
  152.3 87.2 all-gather.7

commit v3 on v2

--- a/solution.py
+++ b/solution.py
@@ -4,6 +4,8 @@
 from jax.sharding import PartitionSpec as P
 
 BLOCK = 256
+LANE_PAD = 128
+WIDE_PARTS = ("y", "z", "core")
 FACTOR_BLOCK = 128
 
 highest = lax.Precision.HIGHEST
@@ -23,7 +25,7 @@
     return lax.dot_general(left, right, (((1,), (0,)), ((), ())), precision=highest)
 
 
-def factor_and_inverse(gathered):
+def factor_and_inverse(gathered, tied, exchange):
     order_size = gathered.shape[0]
     size = FACTOR_BLOCK
     count = order_size // size
@@ -40,6 +42,9 @@
         if k < count - 1:
             factor = factor.at[start + size:, start:start + size].set(contract_rows(column[size:], block_inverse))
         diag_inverses.append(block_inverse)
+        if k == count // 2:
+            factor, tied = lax.optimization_barrier((factor, tied))
+            tied = exchange(tied)
     inverse = jnp.zeros((order_size, order_size), jnp.float32)
     inverse = inverse.at[:size, :size].set(diag_inverses[0])
     for k in range(1, count):
@@ -47,11 +52,11 @@
         partial = matmul(factor[start:start + size, :start], inverse[:start, :start])
         inverse = inverse.at[start:start + size, :start].set(-matmul(diag_inverses[k], partial))
         inverse = inverse.at[start:start + size, start:start + size].set(diag_inverses[k])
-    return factor, inverse
+    return factor, inverse, tied
 
 
 def local(assembled, row_map, fill_pattern, trailing_block):
-    wide_count = lax.axis_size("wide")
+    wide_count = lax.axis_size(WIDE_PARTS)
     col_count = lax.axis_size("col")
     asm_rows, twice_width = assembled.shape
     half_width = twice_width // 2
@@ -60,21 +65,20 @@
     diag_share = twice_width // (col_count * wide_count)
     diag_col = twice_width // col_count
     trail_col = wide_count * trail_rows
-    wide_index = lax.axis_index("wide")
+    wide_index = lax.axis_index(WIDE_PARTS)
     col_index = lax.axis_index("col")
     device_index = wide_index * col_count + col_index
     is_diagonal = row_map < twice_width
 
     order_ids = jnp.argsort(jnp.where(is_diagonal, 0, 1), stable=True)[:diag_share]
-    diag_pack_rows = ((diag_share + 1 + 7) // 8) * 8
-    diag_id_row = jnp.zeros((twice_width,), jnp.float32).at[:diag_share].set(row_map[order_ids].astype(jnp.float32))
+    diag_ids = row_map[order_ids].astype(jnp.float32)
     diag_pack = jnp.concatenate(
-        [assembled[order_ids], diag_id_row[None, :],
-         jnp.zeros((diag_pack_rows - diag_share - 1, twice_width), jnp.float32)], axis=0)
-    diag_wide = lax.all_gather(diag_pack, "wide", axis=0, tiled=True).reshape(wide_count, diag_pack_rows, twice_width)
-    diag_rows = diag_wide[:, :diag_share, :].reshape(wide_count * diag_share, twice_width)
-    diag_slot = diag_wide[:, diag_share, :diag_share].astype(jnp.int32).reshape(-1) - diag_col * col_index
-    diag_block = jnp.zeros((diag_col, twice_width), jnp.float32).at[diag_slot].set(diag_rows, mode="drop")
+        [assembled[order_ids], jnp.broadcast_to(diag_ids[:, None], (diag_share, LANE_PAD))], axis=1)
+    for axis in WIDE_PARTS[::-1]:
+        diag_pack = lax.all_gather(diag_pack, axis, axis=0, tiled=True)
+    diag_slot = diag_pack[:, twice_width].astype(jnp.int32) - diag_col * col_index
+    diag_block = jnp.zeros((diag_col, twice_width), jnp.float32).at[diag_slot].set(
+        diag_pack[:, :twice_width], mode="drop")
     full = lax.all_gather(diag_block, "col", axis=0, tiled=True)
 
     packed_rows = ((asm_rows + 1 + 7) // 8) * 8
@@ -82,7 +86,7 @@
     packed = jnp.concatenate(
         [assembled, id_row[None, :], jnp.zeros((packed_rows - asm_rows - 1, twice_width), jnp.float32)], axis=0)
     packed, full = lax.optimization_barrier((packed, full))
-    gathered = lax.all_gather(packed, "wide", axis=0, tiled=True)
+    gathered = lax.all_gather(packed, WIDE_PARTS, axis=0, tiled=True)
     gathered3 = gathered.reshape(wide_count, packed_rows, twice_width)
     ids = gathered3[:, asm_rows, :asm_rows].astype(jnp.int32)
     trail_id = ids - twice_width
@@ -103,9 +107,15 @@
     column_first = jnp.arange(twice_width) < half_width
     own_keep = jnp.where(column_first[None, :], first_keep[own_src][:, None], second_keep[own_src][:, None])
     masked_own = gathered[own_src] * own_keep
-    masked_range = lax.all_gather(masked_own, "col", axis=0, tiled=True)
+    placed_own = jnp.zeros((col_count * trail_rows, twice_width), jnp.float32)
+    placed_own = lax.dynamic_update_slice_in_dim(placed_own, masked_own, col_index * trail_rows, 0)
 
-    factor, inverse = factor_and_inverse(full)
+    def exchange(tied):
+        placed, first, second, source = tied
+        return (lax.psum(placed, "col"), first, second, source)
+
+    factor, inverse, tied = factor_and_inverse(full, (placed_own, first_keep, second_keep, trail_src), exchange)
+    masked_range, first_keep, second_keep, trail_src = tied
     range_panel = contract_rows(masked_range, inverse)
     panel = lax.dynamic_slice_in_dim(range_panel, col_index * trail_rows, trail_rows, 0)
     range_back = matmul(range_panel, inverse)
@@ -119,6 +129,10 @@
 
 
 def solution(mesh):
-    in_specs = (P(("wide", "col"), None), P(("wide", "col")), P(), P(None, "col", None, "wide"))
-    out_specs = (P(None, "col", None, "wide"), P(("wide", "col"), None), P(("wide", "col"), None))
-    return jax.shard_map(local, mesh=mesh, in_specs=in_specs, out_specs=out_specs, check_vma=False)
+    wide_sizes = (4, 8, 2)
+    split = jax.sharding.Mesh(
+        mesh.devices.reshape(wide_sizes + (mesh.shape["col"],)), WIDE_PARTS + ("col",))
+    rows = WIDE_PARTS + ("col",)
+    in_specs = (P(rows, None), P(rows), P(), P(None, "col", None, WIDE_PARTS))
+    out_specs = (P(None, "col", None, WIDE_PARTS), P(rows, None), P(rows, None))
+    return jax.shard_map(local, mesh=split, in_specs=in_specs, out_specs=out_specs, check_vma=False)

time: 471 us -> 484 us (1.028)
  blocking collectives: 10.3 us -> 27.2 us
    all_gather x2, waiting for transfers between devices: 81.9 us -> 30.2 us  [the longest x1 30.2 us: local(): diag_pack = lax.all_gather(diag_pack, axis, axis=0, tiled=True)]
    psum x0 -> x1, waiting for transfers between devices: none -> 43.4 us  [exchange(): return (lax.psum(placed, 'col'), first, second, source)]
    all_gather x1 -> x2, blocking collectives: 10.3 us -> 27.2 us  [local(): diag_pack = lax.all_gather(diag_pack, axis, axis=0, tiled=True)]
    all_gather x1, waiting for transfers between devices: 47 us -> 52.5 us  [local(): full = lax.all_gather(diag_block, 'col', axis=0, tiled=True)]
    another operation x15 -> x16, other arithmetic: 87.4 us -> 88.5 us  [lower_inverse(): lax.linalg.triangular_solve(lower_factor, identity, left_side=True, lower...]
  transfers between devices with their start and end apart: 3 -> 4, of which waited for: 2 -> 3; matrix products, arithmetic and copies ran while one was open for 55% -> 31% of each run, Pallas kernels for 0% -> 0%
where the time goes in v3:
time: 484 us; the launch traced here: 479 us
  other arithmetic  201 us (42%)
  waiting for transfers between devices  126 us (26%)
  matrix products  72 us (15%)
  local copies, waits for them, and re-layouts  37.5 us (8%)
  blocking collectives  27.2 us (6%)
  between operations  14.5 us (3%)
    another operation x24, other arithmetic, factor_and_inverse(): block = jnp.tril(lax.linalg.cholesky(column[:size], symmetrize_input=False))  99.7 us
    another operation x16, other arithmetic, lower_inverse(): lax.linalg.triangular_solve(lower_factor, identity, left_side=True, lower...  88.5 us
    all_gather x1, waiting for transfers between devices, local(): full = lax.all_gather(diag_block, 'col', axis=0, tiled=True)  52.5 us
    psum x1, waiting for transfers between devices, exchange(): return (lax.psum(placed, 'col'), first, second, source)  43.4 us
    dot_general x17, matrix products, contract_rows(): lax.dot_general(left_rows, right_rows, (((1,), (1,)), ((), ())), precisio...  43.1 us
    all_gather x1, waiting for transfers between devices, local(): diag_pack = lax.all_gather(diag_pack, axis, axis=0, tiled=True)  30.2 us
    all_gather x2, blocking collectives, local(): diag_pack = lax.all_gather(diag_pack, axis, axis=0, tiled=True)  27.2 us
    dot_general x15, matrix products, matmul(): lax.dot_general(left, right, (((1,), (0,)), ((), ())), precision=highest)  26.7 us
  transfers between devices with their start and end apart: 4, of which 3 were waited for; matrix products, arithmetic and copies ran while one was open for 31% of the time, Pallas kernels for 0%

profile of v3, /device:TPU:1, one launch (start us, length us, event | category | flops | bytes accessed | tf_op | source)
XLA Modules:
  0.0 479.0 jit_solution(5068025089527618273)
XLA Ops:
  8.0 2.0 sort.32
  10.0 1.3 gather_fusion.1
  11.3 1.5 gather_fusion
  12.9 4.7 all-gather
  17.6 22.5 %all_gather.16 = f32[64,1152]{1,0:T(8,128)} all-gather(f32[8,1152]{1,0:T(8,128)S(1)} %reshape.996), channel_id=1, replica_groups=mesh['y'=4,'z'=8,'core'=2,'col'=4] {'z'}, dimensions={0}, use_global_device_ids=true | all-gather | bytes 331776 | tf_op jit(solution)/shard_map/all_gather | solution.py:78
  40.2 30.2 %all-gather.5.cloned.1.call-done = f32[256,1152]{1,0:T(8,128)} async-done(((f32[64,1152]{1,0:T(8,128)}), f32[256,1152]{1,0:T(8,128)}) %all-gather.5.cloned.1.call-update) | async-done | bytes 1179664 | tf_op jit(solution)/shard_map/all_gather | solution.py:78
  71.4 2.4 scatter_custom_fusion
  73.9 1.3 copy.51
  76.1 52.5 %all-gather.7.cloned.1.call-done = f32[1024,1024]{0,1:T(8,128)} async-done(((f32[256,1024]{0,1:T(8,128)}), f32[1024,1024]{0,1:T(8,128)}) %all-gather.7.cloned.1.call-update) | async-done | bytes 4194320 | tf_op jit(solution)/shard_map/all_gather | solution.py:82
  128.7 5.5 %copy.52 = f32[1024,1024]{1,0:T(8,128)} copy(f32[1024,1024]{0,1:T(8,128)} %all-gather.7.cloned.1.call-done) | data formatting | bytes 8388608 | tf_op jit(solution)/shard_map/optimization_barrier | solution.py:88
  135.1 1.3 fusion.37
  136.4 11.7 %custom-call.20 = f32[128,128]{1,0:T(8,128)S(1)} custom-call(f32[128,128]{1,0:T(8,128)S(1)} %slice.949), custom_call_target="Cholesky" | custom-call | tf_op jit(solution)/shard_map/cholesky/custom-call.1 | solution.py:39
  149.5 9.8 %custom-call.21 = f32[1,128,128]{1,2,0:T(8,128)S(1)} custom-call(f32[1,128,128]{2,1,0:T(8,128)S(1)} %get-tuple-element.397), custom_call_target="InvertDiagBlocksLowerTriangular" | custom-call | tf_op jit(solution)/shard_map/triangular_solve/custom-call.0 | solution.py:17
  159.3 2.6 scatter.114
  162.1 2.5 scatter.130
  164.6 1.4 constant_dynamic-update-slice_fusion
  166.0 1.7 convolution_subtract_fusion
  167.7 11.7 %custom-call.22 = f32[128,128]{1,0:T(8,128)S(1)} custom-call(f32[128,128]{1,0:T(8,128)S(1)} %slice.953), custom_call_target="Cholesky" | custom-call | tf_op jit(solution)/shard_map/cholesky/custom-call.1 | solution.py:39
  180.1 1.3 select_bitcast_fusion.6
  181.4 10.0 %custom-call.23 = f32[1,128,128]{1,2,0:T(8,128)S(1)} custom-call(f32[1,128,128]{2,1,0:T(8,128)S(1)} %get-tuple-element.411), custom_call_target="InvertDiagBlocksLowerTriangular" | custom-call | tf_op jit(solution)/shard_map/triangular_solve/custom-call.0 | solution.py:17
  191.7 1.3 convolution_dynamic-update-slice_fusion
  192.9 2.2 convolution_subtract_fusion.1
  195.2 11.7 %custom-call.24 = f32[128,128]{1,0:T(8,128)S(1)} custom-call(f32[128,128]{1,0:T(8,128)S(1)} %slice.958), custom_call_target="Cholesky" | custom-call | tf_op jit(solution)/shard_map/cholesky/custom-call.1 | solution.py:39
  207.6 1.3 select_bitcast_fusion.5
  208.9 9.8 %custom-call.25 = f32[1,128,128]{1,2,0:T(8,128)S(1)} custom-call(f32[1,128,128]{2,1,0:T(8,128)S(1)} %get-tuple-element.409), custom_call_target="InvertDiagBlocksLowerTriangular" | custom-call | tf_op jit(solution)/shard_map/triangular_solve/custom-call.0 | solution.py:17
  219.0 1.2 convolution_dynamic-update-slice_fusion.1
  220.2 2.4 convolution_subtract_fusion.2
  222.7 12.1 %custom-call.26 = f32[128,128]{1,0:T(8,128)S(1)} custom-call(f32[128,128]{1,0:T(8,128)S(1)} %slice.963), custom_call_target="Cholesky" | custom-call | tf_op jit(solution)/shard_map/cholesky/custom-call.1 | solution.py:39
  235.5 1.3 select_bitcast_fusion.4
  236.8 9.8 %custom-call.27 = f32[1,128,128]{1,2,0:T(8,128)S(1)} custom-call(f32[1,128,128]{2,1,0:T(8,128)S(1)} %get-tuple-element.407), custom_call_target="InvertDiagBlocksLowerTriangular" | custom-call | tf_op jit(solution)/shard_map/triangular_solve/custom-call.0 | solution.py:17
  248.0 2.4 convolution_subtract_fusion.3
  250.4 11.7 %custom-call.28 = f32[128,128]{1,0:T(8,128)S(1)} custom-call(f32[128,128]{1,0:T(8,128)S(1)} %slice.968), custom_call_target="Cholesky" | custom-call | tf_op jit(solution)/shard_map/cholesky/custom-call.1 | solution.py:39
  262.8 1.3 select_bitcast_fusion.3
  264.1 9.9 %custom-call.29 = f32[1,128,128]{1,2,0:T(8,128)S(1)} custom-call(f32[1,128,128]{2,1,0:T(8,128)S(1)} %get-tuple-element.405), custom_call_target="InvertDiagBlocksLowerTriangular" | custom-call | tf_op jit(solution)/shard_map/triangular_solve/custom-call.0 | solution.py:17
  276.6 5.7 %sort.33 = (s32[2560]{0:T(1024)}, s32[2560]{0:T(1024)S(1)}) sort(s32[2560]{0:T(1024)S(1)} %reshape.917, s32[2560]{0:T(1024)S(1)} %iota.303), dimensions={0}, to_apply=%region_4.7 | sort | flops 30720 | bytes 40960 | tf_op jit(solution)/shard_map/sort | solution.py:97
  284.2 4.6 gather_fusion.2
  289.0 2.5 convolution_subtract_fusion.4
  291.5 11.7 %custom-call.30 = f32[128,128]{1,0:T(8,128)S(1)} custom-call(f32[128,128]{1,0:T(8,128)S(1)} %slice.973), custom_call_target="Cholesky" | custom-call | tf_op jit(solution)/shard_map/cholesky/custom-call.1 | solution.py:39
  303.9 1.3 select_bitcast_fusion.2
  305.2 9.8 %custom-call.31 = f32[1,128,128]{1,2,0:T(8,128)S(1)} custom-call(f32[1,128,128]{2,1,0:T(8,128)S(1)} %get-tuple-element.403), custom_call_target="InvertDiagBlocksLowerTriangular" | custom-call | tf_op jit(solution)/shard_map/triangular_solve/custom-call.0 | solution.py:17
  316.3 2.1 convolution_subtract_fusion.5
  318.4 11.9 %custom-call.32 = f32[128,128]{1,0:T(8,128)S(1)} custom-call(f32[128,128]{1,0:T(8,128)S(1)} %slice.978), custom_call_target="Cholesky" | custom-call | tf_op jit(solution)/shard_map/cholesky/custom-call.1 | solution.py:39
  330.9 1.3 select_bitcast_fusion.1
  332.2 9.8 %custom-call.33 = f32[1,128,128]{1,2,0:T(8,128)S(1)} custom-call(f32[1,128,128]{2,1,0:T(8,128)S(1)} %get-tuple-element.401), custom_call_target="InvertDiagBlocksLowerTriangular" | custom-call | tf_op jit(solution)/shard_map/triangular_solve/custom-call.0 | solution.py:17
  343.3 1.8 convolution_subtract_fusion.6
  345.1 11.7 %custom-call.34 = f32[128,128]{1,0:T(8,128)S(1)} custom-call(f32[128,128]{1,0:T(8,128)S(1)} %convolution_subtract_fusion.6), custom_call_target="Cholesky" | custom-call | tf_op jit(solution)/shard_map/cholesky/custom-call.1 | solution.py:39
  357.5 1.3 select_bitcast_fusion
  361.3 1.3 fusion.55
  364.2 1.7 fusion.35
  367.6 2.4 fusion.26
  371.7 2.8 fusion.17
  376.3 3.2 fusion.15
  379.5 1.3 fusion.20
  381.4 4.2 fusion.13
  385.6 9.8 %custom-call.35 = f32[1,128,128]{1,2,0:T(8,128)S(1)} custom-call(f32[1,128,128]{2,1,0:T(8,128)S(1)} %get-tuple-element.399), custom_call_target="InvertDiagBlocksLowerTriangular" | custom-call | tf_op jit(solution)/shard_map/triangular_solve/custom-call.0 | solution.py:17
  395.8 1.4 constant_dynamic-slice_fusion.1
  397.1 1.3 fusion.19
  399.1 43.4 %all-reduce.7.cloned.1.call-done = f32[128,1024]{1,0:T(8,128)} async-done(((f32[128,1024]{1,0:T(8,128)}), f32[128,1024]{1,0:T(8,128)}) %all-reduce.7.cloned.1.call-update) | async-done | bytes 524304 | tf_op jit(solution)/shard_map/psum | solution.py:115
  442.5 7.1 %fusion.111 = f32[128,1024]{1,0:T(8,128)S(1)} fusion(f32[128,1024]{1,0:T(8,128)} %all-reduce.7.cloned.1.call-done, f32[1024,1024]{1,0:T(8,128)} %constant_dynamic-update-slice_fusion.4), kind=kOutput, calls=%fused_computation.225 | convolution fusion | flops 1610612736 | bytes 5242880 | tf_op jit(solution)/shard_map/dot_general | solution.py:21
  449.6 2.4 fusion.112
  452.7 6.4 %fusion.4 = f32[2560,128]{1,0:T(8,128)S(1)} fusion(f32[2560,1024]{1,0:T(8,128)} %all-gather.9.cloned.1.call-done, f32[2560]{0:T(1024)S(1)} %convert_element_type.54, f32[128,1024]{1,0:T(8,128)S(1)} %fusion.112), kind=kOutput, calls=%fused_computation.11 | convolution fusion | flops 2013593600 | bytes 6828032 | tf_op jit(solution)/shard_map/dot_general | solution.py:21
  459.1 6.5 %fusion.10 = f32[2560,128]{1,0:T(8,128)S(1)} fusion(f32[2560,128]{1,0:T(8,128)S(1)} %fusion.4, f32[2560,1024]{1,0:T(8,128)} %all-gather.9.cloned.1.call-done, f32[2560]{0:T(1024)S(1)} %convert_element_type.55, f32[128,1024]{1,0:T(8,128)S(1)} %fusion.112), kind=kOutput, calls=%fused_computation.13 | convolution fusion | flops 2013921280 | bytes 8138752 | tf_op jit(solution)/shard_map/dot_general | solution.py:21
  465.6 5.5 %gather_fusion.5 = f32[2048,128]{1,0:T(8,128)S(1)} fusion(f32[2560,128]{1,0:T(8,128)S(1)} %fusion.10, s32[2048]{0:T(1024)S(1)} %fusion.110), kind=kCustom, calls=%fused_computation.5 | custom fusion | bytes 2105344 | tf_op jit(solution)/shard_map/gather | solution.py:125
  471.1 1.2 sub.59
  (103 shorter events, 30.5 us)
Async XLA Ops:
  7.2 68.2 %copy-start.3 = (f32[36,1024]{1,0:T(8,128)S(1)}, f32[36,1024]{1,0:T(8,128)}, u32[]{:S(2)}) copy-start(f32[36,1024]{1,0:T(8,128)} %param.69) | copy-start | bytes 442372
  7.2 121.5 %copy-start.4 = (s32[2,32]{1,0:T(2,128)S(1)}, s32[2,32]{1,0:T(2,128)}, u32[]{:S(2)}) copy-start(s32[2,32]{1,0:T(2,128)} %param.71) | copy-start | bytes 772
  7.2 63.2 %all-gather.5.cloned.1.call-start = ((), (), s32[]{:S(2)}) async-start(), calls=%async_computation | async-start | bytes 1474560 | tf_op jit(solution)/shard_map/all_gather | solution.py:78
  40.1 88.5 %all-gather.7.cloned.1.call-start = ((), (), s32[]{:S(2)}) async-start(), calls=%async_computation.1 | async-start | bytes 5242880 | tf_op jit(solution)/shard_map/all_gather | solution.py:82
  75.2 200.3 %all-gather.9.cloned.1.call-start = ((), (), s32[]{:S(2)}) async-start(), calls=%async_computation.2 | async-start | bytes 10649600 | tf_op jit(solution)/shard_map/all_gather | solution.py:89
  128.6 313.9 %all-reduce.7.cloned.1.call-start = ((), (), s32[]{:S(2)}) async-start(), calls=%async_computation.3 | async-start | bytes 1048576 | tf_op jit(solution)/shard_map/psum | solution.py:115
  289.0 77.0 %copy-start.1 = (f32[128,1024]{1,0:T(8,128)}, f32[128,1024]{1,0:T(8,128)S(1)}, u32[]{:S(2)}) copy-start(f32[128,1024]{1,0:T(8,128)S(1)} %multiply_dynamic-update-slice_fusion) | copy-start | bytes 1572868
  442.5 7.1 %copy-start = (f32[1024,1024]{1,0:T(8,128)S(1)}, f32[1024,1024]{1,0:T(8,128)}, u32[]{:S(2)}) copy-start(f32[1024,1024]{1,0:T(8,128)} %constant_dynamic-update-slice_fusion.4) | copy-start | bytes 12582916
  465.6 5.5 %copy-start.2 = (f32[64,1,32,128]{3,2,1,0:T(8,128)S(1)}, f32[64,1,32,128]{3,2,1,0:T(8,128)}, u32[]{:S(2)}) copy-start(f32[64,1,32,128]{3,2,1,0:T(8,128)} %param.72) | copy-start | bytes 3145732
Sparse Core Ops, SparseCore 0:
  40.2 30.1 all-gather.4
  75.3 53.2 all-gather.6
  131.4 87.2 all-gather.8
  395.9 46.6 all-reduce.6

commit v4 on v3

--- a/solution.py
+++ b/solution.py
@@ -107,14 +107,11 @@
     column_first = jnp.arange(twice_width) < half_width
     own_keep = jnp.where(column_first[None, :], first_keep[own_src][:, None], second_keep[own_src][:, None])
     masked_own = gathered[own_src] * own_keep
-    placed_own = jnp.zeros((col_count * trail_rows, twice_width), jnp.float32)
-    placed_own = lax.dynamic_update_slice_in_dim(placed_own, masked_own, col_index * trail_rows, 0)
+    def exchange(tied):
+        own, first, second, source = tied
+        return (lax.all_gather(own, "col", axis=0, tiled=True), first, second, source)
 
-    def exchange(tied):
-        placed, first, second, source = tied
-        return (lax.psum(placed, "col"), first, second, source)
-
-    factor, inverse, tied = factor_and_inverse(full, (placed_own, first_keep, second_keep, trail_src), exchange)
+    factor, inverse, tied = factor_and_inverse(full, (masked_own, first_keep, second_keep, trail_src), exchange)
     masked_range, first_keep, second_keep, trail_src = tied
     range_panel = contract_rows(masked_range, inverse)
     panel = lax.dynamic_slice_in_dim(range_panel, col_index * trail_rows, trail_rows, 0)

time: 484 us -> 452 us (0.934)
  waiting for transfers between devices: 126 us -> 82.8 us
  blocking collectives: 27.2 us -> 37.3 us
    psum x1 -> x0, waiting for transfers between devices: 43.4 us -> none  [exchange(): return (lax.psum(placed, 'col'), first, second, source)]
    all_gather x0 -> x1, blocking collectives: none -> 10.2 us  [exchange(): lax.all_gather(own, 'col', axis=0, tiled=True)]
  transfers between devices with their start and end apart: 4 -> 3, of which waited for: 3 -> 2; matrix products, arithmetic and copies ran while one was open for 31% -> 33% of each run, Pallas kernels for 0% -> 0%
where the time goes in v4:
time: 452 us; the launch traced here: 445 us
  other arithmetic  201 us (44%)
  waiting for transfers between devices  82.8 us (18%)
  matrix products  71.4 us (16%)
  local copies, waits for them, and re-layouts  37.4 us (8%)
  blocking collectives  37.3 us (8%)
  between operations  14.5 us (3%)
    another operation x24, other arithmetic, factor_and_inverse(): block = jnp.tril(lax.linalg.cholesky(column[:size], symmetrize_input=False))  99.7 us
    another operation x16, other arithmetic, lower_inverse(): lax.linalg.triangular_solve(lower_factor, identity, left_side=True, lower...  88.5 us
    all_gather x1, waiting for transfers between devices, local(): full = lax.all_gather(diag_block, 'col', axis=0, tiled=True)  52.5 us
    dot_general x17, matrix products, contract_rows(): lax.dot_general(left_rows, right_rows, (((1,), (1,)), ((), ())), precisio...  42.4 us
    all_gather x1, waiting for transfers between devices, local(): diag_pack = lax.all_gather(diag_pack, axis, axis=0, tiled=True)  30.2 us
    all_gather x2, blocking collectives, local(): diag_pack = lax.all_gather(diag_pack, axis, axis=0, tiled=True)  27.2 us
    dot_general x15, matrix products, matmul(): lax.dot_general(left, right, (((1,), (0,)), ((), ())), precision=highest)  26.7 us
    all_gather x1, blocking collectives, exchange(): lax.all_gather(own, 'col', axis=0, tiled=True)  10.2 us
  transfers between devices with their start and end apart: 3, of which 2 were waited for; matrix products, arithmetic and copies ran while one was open for 33% of the time, Pallas kernels for 0%

profile of v4, /device:TPU:1, one launch (start us, length us, event | category | flops | bytes accessed | tf_op | source)
XLA Modules:
  0.0 445.0 jit_solution(649123525606412941)
XLA Ops:
  8.0 2.0 sort.32
  10.0 1.3 gather_fusion.1
  11.3 1.5 gather_fusion
  12.9 4.7 %all-gather = f32[2,4,1152]{2,1,0:T(4,128)S(1)} all-gather(f32[1,4,1152]{2,1,0:T(4,128)S(1)} %maximum_bitcast_fusion), channel_id=1, replica_groups=mesh['y'=4,'z'=8,'core'=2,'col'=4] {'core'}, dimensions={0}, use_global_device_ids=true | all-gather | bytes 55296 | tf_op jit(solution)/shard_map/all_gather | solution.py:78
  17.6 22.5 %all_gather.19 = f32[64,1152]{1,0:T(8,128)} all-gather(f32[8,1152]{1,0:T(8,128)S(1)} %reshape.996), channel_id=1, replica_groups=mesh['y'=4,'z'=8,'core'=2,'col'=4] {'z'}, dimensions={0}, use_global_device_ids=true | all-gather | bytes 331776 | tf_op jit(solution)/shard_map/all_gather | solution.py:78
  40.2 30.2 %all-gather.5.cloned.1.call-done = f32[256,1152]{1,0:T(8,128)} async-done(((f32[64,1152]{1,0:T(8,128)}), f32[256,1152]{1,0:T(8,128)}) %all-gather.5.cloned.1.call-update) | async-done | bytes 1179664 | tf_op jit(solution)/shard_map/all_gather | solution.py:78
  71.4 2.4 scatter_custom_fusion
  73.9 1.3 copy.51
  76.1 52.5 %all-gather.7.cloned.1.call-done = f32[1024,1024]{0,1:T(8,128)} async-done(((f32[256,1024]{0,1:T(8,128)}), f32[1024,1024]{0,1:T(8,128)}) %all-gather.7.cloned.1.call-update) | async-done | bytes 4194320 | tf_op jit(solution)/shard_map/all_gather | solution.py:82
  128.7 5.5 %copy.52 = f32[1024,1024]{1,0:T(8,128)} copy(f32[1024,1024]{0,1:T(8,128)} %all-gather.7.cloned.1.call-done) | data formatting | bytes 8388608 | tf_op jit(solution)/shard_map/optimization_barrier | solution.py:88
  135.1 1.3 fusion.37
  136.4 11.7 %custom-call.20 = f32[128,128]{1,0:T(8,128)S(1)} custom-call(f32[128,128]{1,0:T(8,128)S(1)} %slice.949), custom_call_target="Cholesky" | custom-call | tf_op jit(solution)/shard_map/cholesky/custom-call.1 | solution.py:39
  149.4 9.8 %custom-call.21 = f32[1,128,128]{1,2,0:T(8,128)S(1)} custom-call(f32[1,128,128]{2,1,0:T(8,128)S(1)} %get-tuple-element.397), custom_call_target="InvertDiagBlocksLowerTriangular" | custom-call | tf_op jit(solution)/shard_map/triangular_solve/custom-call.0 | solution.py:17
  159.2 2.6 scatter.114
  162.1 2.5 scatter.130
  164.6 1.3 constant_dynamic-update-slice_fusion
  165.9 1.7 convolution_subtract_fusion
  167.6 11.7 %custom-call.22 = f32[128,128]{1,0:T(8,128)S(1)} custom-call(f32[128,128]{1,0:T(8,128)S(1)} %slice.953), custom_call_target="Cholesky" | custom-call | tf_op jit(solution)/shard_map/cholesky/custom-call.1 | solution.py:39
  180.0 1.3 select_bitcast_fusion.6
  181.3 10.0 %custom-call.23 = f32[1,128,128]{1,2,0:T(8,128)S(1)} custom-call(f32[1,128,128]{2,1,0:T(8,128)S(1)} %get-tuple-element.411), custom_call_target="InvertDiagBlocksLowerTriangular" | custom-call | tf_op jit(solution)/shard_map/triangular_solve/custom-call.0 | solution.py:17
  191.6 1.3 convolution_dynamic-update-slice_fusion
  192.9 2.3 convolution_subtract_fusion.1
  195.1 11.7 %custom-call.24 = f32[128,128]{1,0:T(8,128)S(1)} custom-call(f32[128,128]{1,0:T(8,128)S(1)} %slice.958), custom_call_target="Cholesky" | custom-call | tf_op jit(solution)/shard_map/cholesky/custom-call.1 | solution.py:39
  207.5 1.3 select_bitcast_fusion.5
  208.9 9.8 %custom-call.25 = f32[1,128,128]{1,2,0:T(8,128)S(1)} custom-call(f32[1,128,128]{2,1,0:T(8,128)S(1)} %get-tuple-element.409), custom_call_target="InvertDiagBlocksLowerTriangular" | custom-call | tf_op jit(solution)/shard_map/triangular_solve/custom-call.0 | solution.py:17
  219.0 1.2 convolution_dynamic-update-slice_fusion.1
  220.2 2.4 convolution_subtract_fusion.2
  222.7 12.1 %custom-call.26 = f32[128,128]{1,0:T(8,128)S(1)} custom-call(f32[128,128]{1,0:T(8,128)S(1)} %slice.963), custom_call_target="Cholesky" | custom-call | tf_op jit(solution)/shard_map/cholesky/custom-call.1 | solution.py:39
  235.4 1.3 select_bitcast_fusion.4
  236.7 9.8 %custom-call.27 = f32[1,128,128]{1,2,0:T(8,128)S(1)} custom-call(f32[1,128,128]{2,1,0:T(8,128)S(1)} %get-tuple-element.407), custom_call_target="InvertDiagBlocksLowerTriangular" | custom-call | tf_op jit(solution)/shard_map/triangular_solve/custom-call.0 | solution.py:17
  248.0 2.4 convolution_subtract_fusion.3
  250.4 11.7 %custom-call.28 = f32[128,128]{1,0:T(8,128)S(1)} custom-call(f32[128,128]{1,0:T(8,128)S(1)} %slice.968), custom_call_target="Cholesky" | custom-call | tf_op jit(solution)/shard_map/cholesky/custom-call.1 | solution.py:39
  262.8 1.3 select_bitcast_fusion.3
  264.1 9.9 %custom-call.29 = f32[1,128,128]{1,2,0:T(8,128)S(1)} custom-call(f32[1,128,128]{2,1,0:T(8,128)S(1)} %get-tuple-element.405), custom_call_target="InvertDiagBlocksLowerTriangular" | custom-call | tf_op jit(solution)/shard_map/triangular_solve/custom-call.0 | solution.py:17
  276.6 5.7 %sort.33 = (s32[2560]{0:T(1024)}, s32[2560]{0:T(1024)S(1)}) sort(s32[2560]{0:T(1024)S(1)} %reshape.917, s32[2560]{0:T(1024)S(1)} %iota.303), dimensions={0}, to_apply=%region_4.7 | sort | flops 30720 | bytes 40960 | tf_op jit(solution)/shard_map/sort | solution.py:97
  284.1 4.6 %gather_fusion.2 = f32[32,1024]{1,0:T(8,128)S(1)} fusion(f32[2560,1024]{1,0:T(8,128)} %all-gather.9.cloned.1.call-done, s32[1024]{0:T(1024)S(1)} %pad_clamp_fusion), kind=kCustom, calls=%fused_computation.2 | custom fusion | bytes 262272 | tf_op jit(solution)/shard_map/gather | solution.py:109
  288.9 2.3 convolution_subtract_fusion.4
  291.2 11.7 %custom-call.30 = f32[128,128]{1,0:T(8,128)S(1)} custom-call(f32[128,128]{1,0:T(8,128)S(1)} %slice.973), custom_call_target="Cholesky" | custom-call | tf_op jit(solution)/shard_map/cholesky/custom-call.1 | solution.py:39
  303.6 1.3 select_bitcast_fusion.2
  304.9 9.8 %custom-call.31 = f32[1,128,128]{1,2,0:T(8,128)S(1)} custom-call(f32[1,128,128]{2,1,0:T(8,128)S(1)} %get-tuple-element.403), custom_call_target="InvertDiagBlocksLowerTriangular" | custom-call | tf_op jit(solution)/shard_map/triangular_solve/custom-call.0 | solution.py:17
  316.0 2.1 convolution_subtract_fusion.5
  318.1 11.9 %custom-call.32 = f32[128,128]{1,0:T(8,128)S(1)} custom-call(f32[128,128]{1,0:T(8,128)S(1)} %slice.978), custom_call_target="Cholesky" | custom-call | tf_op jit(solution)/shard_map/cholesky/custom-call.1 | solution.py:39
  330.7 1.3 select_bitcast_fusion.1
  332.0 9.8 %custom-call.33 = f32[1,128,128]{1,2,0:T(8,128)S(1)} custom-call(f32[1,128,128]{2,1,0:T(8,128)S(1)} %get-tuple-element.401), custom_call_target="InvertDiagBlocksLowerTriangular" | custom-call | tf_op jit(solution)/shard_map/triangular_solve/custom-call.0 | solution.py:17
  343.0 1.8 convolution_subtract_fusion.6
  344.8 11.7 %custom-call.34 = f32[128,128]{1,0:T(8,128)S(1)} custom-call(f32[128,128]{1,0:T(8,128)S(1)} %convolution_subtract_fusion.6), custom_call_target="Cholesky" | custom-call | tf_op jit(solution)/shard_map/cholesky/custom-call.1 | solution.py:39
  357.2 1.3 select_bitcast_fusion
  361.0 1.3 fusion.55
  363.9 1.7 fusion.35
  367.3 2.4 fusion.26
  371.4 2.8 fusion.17
  376.0 3.2 fusion.15
  379.2 1.3 fusion.20
  381.1 4.2 fusion.13
  385.3 9.8 %custom-call.35 = f32[1,128,128]{1,2,0:T(8,128)S(1)} custom-call(f32[1,128,128]{2,1,0:T(8,128)S(1)} %get-tuple-element.399), custom_call_target="InvertDiagBlocksLowerTriangular" | custom-call | tf_op jit(solution)/shard_map/triangular_solve/custom-call.0 | solution.py:17
  395.4 1.3 fusion.19
  397.4 10.2 %all_gather.23 = f32[128,1024]{1,0:T(8,128)S(1)} all-gather(f32[32,1024]{1,0:T(8,128)S(1)} %select_multiply_fusion), channel_id=1, replica_groups=mesh['y'=4,'z'=8,'core'=2,'col'=4] {'col'}, dimensions={0}, use_global_device_ids=true | all-gather | bytes 655360 | tf_op jit(solution)/shard_map/all_gather | solution.py:112
  407.6 6.6 %fusion.111 = f32[128,1024]{1,0:T(8,128)S(1)} fusion(f32[128,1024]{1,0:T(8,128)S(1)} %all_gather.23, f32[1024,1024]{1,0:T(8,128)} %constant_dynamic-update-slice_fusion.4), kind=kOutput, calls=%fused_computation.225 | convolution fusion | flops 1610612736 | bytes 5242880 | tf_op jit(solution)/shard_map/dot_general | solution.py:21
  414.2 2.4 fusion.112
  417.3 1.4 constant_dynamic-slice_fusion.1
  418.6 6.4 %fusion.4 = f32[2560,128]{1,0:T(8,128)S(1)} fusion(f32[2560,1024]{1,0:T(8,128)} %all-gather.9.cloned.1.call-done, f32[2560]{0:T(1024)S(1)} %convert_element_type.54, f32[128,1024]{1,0:T(8,128)S(1)} %fusion.112), kind=kOutput, calls=%fused_computation.11 | convolution fusion | flops 2013593600 | bytes 6828032 | tf_op jit(solution)/shard_map/dot_general | solution.py:21
  425.1 6.5 %fusion.10 = f32[2560,128]{1,0:T(8,128)S(1)} fusion(f32[2560,128]{1,0:T(8,128)S(1)} %fusion.4, f32[2560,1024]{1,0:T(8,128)} %all-gather.9.cloned.1.call-done, f32[2560]{0:T(1024)S(1)} %convert_element_type.55, f32[128,1024]{1,0:T(8,128)S(1)} %fusion.112), kind=kOutput, calls=%fused_computation.13 | convolution fusion | flops 2013921280 | bytes 8138752 | tf_op jit(solution)/shard_map/dot_general | solution.py:21
  431.6 5.5 %gather_fusion.5 = f32[2048,128]{1,0:T(8,128)S(1)} fusion(f32[2560,128]{1,0:T(8,128)S(1)} %fusion.10, s32[2048]{0:T(1024)S(1)} %fusion.110), kind=kCustom, calls=%fused_computation.5 | custom fusion | bytes 2105344 | tf_op jit(solution)/shard_map/gather | solution.py:122
  437.1 1.2 sub.59
  (98 shorter events, 30.4 us)
Async XLA Ops:
  7.2 68.2 %copy-start.2 = (f32[36,1024]{1,0:T(8,128)S(1)}, f32[36,1024]{1,0:T(8,128)}, u32[]{:S(2)}) copy-start(f32[36,1024]{1,0:T(8,128)} %param.69) | copy-start | bytes 442372
  7.2 121.5 %copy-start.3 = (s32[2,32]{1,0:T(2,128)S(1)}, s32[2,32]{1,0:T(2,128)}, u32[]{:S(2)}) copy-start(s32[2,32]{1,0:T(2,128)} %param.71) | copy-start | bytes 772
  7.2 63.2 %all-gather.5.cloned.1.call-start = ((), (), s32[]{:S(2)}) async-start(), calls=%async_computation | async-start | bytes 1474560 | tf_op jit(solution)/shard_map/all_gather | solution.py:78
  40.1 88.5 %all-gather.7.cloned.1.call-start = ((), (), s32[]{:S(2)}) async-start(), calls=%async_computation.1 | async-start | bytes 5242880 | tf_op jit(solution)/shard_map/all_gather | solution.py:82
  75.2 200.2 %all-gather.9.cloned.1.call-start = ((), (), s32[]{:S(2)}) async-start(), calls=%async_computation.2 | async-start | bytes 10649600 | tf_op jit(solution)/shard_map/all_gather | solution.py:89
  397.4 16.8 %copy-start = (f32[1024,1024]{1,0:T(8,128)S(1)}, f32[1024,1024]{1,0:T(8,128)}, u32[]{:S(2)}) copy-start(f32[1024,1024]{1,0:T(8,128)} %constant_dynamic-update-slice_fusion.4) | copy-start | bytes 12582916
  431.6 5.5 %copy-start.1 = (f32[64,1,32,128]{3,2,1,0:T(8,128)S(1)}, f32[64,1,32,128]{3,2,1,0:T(8,128)}, u32[]{:S(2)}) copy-start(f32[64,1,32,128]{3,2,1,0:T(8,128)} %param.72) | copy-start | bytes 3145732
Sparse Core Ops, SparseCore 0:
  40.2 30.1 all-gather.4
  75.3 53.2 all-gather.6
  131.4 87.4 all-gather.8

commit v5 on v4

--- a/solution.py
+++ b/solution.py
@@ -74,12 +74,11 @@
     diag_ids = row_map[order_ids].astype(jnp.float32)
     diag_pack = jnp.concatenate(
         [assembled[order_ids], jnp.broadcast_to(diag_ids[:, None], (diag_share, LANE_PAD))], axis=1)
-    for axis in WIDE_PARTS[::-1]:
+    for axis in ("core", "z", ("y", "col")):
         diag_pack = lax.all_gather(diag_pack, axis, axis=0, tiled=True)
-    diag_slot = diag_pack[:, twice_width].astype(jnp.int32) - diag_col * col_index
-    diag_block = jnp.zeros((diag_col, twice_width), jnp.float32).at[diag_slot].set(
+    diag_slot = diag_pack[:, twice_width].astype(jnp.int32)
+    full = jnp.zeros((twice_width, twice_width), jnp.float32).at[diag_slot].set(
         diag_pack[:, :twice_width], mode="drop")
-    full = lax.all_gather(diag_block, "col", axis=0, tiled=True)
 
     packed_rows = ((asm_rows + 1 + 7) // 8) * 8
     id_row = jnp.zeros((twice_width,), jnp.float32).at[:asm_rows].set(row_map.astype(jnp.float32))
@@ -109,7 +108,15 @@
     masked_own = gathered[own_src] * own_keep
     def exchange(tied):
         own, first, second, source = tied
-        return (lax.all_gather(own, "col", axis=0, tiled=True), first, second, source)
+        rows = own.shape[0]
+        owners = jnp.zeros((col_count * rows, own.shape[1]), jnp.float32)
+        owners = lax.dynamic_update_slice_in_dim(owners, own, col_index * rows, 0)
+        for shift in range(1, col_count):
+            pairs = [(c, (c + shift) % col_count) for c in range(col_count)]
+            arrived = lax.ppermute(own, "col", pairs)
+            owners = lax.dynamic_update_slice_in_dim(
+                owners, arrived, ((col_index - shift) % col_count) * rows, 0)
+        return (owners, first, second, source)
 
     factor, inverse, tied = factor_and_inverse(full, (masked_own, first_keep, second_keep, trail_src), exchange)
     masked_range, first_keep, second_keep, trail_src = tied

time: 452 us -> 431 us (0.954)
  waiting for transfers between devices: 82.8 us -> 62.4 us
  blocking collectives: 37.3 us -> 27.2 us
  local copies, waits for them, and re-layouts: 37.4 us -> 42.8 us
  starting transfers between devices: 0.12 us -> 4.93 us
    all_gather x1 -> x0, waiting for transfers between devices: 52.5 us -> none  [local(): full = lax.all_gather(diag_block, 'col', axis=0, tiled=True)]
    all_gather x1, waiting for transfers between devices: 30.2 us -> 62.3 us  [local(): diag_pack = lax.all_gather(diag_pack, axis, axis=0, tiled=True)]
    all_gather x1 -> x0, blocking collectives: 10.2 us -> none  [exchange(): lax.all_gather(own, 'col', axis=0, tiled=True)]
    ppermute x0 -> x3, starting transfers between devices: none -> 4.85 us  [exchange(): arrived = lax.ppermute(own, 'col', pairs)]
    scatter x2 -> x1, local copies, waits for them, and re-layouts: 3.74 us -> 8.35 us  [local(): jnp.zeros((twice_width, twice_width), jnp.float32).at[diag_slot]]
  transfers between devices with their start and end apart: 3 -> 5, of which waited for: 2 -> 1; matrix products, arithmetic and copies ran while one was open for 33% -> 61% of each run, Pallas kernels for 0% -> 0%
where the time goes in v5:
time: 431 us; the launch traced here: 426 us
  other arithmetic  203 us (47%)
  matrix products  71.3 us (17%)
  waiting for transfers between devices  62.4 us (14%)
  local copies, waits for them, and re-layouts  42.8 us (10%)
  blocking collectives  27.2 us (6%)
  between operations  14.9 us (3%)
  starting transfers between devices  4.93 us (1%)
    another operation x24, other arithmetic, factor_and_inverse(): block = jnp.tril(lax.linalg.cholesky(column[:size], symmetrize_input=False))  99.5 us
    another operation x16, other arithmetic, lower_inverse(): lax.linalg.triangular_solve(lower_factor, identity, left_side=True, lower...  88.9 us
    all_gather x1, waiting for transfers between devices, local(): diag_pack = lax.all_gather(diag_pack, axis, axis=0, tiled=True)  62.3 us
    dot_general x17, matrix products, contract_rows(): lax.dot_general(left_rows, right_rows, (((1,), (1,)), ((), ())), precisio...  42.6 us
    all_gather x2, blocking collectives, local(): diag_pack = lax.all_gather(diag_pack, axis, axis=0, tiled=True)  27.2 us
    dot_general x15, matrix products, matmul(): lax.dot_general(left, right, (((1,), (0,)), ((), ())), precision=highest)  26.5 us
  transfers between devices with their start and end apart: 5, of which 1 were waited for; matrix products, arithmetic and copies ran while one was open for 61% of the time, Pallas kernels for 0%

profile of v5, /device:TPU:1, one launch (start us, length us, event | category | flops | bytes accessed | tf_op | source)
XLA Modules:
  0.0 426.1 jit_solution(7633676759942442924)
XLA Ops:
  7.9 2.0 sort.32
  10.0 1.3 gather_fusion.1
  11.3 1.5 gather_fusion
  12.9 4.7 %all-gather = f32[2,4,1152]{2,1,0:T(4,128)S(1)} all-gather(f32[1,4,1152]{2,1,0:T(4,128)S(1)} %maximum_bitcast_fusion), channel_id=1, replica_groups=mesh['y'=4,'z'=8,'core'=2,'col'=4] {'core'}, dimensions={0}, use_global_device_ids=true | all-gather | bytes 55296 | tf_op jit(solution)/shard_map/all_gather | solution.py:78
  17.6 22.5 %all_gather.13 = f32[64,1152]{1,0:T(8,128)} all-gather(f32[8,1152]{1,0:T(8,128)S(1)} %reshape.996), channel_id=1, replica_groups=mesh['y'=4,'z'=8,'core'=2,'col'=4] {'z'}, dimensions={0}, use_global_device_ids=true | all-gather | bytes 331776 | tf_op jit(solution)/shard_map/all_gather | solution.py:78
  40.2 1.7 fusion.79
  41.9 62.3 %all-gather.4.cloned.1.call-done = f32[1024,1152]{1,0:T(8,128)} async-done(((f32[64,1152]{1,0:T(8,128)}), f32[1024,1152]{1,0:T(8,128)}) %all-gather.4.cloned.1.call-update) | async-done | bytes 4718608 | tf_op jit(solution)/shard_map/all_gather | solution.py:78
  104.2 1.3 fusion.38
  105.5 8.4 %scatter_custom_fusion = f32[1024,1024]{1,0:T(8,128)} fusion(s32[1024]{0:T(1024)S(1)} %fusion.38, f32[1024,1152]{1,0:T(8,128)} %all-gather.4.cloned.1.call-done, f32[]{:T(128)} %constant.876.clone.1), kind=kCustom, calls=%fused_computation.11 | custom fusion | bytes 8389120 | tf_op jit(solution)/shard_map/scatter | solution.py:80
  113.9 5.9 %copy.51 = f32[1024,1024]{0,1:T(8,128)} copy(f32[1024,1024]{1,0:T(8,128)} %scatter_custom_fusion) | data formatting | bytes 8388608 | tf_op jit(solution)/shard_map/optimization_barrier | solution.py:87
  120.7 1.3 fusion.40
  122.0 11.7 %custom-call.20 = f32[128,128]{1,0:T(8,128)S(1)} custom-call(f32[128,128]{1,0:T(8,128)S(1)} %slice.949), custom_call_target="Cholesky" | custom-call | tf_op jit(solution)/shard_map/cholesky/custom-call.1 | solution.py:39
  135.0 9.8 %custom-call.21 = f32[1,128,128]{1,2,0:T(8,128)S(1)} custom-call(f32[1,128,128]{2,1,0:T(8,128)S(1)} %get-tuple-element.397), custom_call_target="InvertDiagBlocksLowerTriangular" | custom-call | tf_op jit(solution)/shard_map/triangular_solve/custom-call.0 | solution.py:17
  144.9 2.6 scatter.114
  147.7 2.6 scatter.130
  150.3 1.3 constant_dynamic-update-slice_fusion.4
  151.7 1.7 convolution_subtract_fusion
  153.4 11.7 %custom-call.22 = f32[128,128]{1,0:T(8,128)S(1)} custom-call(f32[128,128]{1,0:T(8,128)S(1)} %slice.953), custom_call_target="Cholesky" | custom-call | tf_op jit(solution)/shard_map/cholesky/custom-call.1 | solution.py:39
  165.8 1.3 select_bitcast_fusion.6
  167.1 9.9 %custom-call.23 = f32[1,128,128]{1,2,0:T(8,128)S(1)} custom-call(f32[1,128,128]{2,1,0:T(8,128)S(1)} %get-tuple-element.411), custom_call_target="InvertDiagBlocksLowerTriangular" | custom-call | tf_op jit(solution)/shard_map/triangular_solve/custom-call.0 | solution.py:17
  177.3 1.3 convolution_dynamic-update-slice_fusion
  178.6 2.2 convolution_subtract_fusion.1
  180.8 11.7 %custom-call.24 = f32[128,128]{1,0:T(8,128)S(1)} custom-call(f32[128,128]{1,0:T(8,128)S(1)} %slice.958), custom_call_target="Cholesky" | custom-call | tf_op jit(solution)/shard_map/cholesky/custom-call.1 | solution.py:39
  193.2 1.3 select_bitcast_fusion.5
  194.5 9.8 %custom-call.25 = f32[1,128,128]{1,2,0:T(8,128)S(1)} custom-call(f32[1,128,128]{2,1,0:T(8,128)S(1)} %get-tuple-element.409), custom_call_target="InvertDiagBlocksLowerTriangular" | custom-call | tf_op jit(solution)/shard_map/triangular_solve/custom-call.0 | solution.py:17
  204.6 1.2 convolution_dynamic-update-slice_fusion.1
  205.9 2.4 convolution_subtract_fusion.2
  208.3 12.1 %custom-call.26 = f32[128,128]{1,0:T(8,128)S(1)} custom-call(f32[128,128]{1,0:T(8,128)S(1)} %slice.963), custom_call_target="Cholesky" | custom-call | tf_op jit(solution)/shard_map/cholesky/custom-call.1 | solution.py:39
  221.1 1.3 select_bitcast_fusion.4
  222.4 9.8 %custom-call.27 = f32[1,128,128]{1,2,0:T(8,128)S(1)} custom-call(f32[1,128,128]{2,1,0:T(8,128)S(1)} %get-tuple-element.407), custom_call_target="InvertDiagBlocksLowerTriangular" | custom-call | tf_op jit(solution)/shard_map/triangular_solve/custom-call.0 | solution.py:17
  233.6 2.4 convolution_subtract_fusion.3
  236.1 11.7 %custom-call.28 = f32[128,128]{1,0:T(8,128)S(1)} custom-call(f32[128,128]{1,0:T(8,128)S(1)} %slice.968), custom_call_target="Cholesky" | custom-call | tf_op jit(solution)/shard_map/cholesky/custom-call.1 | solution.py:39
  248.4 1.3 select_bitcast_fusion.3
  249.7 9.9 %custom-call.29 = f32[1,128,128]{1,2,0:T(8,128)S(1)} custom-call(f32[1,128,128]{2,1,0:T(8,128)S(1)} %get-tuple-element.405), custom_call_target="InvertDiagBlocksLowerTriangular" | custom-call | tf_op jit(solution)/shard_map/triangular_solve/custom-call.0 | solution.py:17
  262.3 5.7 %sort.33 = (s32[2560]{0:T(1024)}, s32[2560]{0:T(1024)S(1)}) sort(s32[2560]{0:T(1024)S(1)} %reshape.917, s32[2560]{0:T(1024)S(1)} %iota.303), dimensions={0}, to_apply=%region_4.7 | sort | flops 30720 | bytes 40960 | tf_op jit(solution)/shard_map/sort | solution.py:96
  269.8 4.6 %gather_fusion.2 = f32[32,1024]{1,0:T(8,128)S(1)} fusion(f32[2560,1024]{1,0:T(8,128)} %all-gather.6.cloned.1.call-done, s32[1024]{0:T(1024)S(1)} %pad_clamp_fusion), kind=kCustom, calls=%fused_computation.2 | custom fusion | bytes 262272 | tf_op jit(solution)/shard_map/gather | solution.py:108
  274.6 1.3 collective-permute-start
  275.8 2.4 collective-permute-start.1
  279.4 2.3 convolution_subtract_fusion.4
  281.8 11.7 %custom-call.30 = f32[128,128]{1,0:T(8,128)S(1)} custom-call(f32[128,128]{1,0:T(8,128)S(1)} %slice.973), custom_call_target="Cholesky" | custom-call | tf_op jit(solution)/shard_map/cholesky/custom-call.1 | solution.py:39
  294.2 1.3 select_bitcast_fusion.2
  295.5 9.8 %custom-call.31 = f32[1,128,128]{1,2,0:T(8,128)S(1)} custom-call(f32[1,128,128]{2,1,0:T(8,128)S(1)} %get-tuple-element.403), custom_call_target="InvertDiagBlocksLowerTriangular" | custom-call | tf_op jit(solution)/shard_map/triangular_solve/custom-call.0 | solution.py:17
  306.5 2.1 convolution_subtract_fusion.5
  308.6 11.7 %custom-call.32 = f32[128,128]{1,0:T(8,128)S(1)} custom-call(f32[128,128]{1,0:T(8,128)S(1)} %slice.978), custom_call_target="Cholesky" | custom-call | tf_op jit(solution)/shard_map/cholesky/custom-call.1 | solution.py:39
  321.0 1.3 select_bitcast_fusion.1
  322.3 10.2 %custom-call.33 = f32[1,128,128]{1,2,0:T(8,128)S(1)} custom-call(f32[1,128,128]{2,1,0:T(8,128)S(1)} %get-tuple-element.401), custom_call_target="InvertDiagBlocksLowerTriangular" | custom-call | tf_op jit(solution)/shard_map/triangular_solve/custom-call.0 | solution.py:17
  333.7 1.8 convolution_subtract_fusion.6
  335.5 11.7 %custom-call.34 = f32[128,128]{1,0:T(8,128)S(1)} custom-call(f32[128,128]{1,0:T(8,128)S(1)} %convolution_subtract_fusion.6), custom_call_target="Cholesky" | custom-call | tf_op jit(solution)/shard_map/cholesky/custom-call.1 | solution.py:39
  347.9 1.3 select_bitcast_fusion
  351.7 1.3 fusion.60
  354.6 1.7 fusion.36
  358.0 2.0 fusion.29
  361.8 2.8 fusion.20
  366.3 3.4 fusion.17
  369.8 1.2 fusion.23
  371.6 4.2 fusion.15
  375.8 9.8 %custom-call.35 = f32[1,128,128]{1,2,0:T(8,128)S(1)} custom-call(f32[1,128,128]{2,1,0:T(8,128)S(1)} %get-tuple-element.399), custom_call_target="InvertDiagBlocksLowerTriangular" | custom-call | tf_op jit(solution)/shard_map/triangular_solve/custom-call.0 | solution.py:17
  385.9 1.3 fusion.22
  387.9 1.5 constant_dynamic-slice_fusion.1
  389.6 6.6 %fusion.117 = f32[128,1024]{1,0:T(8,128)S(1)} fusion(f32[128,1024]{1,0:T(8,128)S(1)} %constant_dynamic-update-slice_fusion, f32[1024,1024]{1,0:T(8,128)} %constant_dynamic-update-slice_fusion.9), kind=kOutput, calls=%fused_computation.235 | convolution fusion | flops 1610612736 | bytes 5242880 | tf_op jit(solution)/shard_map/dot_general | solution.py:21
  396.1 2.4 fusion.118
  399.2 6.6 %fusion.6 = f32[2560,128]{1,0:T(8,128)S(1)} fusion(f32[2560,1024]{1,0:T(8,128)} %all-gather.6.cloned.1.call-done, f32[2560]{0:T(1024)S(1)} %convert_element_type.54, f32[128,1024]{1,0:T(8,128)S(1)} %fusion.118), kind=kOutput, calls=%fused_computation.13 | convolution fusion | flops 2013593600 | bytes 6828032 | tf_op jit(solution)/shard_map/dot_general | solution.py:21
  405.9 6.5 %fusion.12 = f32[2560,128]{1,0:T(8,128)S(1)} fusion(f32[2560,128]{1,0:T(8,128)S(1)} %fusion.6, f32[2560,1024]{1,0:T(8,128)} %all-gather.6.cloned.1.call-done, f32[2560]{0:T(1024)S(1)} %convert_element_type.55, f32[128,1024]{1,0:T(8,128)S(1)} %fusion.118), kind=kOutput, calls=%fused_computation.15 | convolution fusion | flops 2013921280 | bytes 8138752 | tf_op jit(solution)/shard_map/dot_general | solution.py:21
  412.4 5.5 %gather_fusion.5 = f32[2048,128]{1,0:T(8,128)S(1)} fusion(f32[2560,128]{1,0:T(8,128)S(1)} %fusion.12, s32[2048]{0:T(1024)S(1)} %fusion.116), kind=kCustom, calls=%fused_computation.5 | custom fusion | bytes 2105344 | tf_op jit(solution)/shard_map/gather | solution.py:129
  (102 shorter events, 31.1 us)
Async XLA Ops:
  7.2 97.0 %all-gather.4.cloned.1.call-start = ((), (), s32[]{:S(2)}) async-start(), calls=%async_computation | async-start | bytes 5013504 | tf_op jit(solution)/shard_map/all_gather | solution.py:78
  40.1 221.0 %all-gather.6.cloned.1.call-start = ((), (), s32[]{:S(2)}) async-start(), calls=%async_computation.1 | async-start | bytes 10649600 | tf_op jit(solution)/shard_map/all_gather | solution.py:88
  105.4 8.5 %copy-start.2 = (s32[2,32]{1,0:T(2,128)S(1)}, s32[2,32]{1,0:T(2,128)}, u32[]{:S(2)}) copy-start(s32[2,32]{1,0:T(2,128)} %param.71) | copy-start | bytes 772
  274.6 114.9 %collective-permute-start = (f32[32,1024]{1,0:T(8,128)S(1)}, f32[32,1024]{1,0:T(8,128)S(1)}, u32[]{:S(2)}, u32[]{:S(2)}) collective-permute-start(f32[32,1024]{1,0:T(8,128)S(1)} %select_multiply_fusion), channel_id=1, source_target_pairs={{0,1},{1,2},{2,3},{3,0},{4,5},{5,6},{6,7},{7,4},{8,9},{9,10},{10,1... | collective-permute-start | bytes 393224 | tf_op jit(solution)/shard_map/ppermute | solution.py:116
  275.8 113.6 %collective-permute-start.1 = (f32[32,1024]{1,0:T(8,128)S(1)}, f32[32,1024]{1,0:T(8,128)S(1)}, u32[]{:S(2)}, u32[]{:S(2)}) collective-permute-start(f32[32,1024]{1,0:T(8,128)S(1)} %select_multiply_fusion), channel_id=1, source_target_pairs={{0,2},{1,3},{2,0},{3,1},{4,6},{5,7},{6,4},{7,5},{8,10},{9,11},{10,... | collective-permute-start | bytes 393224 | tf_op jit(solution)/shard_map/ppermute | solution.py:116
  278.2 111.3 %collective-permute-start.2 = (f32[32,1024]{1,0:T(8,128)S(1)}, f32[32,1024]{1,0:T(8,128)S(1)}, u32[]{:S(2)}, u32[]{:S(2)}) collective-permute-start(f32[32,1024]{1,0:T(8,128)S(1)} %select_multiply_fusion), channel_id=1, source_target_pairs={{0,3},{1,0},{2,1},{3,2},{4,7},{5,4},{6,5},{7,6},{8,11},{9,8},{10,9... | collective-permute-start | bytes 393224 | tf_op jit(solution)/shard_map/ppermute | solution.py:116
  387.9 8.2 %copy-start = (f32[1024,1024]{1,0:T(8,128)S(1)}, f32[1024,1024]{1,0:T(8,128)}, u32[]{:S(2)}) copy-start(f32[1024,1024]{1,0:T(8,128)} %constant_dynamic-update-slice_fusion.9) | copy-start | bytes 12582916
  412.4 5.5 %copy-start.1 = (f32[64,1,32,128]{3,2,1,0:T(8,128)S(1)}, f32[64,1,32,128]{3,2,1,0:T(8,128)}, u32[]{:S(2)}) copy-start(f32[64,1,32,128]{3,2,1,0:T(8,128)} %param.72) | copy-start | bytes 3145732
Sparse Core Ops, SparseCore 0:
  40.2 63.9 all-gather.3
  114.0 86.9 all-gather.5

commit v6 on v5

--- a/solution.py
+++ b/solution.py
@@ -74,30 +74,27 @@
     diag_ids = row_map[order_ids].astype(jnp.float32)
     diag_pack = jnp.concatenate(
         [assembled[order_ids], jnp.broadcast_to(diag_ids[:, None], (diag_share, LANE_PAD))], axis=1)
-    for axis in ("core", "z", ("y", "col")):
+    for axis in (("z", "core"), ("y", "col")):
         diag_pack = lax.all_gather(diag_pack, axis, axis=0, tiled=True)
     diag_slot = diag_pack[:, twice_width].astype(jnp.int32)
     full = jnp.zeros((twice_width, twice_width), jnp.float32).at[diag_slot].set(
         diag_pack[:, :twice_width], mode="drop")
 
-    packed_rows = ((asm_rows + 1 + 7) // 8) * 8
-    id_row = jnp.zeros((twice_width,), jnp.float32).at[:asm_rows].set(row_map.astype(jnp.float32))
+    trail_order = jnp.argsort(jnp.where(is_diagonal, 1, 0), stable=True)[:asm_rows - diag_share]
+    trail_ids = row_map[trail_order]
     packed = jnp.concatenate(
-        [assembled, id_row[None, :], jnp.zeros((packed_rows - asm_rows - 1, twice_width), jnp.float32)], axis=0)
+        [assembled[trail_order],
+         jnp.broadcast_to(trail_ids.astype(jnp.float32)[:, None], (asm_rows - diag_share, LANE_PAD))], axis=1)
     packed, full = lax.optimization_barrier((packed, full))
     gathered = lax.all_gather(packed, WIDE_PARTS, axis=0, tiled=True)
-    gathered3 = gathered.reshape(wide_count, packed_rows, twice_width)
-    ids = gathered3[:, asm_rows, :asm_rows].astype(jnp.int32)
+    ids = gathered[:, twice_width].astype(jnp.int32)
+    gathered = gathered[:, :twice_width]
     trail_id = ids - twice_width
-    trail_slot = (trail_id // (trail_rows * col_count)) * trail_rows + trail_id % trail_rows
-    key = jnp.where(ids >= twice_width, trail_slot, trail_col)
-    key = jnp.concatenate([key, jnp.full((wide_count, packed_rows - asm_rows), trail_col, jnp.int32)], axis=1)
-    key = key.reshape(-1)
+    key = (trail_id // (trail_rows * col_count)) * trail_rows + trail_id % trail_rows
     _, order = lax.sort((key, jnp.arange(key.shape[0], dtype=jnp.int32)), num_keys=1)
-    trail_src = order[:trail_col]
+    trail_src = order
 
-    block_of = jnp.concatenate(
-        [trail_id // BLOCK, jnp.full((wide_count, packed_rows - asm_rows), -1, jnp.int32)], axis=1).reshape(-1)
+    block_of = trail_id // BLOCK
     block_hits = (block_of[:, None] == jnp.arange(blocks)[None, :]).astype(jnp.int32)
     first_keep = jnp.sum(block_hits * fill_pattern[0][None, :], axis=1).astype(jnp.float32)
     second_keep = jnp.sum(block_hits * fill_pattern[1][None, :], axis=1).astype(jnp.float32)

time: 431 us -> 424 us (0.984)
  waiting for transfers between devices: 62.4 us -> 51.7 us
  local copies, waits for them, and re-layouts: 42.8 us -> 51.2 us
  blocking collectives: 27.2 us -> 22.1 us
    all_gather x1, waiting for transfers between devices: 62.3 us -> 51.6 us  [local(): diag_pack = lax.all_gather(diag_pack, axis, axis=0, tiled=True)]
    slice x2 -> x1, local copies, waits for them, and re-layouts: 0.98 us -> 8.35 us  [local(): gathered = gathered[:, :twice_width]]
    all_gather x2 -> x1, blocking collectives: 27.2 us -> 22.1 us  [local(): diag_pack = lax.all_gather(diag_pack, axis, axis=0, tiled=True)]
  transfers between devices with their start and end apart: 5 -> 5, of which waited for: 1 -> 1; matrix products, arithmetic and copies ran while one was open for 61% -> 62% of each run, Pallas kernels for 0% -> 0%
where the time goes in v6:
time: 424 us; the launch traced here: 419 us
  other arithmetic  205 us (48%)
  matrix products  69 us (16%)
  waiting for transfers between devices  51.7 us (12%)
  local copies, waits for them, and re-layouts  51.2 us (12%)
  blocking collectives  22.1 us (5%)
  between operations  14.9 us (4%)
  starting transfers between devices  4.91 us (1%)
    another operation x24, other arithmetic, factor_and_inverse(): block = jnp.tril(lax.linalg.cholesky(column[:size], symmetrize_input=False))  99.5 us
    another operation x16, other arithmetic, lower_inverse(): lax.linalg.triangular_solve(lower_factor, identity, left_side=True, lower...  88.9 us
    all_gather x1, waiting for transfers between devices, local(): diag_pack = lax.all_gather(diag_pack, axis, axis=0, tiled=True)  51.6 us
    dot_general x17, matrix products, contract_rows(): lax.dot_general(left_rows, right_rows, (((1,), (1,)), ((), ())), precisio...  40.3 us
    dot_general x15, matrix products, matmul(): lax.dot_general(left, right, (((1,), (0,)), ((), ())), precision=highest)  26.4 us
    all_gather x1, blocking collectives, local(): diag_pack = lax.all_gather(diag_pack, axis, axis=0, tiled=True)  22.1 us
  transfers between devices with their start and end apart: 5, of which 1 were waited for; matrix products, arithmetic and copies ran while one was open for 62% of the time, Pallas kernels for 0%

profile of v6, /device:TPU:1, one launch (start us, length us, event | category | flops | bytes accessed | tf_op | source)
XLA Modules:
  0.0 419.2 jit_solution(13847846254501352172)
XLA Ops:
  7.9 2.0 sort.47
  10.0 1.3 gather_fusion.3
  11.9 22.1 %all-gather = f32[16,4,1152]{2,1,0:T(4,128)S(1)} all-gather(f32[1,4,1152]{2,1,0:T(4,128)S(1)} %maximum_bitcast_fusion), channel_id=1, replica_groups=mesh['y'=4,'z'=8,'core'=2,'col'=4] {'z','core'}, dimensions={0}, use_global_device_ids=true | all-gather | bytes 313344 | tf_op jit(solution)/shard_map/all_gather | solution.py:78
  34.9 2.0 sort.46
  37.6 1.4 gather_fusion.1
  39.7 51.6 %all-gather.4.cloned.1.call-done = f32[1024,1152]{1,0:T(8,128)} async-done(((f32[64,1152]{1,0:T(8,128)}), f32[1024,1152]{1,0:T(8,128)}) %all-gather.4.cloned.1.call-update) | async-done | bytes 4718608 | tf_op jit(solution)/shard_map/all_gather | solution.py:78
  91.3 1.3 fusion.43
  92.6 8.4 %scatter_custom_fusion = f32[1024,1024]{1,0:T(8,128)} fusion(s32[1024]{0:T(1024)S(1)} %fusion.43, f32[1024,1152]{1,0:T(8,128)} %all-gather.4.cloned.1.call-done, f32[]{:T(128)} %constant.853.clone.1), kind=kCustom, calls=%fused_computation.13 | custom fusion | bytes 8389120 | tf_op jit(solution)/shard_map/scatter | solution.py:80
  101.1 5.9 %copy.47 = f32[1024,1024]{0,1:T(8,128)} copy(f32[1024,1024]{1,0:T(8,128)} %scatter_custom_fusion) | data formatting | bytes 8388608 | tf_op jit(solution)/shard_map/optimization_barrier | solution.py:88
  107.9 1.3 fusion.45
  109.2 11.7 %custom-call.20 = f32[128,128]{1,0:T(8,128)S(1)} custom-call(f32[128,128]{1,0:T(8,128)S(1)} %slice.948), custom_call_target="Cholesky" | custom-call | tf_op jit(solution)/shard_map/cholesky/custom-call.1 | solution.py:39
  122.3 9.8 %custom-call.21 = f32[1,128,128]{1,2,0:T(8,128)S(1)} custom-call(f32[1,128,128]{2,1,0:T(8,128)S(1)} %get-tuple-element.389), custom_call_target="InvertDiagBlocksLowerTriangular" | custom-call | tf_op jit(solution)/shard_map/triangular_solve/custom-call.0 | solution.py:17
  132.1 2.5 scatter.109
  134.9 2.5 scatter.125
  137.4 1.3 constant_dynamic-update-slice_fusion.4
  138.7 1.7 convolution_subtract_fusion
  140.4 11.7 %custom-call.22 = f32[128,128]{1,0:T(8,128)S(1)} custom-call(f32[128,128]{1,0:T(8,128)S(1)} %slice.952), custom_call_target="Cholesky" | custom-call | tf_op jit(solution)/shard_map/cholesky/custom-call.1 | solution.py:39
  152.8 1.3 select_bitcast_fusion.6
  154.1 10.0 %custom-call.23 = f32[1,128,128]{1,2,0:T(8,128)S(1)} custom-call(f32[1,128,128]{2,1,0:T(8,128)S(1)} %get-tuple-element.403), custom_call_target="InvertDiagBlocksLowerTriangular" | custom-call | tf_op jit(solution)/shard_map/triangular_solve/custom-call.0 | solution.py:17
  164.4 1.3 convolution_dynamic-update-slice_fusion
  165.6 2.5 convolution_subtract_fusion.1
  168.1 11.7 %custom-call.24 = f32[128,128]{1,0:T(8,128)S(1)} custom-call(f32[128,128]{1,0:T(8,128)S(1)} %slice.957), custom_call_target="Cholesky" | custom-call | tf_op jit(solution)/shard_map/cholesky/custom-call.1 | solution.py:39
  180.5 1.3 select_bitcast_fusion.5
  181.8 9.8 %custom-call.25 = f32[1,128,128]{1,2,0:T(8,128)S(1)} custom-call(f32[1,128,128]{2,1,0:T(8,128)S(1)} %get-tuple-element.401), custom_call_target="InvertDiagBlocksLowerTriangular" | custom-call | tf_op jit(solution)/shard_map/triangular_solve/custom-call.0 | solution.py:17
  191.9 1.2 convolution_dynamic-update-slice_fusion.1
  193.1 2.4 convolution_subtract_fusion.2
  195.6 12.1 %custom-call.26 = f32[128,128]{1,0:T(8,128)S(1)} custom-call(f32[128,128]{1,0:T(8,128)S(1)} %slice.962), custom_call_target="Cholesky" | custom-call | tf_op jit(solution)/shard_map/cholesky/custom-call.1 | solution.py:39
  208.4 1.3 select_bitcast_fusion.4
  209.7 9.8 %custom-call.27 = f32[1,128,128]{1,2,0:T(8,128)S(1)} custom-call(f32[1,128,128]{2,1,0:T(8,128)S(1)} %get-tuple-element.399), custom_call_target="InvertDiagBlocksLowerTriangular" | custom-call | tf_op jit(solution)/shard_map/triangular_solve/custom-call.0 | solution.py:17
  220.9 2.4 convolution_subtract_fusion.3
  223.3 11.7 %custom-call.28 = f32[128,128]{1,0:T(8,128)S(1)} custom-call(f32[128,128]{1,0:T(8,128)S(1)} %slice.967), custom_call_target="Cholesky" | custom-call | tf_op jit(solution)/shard_map/cholesky/custom-call.1 | solution.py:39
  235.7 1.3 select_bitcast_fusion.3
  237.0 9.9 %custom-call.29 = f32[1,128,128]{1,2,0:T(8,128)S(1)} custom-call(f32[1,128,128]{2,1,0:T(8,128)S(1)} %get-tuple-element.397), custom_call_target="InvertDiagBlocksLowerTriangular" | custom-call | tf_op jit(solution)/shard_map/triangular_solve/custom-call.0 | solution.py:17
  248.4 2.4 fusion.30
  250.9 5.0 %sort.48 = (s32[2048]{0:T(1024)}, s32[2048]{0:T(1024)S(1)}) sort(s32[2048]{0:T(1024)S(1)} %fusion.111, s32[2048]{0:T(1024)S(1)} %iota.307), dimensions={0}, to_apply=%region_5.8 | sort | flops 22528 | bytes 32768 | tf_op jit(solution)/shard_map/sort | solution.py:94
  257.6 8.4 %slice.969 = f32[2048,1024]{1,0:T(8,128)} slice(f32[2048,1152]{1,0:T(8,128)} %all-gather.6.cloned.1.call-done), slice={[0:2048], [0:1024]} | slice | bytes 16777216 | tf_op jit(solution)/shard_map/slice | solution.py:91
  265.9 4.1 gather_fusion.4
  271.3 2.5 collective-permute-start.1
  274.9 2.3 convolution_subtract_fusion.4
  277.3 11.7 %custom-call.30 = f32[128,128]{1,0:T(8,128)S(1)} custom-call(f32[128,128]{1,0:T(8,128)S(1)} %slice.973), custom_call_target="Cholesky" | custom-call | tf_op jit(solution)/shard_map/cholesky/custom-call.1 | solution.py:39
  289.7 1.3 select_bitcast_fusion.2
  290.9 9.8 %custom-call.31 = f32[1,128,128]{1,2,0:T(8,128)S(1)} custom-call(f32[1,128,128]{2,1,0:T(8,128)S(1)} %get-tuple-element.395), custom_call_target="InvertDiagBlocksLowerTriangular" | custom-call | tf_op jit(solution)/shard_map/triangular_solve/custom-call.0 | solution.py:17
  302.0 2.1 convolution_subtract_fusion.5
  304.1 11.7 %custom-call.32 = f32[128,128]{1,0:T(8,128)S(1)} custom-call(f32[128,128]{1,0:T(8,128)S(1)} %slice.978), custom_call_target="Cholesky" | custom-call | tf_op jit(solution)/shard_map/cholesky/custom-call.1 | solution.py:39
  316.5 1.3 select_bitcast_fusion.1
  317.8 10.2 %custom-call.33 = f32[1,128,128]{1,2,0:T(8,128)S(1)} custom-call(f32[1,128,128]{2,1,0:T(8,128)S(1)} %get-tuple-element.393), custom_call_target="InvertDiagBlocksLowerTriangular" | custom-call | tf_op jit(solution)/shard_map/triangular_solve/custom-call.0 | solution.py:17
  329.2 1.8 convolution_subtract_fusion.6
  331.0 11.7 %custom-call.34 = f32[128,128]{1,0:T(8,128)S(1)} custom-call(f32[128,128]{1,0:T(8,128)S(1)} %convolution_subtract_fusion.6), custom_call_target="Cholesky" | custom-call | tf_op jit(solution)/shard_map/cholesky/custom-call.1 | solution.py:39
  343.4 1.3 select_bitcast_fusion
  347.2 1.3 fusion.65
  350.1 1.7 fusion.41
  353.5 2.0 fusion.31
  357.2 2.8 fusion.20
  361.8 3.4 fusion.17
  365.2 1.2 fusion.23
  367.1 4.2 fusion.6
  371.3 9.8 %custom-call.35 = f32[1,128,128]{1,2,0:T(8,128)S(1)} custom-call(f32[1,128,128]{2,1,0:T(8,128)S(1)} %get-tuple-element.391), custom_call_target="InvertDiagBlocksLowerTriangular" | custom-call | tf_op jit(solution)/shard_map/triangular_solve/custom-call.0 | solution.py:17
  381.4 1.3 fusion.22
  383.5 1.5 constant_dynamic-slice_fusion
  385.1 6.6 %fusion.115 = f32[128,1024]{1,0:T(8,128)S(1)} fusion(f32[128,1024]{1,0:T(8,128)S(1)} %constant_dynamic-update-slice_fusion, f32[1024,1024]{1,0:T(8,128)} %constant_dynamic-update-slice_fusion.9), kind=kOutput, calls=%fused_computation.235 | convolution fusion | flops 1610612736 | bytes 5242880 | tf_op jit(solution)/shard_map/dot_general | solution.py:21
  391.7 2.4 fusion.116
  394.8 5.4 %fusion.14 = f32[2048,128]{1,0:T(8,128)S(1)} fusion(f32[2048,1152]{1,0:T(8,128)} %all-gather.6.cloned.1.call-done, f32[2048]{0:T(1024)S(1)} %convert_element_type.60, f32[128,1024]{1,0:T(8,128)S(1)} %fusion.116), kind=kOutput, calls=%fused_computation.19 | convolution fusion | flops 1610874880 | bytes 5513216 | tf_op jit(solution)/shard_map/dot_general | solution.py:21
  400.2 5.2 %fusion.11 = f32[2048,128]{1,0:T(8,128)S(1)} fusion(f32[2048,128]{1,0:T(8,128)S(1)} %fusion.14, f32[2048,1152]{1,0:T(8,128)} %all-gather.6.cloned.1.call-done, f32[2048]{0:T(1024)S(1)} %convert_element_type.59, f32[128,1024]{1,0:T(8,128)S(1)} %fusion.116), kind=kOutput, calls=%fused_computation.18 | convolution fusion | flops 1611137024 | bytes 6561792 | tf_op jit(solution)/shard_map/dot_general | solution.py:21
  405.4 5.5 %gather_fusion.7 = f32[2048,128]{1,0:T(8,128)S(1)} fusion(f32[2048,128]{1,0:T(8,128)S(1)} %fusion.11, s32[2048]{0:T(1024)S(1)} %fusion.112), kind=kCustom, calls=%fused_computation.7 | custom fusion | bytes 2105344 | tf_op jit(solution)/shard_map/gather | solution.py:126
  (105 shorter events, 33.7 us)
Async XLA Ops:
  7.2 4.1 copy-start
  7.2 84.2 %all-gather.4.cloned.1.call-start = ((), (), s32[]{:S(2)}) async-start(), calls=%async_computation | async-start | bytes 5013504 | tf_op jit(solution)/shard_map/all_gather | solution.py:78
  34.9 213.6 %all-gather.6.cloned.1.call-start = ((), (), s32[]{:S(2)}) async-start(), calls=%async_computation.1 | async-start | bytes 9584640 | tf_op jit(solution)/shard_map/all_gather | solution.py:89
  92.6 8.5 %copy-start.3 = (s32[2,32]{1,0:T(2,128)S(1)}, s32[2,32]{1,0:T(2,128)}, u32[]{:S(2)}) copy-start(s32[2,32]{1,0:T(2,128)} %param.69) | copy-start | bytes 772
  270.1 114.9 %collective-permute-start = (f32[32,1024]{1,0:T(8,128)S(1)}, f32[32,1024]{1,0:T(8,128)S(1)}, u32[]{:S(2)}, u32[]{:S(2)}) collective-permute-start(f32[32,1024]{1,0:T(8,128)S(1)} %select_multiply_fusion), channel_id=1, source_target_pairs={{0,1},{1,2},{2,3},{3,0},{4,5},{5,6},{6,7},{7,4},{8,9},{9,10},{10,1... | collective-permute-start | bytes 393224 | tf_op jit(solution)/shard_map/ppermute | solution.py:113
  271.3 113.8 %collective-permute-start.1 = (f32[32,1024]{1,0:T(8,128)S(1)}, f32[32,1024]{1,0:T(8,128)S(1)}, u32[]{:S(2)}, u32[]{:S(2)}) collective-permute-start(f32[32,1024]{1,0:T(8,128)S(1)} %select_multiply_fusion), channel_id=1, source_target_pairs={{0,2},{1,3},{2,0},{3,1},{4,6},{5,7},{6,4},{7,5},{8,10},{9,11},{10,... | collective-permute-start | bytes 393224 | tf_op jit(solution)/shard_map/ppermute | solution.py:113
  273.7 111.3 %collective-permute-start.2 = (f32[32,1024]{1,0:T(8,128)S(1)}, f32[32,1024]{1,0:T(8,128)S(1)}, u32[]{:S(2)}, u32[]{:S(2)}) collective-permute-start(f32[32,1024]{1,0:T(8,128)S(1)} %select_multiply_fusion), channel_id=1, source_target_pairs={{0,3},{1,0},{2,1},{3,2},{4,7},{5,4},{6,5},{7,6},{8,11},{9,8},{10,9... | collective-permute-start | bytes 393224 | tf_op jit(solution)/shard_map/ppermute | solution.py:113
  383.5 8.2 %copy-start.1 = (f32[1024,1024]{1,0:T(8,128)S(1)}, f32[1024,1024]{1,0:T(8,128)}, u32[]{:S(2)}) copy-start(f32[1024,1024]{1,0:T(8,128)} %constant_dynamic-update-slice_fusion.9) | copy-start | bytes 12582916
  405.4 5.5 %copy-start.2 = (f32[64,1,32,128]{3,2,1,0:T(8,128)S(1)}, f32[64,1,32,128]{3,2,1,0:T(8,128)}, u32[]{:S(2)}) copy-start(f32[64,1,32,128]{3,2,1,0:T(8,128)} %param.70) | copy-start | bytes 3145732
Sparse Core Ops, SparseCore 0:
  35.0 56.3 all-gather.3
  101.2 85.1 all-gather.5

commit v7 on v6

--- a/solution.py
+++ b/solution.py
@@ -120,8 +120,10 @@
     range_panel = contract_rows(masked_range, inverse)
     panel = lax.dynamic_slice_in_dim(range_panel, col_index * trail_rows, trail_rows, 0)
     range_back = matmul(range_panel, inverse)
-    first_part = contract_rows(gathered[:, :half_width], range_back[:, :half_width])
-    second_part = contract_rows(gathered[:, half_width:], range_back[:, half_width:])
+    first_part = lax.dot_general(gathered[:, :half_width], range_back[:, :half_width],
+                                 (((1,), (1,)), ((), ())), precision=lax.Precision.HIGH)
+    second_part = lax.dot_general(gathered[:, half_width:], range_back[:, half_width:],
+                                  (((1,), (1,)), ((), ())), precision=lax.Precision.HIGH)
     update_all = first_keep[:, None] * first_part + second_keep[:, None] * second_part
     update = update_all[trail_src]
     schur = trailing_block - update.reshape(trailing_block.shape)

time: 424 us -> 421 us (level)
    dot_general x17 -> x15, matrix products: 40.3 us -> 29.6 us  [contract_rows(): lax.dot_general(left_rows, right_rows, (((1,), (1,)), ((), ())), precisio...]
    dot_general x0 -> x2, matrix products: none -> 8.27 us  [the longest x1 4.23 us: local(): lax.dot_general(gathered[:, half_width:], range_back[:, half_width:], (((...]
  transfers between devices with their start and end apart: 5 -> 5, of which waited for: 1 -> 1; matrix products, arithmetic and copies ran while one was open for 62% -> 63% of each run, Pallas kernels for 0% -> 0%
where the time goes in v7:
time: 421 us; the launch traced here: 417 us
  other arithmetic  205 us (49%)
  matrix products  66.6 us (16%)
  waiting for transfers between devices  51.7 us (12%)
  local copies, waits for them, and re-layouts  51.2 us (12%)
  blocking collectives  22.1 us (5%)
  between operations  14.9 us (4%)
  starting transfers between devices  4.91 us (1%)
    another operation x24, other arithmetic, factor_and_inverse(): block = jnp.tril(lax.linalg.cholesky(column[:size], symmetrize_input=False))  99.5 us
    another operation x16, other arithmetic, lower_inverse(): lax.linalg.triangular_solve(lower_factor, identity, left_side=True, lower...  88.9 us
    all_gather x1, waiting for transfers between devices, local(): diag_pack = lax.all_gather(diag_pack, axis, axis=0, tiled=True)  51.6 us
    dot_general x15, matrix products, contract_rows(): lax.dot_general(left_rows, right_rows, (((1,), (1,)), ((), ())), precisio...  29.6 us
    dot_general x15, matrix products, matmul(): lax.dot_general(left, right, (((1,), (0,)), ((), ())), precision=highest)  26.4 us
    all_gather x1, blocking collectives, local(): diag_pack = lax.all_gather(diag_pack, axis, axis=0, tiled=True)  22.1 us
  transfers between devices with their start and end apart: 5, of which 1 were waited for; matrix products, arithmetic and copies ran while one was open for 63% of the time, Pallas kernels for 0%

profile of v7, /device:TPU:1, one launch (start us, length us, event | category | flops | bytes accessed | tf_op | source)
XLA Modules:
  0.0 416.8 jit_solution(17964909072754300134)
XLA Ops:
  7.9 2.0 sort.47
  10.0 1.3 gather_fusion.3
  11.9 22.1 %all-gather = f32[16,4,1152]{2,1,0:T(4,128)S(1)} all-gather(f32[1,4,1152]{2,1,0:T(4,128)S(1)} %maximum_bitcast_fusion), channel_id=1, replica_groups=mesh['y'=4,'z'=8,'core'=2,'col'=4] {'z','core'}, dimensions={0}, use_global_device_ids=true | all-gather | bytes 313344 | tf_op jit(solution)/shard_map/all_gather | solution.py:78
  34.9 2.0 sort.46
  37.6 1.4 gather_fusion.1
  39.7 51.6 %all-gather.4.cloned.1.call-done = f32[1024,1152]{1,0:T(8,128)} async-done(((f32[64,1152]{1,0:T(8,128)}), f32[1024,1152]{1,0:T(8,128)}) %all-gather.4.cloned.1.call-update) | async-done | bytes 4718608 | tf_op jit(solution)/shard_map/all_gather | solution.py:78
  91.3 1.3 fusion.43
  92.6 8.4 %scatter_custom_fusion = f32[1024,1024]{1,0:T(8,128)} fusion(s32[1024]{0:T(1024)S(1)} %fusion.43, f32[1024,1152]{1,0:T(8,128)} %all-gather.4.cloned.1.call-done, f32[]{:T(128)} %constant.853.clone.1), kind=kCustom, calls=%fused_computation.13 | custom fusion | bytes 8389120 | tf_op jit(solution)/shard_map/scatter | solution.py:80
  101.1 5.9 %copy.47 = f32[1024,1024]{0,1:T(8,128)} copy(f32[1024,1024]{1,0:T(8,128)} %scatter_custom_fusion) | data formatting | bytes 8388608 | tf_op jit(solution)/shard_map/optimization_barrier | solution.py:88
  107.9 1.3 fusion.45
  109.2 11.7 %custom-call.20 = f32[128,128]{1,0:T(8,128)S(1)} custom-call(f32[128,128]{1,0:T(8,128)S(1)} %slice.948), custom_call_target="Cholesky" | custom-call | tf_op jit(solution)/shard_map/cholesky/custom-call.1 | solution.py:39
  122.3 9.8 %custom-call.21 = f32[1,128,128]{1,2,0:T(8,128)S(1)} custom-call(f32[1,128,128]{2,1,0:T(8,128)S(1)} %get-tuple-element.389), custom_call_target="InvertDiagBlocksLowerTriangular" | custom-call | tf_op jit(solution)/shard_map/triangular_solve/custom-call.0 | solution.py:17
  132.1 2.5 scatter.109
  134.9 2.5 scatter.125
  137.4 1.3 constant_dynamic-update-slice_fusion.4
  138.7 1.7 convolution_subtract_fusion
  140.4 11.7 %custom-call.22 = f32[128,128]{1,0:T(8,128)S(1)} custom-call(f32[128,128]{1,0:T(8,128)S(1)} %slice.952), custom_call_target="Cholesky" | custom-call | tf_op jit(solution)/shard_map/cholesky/custom-call.1 | solution.py:39
  152.8 1.3 select_bitcast_fusion.6
  154.1 10.0 %custom-call.23 = f32[1,128,128]{1,2,0:T(8,128)S(1)} custom-call(f32[1,128,128]{2,1,0:T(8,128)S(1)} %get-tuple-element.403), custom_call_target="InvertDiagBlocksLowerTriangular" | custom-call | tf_op jit(solution)/shard_map/triangular_solve/custom-call.0 | solution.py:17
  164.4 1.3 convolution_dynamic-update-slice_fusion
  165.6 2.5 convolution_subtract_fusion.1
  168.1 11.7 %custom-call.24 = f32[128,128]{1,0:T(8,128)S(1)} custom-call(f32[128,128]{1,0:T(8,128)S(1)} %slice.957), custom_call_target="Cholesky" | custom-call | tf_op jit(solution)/shard_map/cholesky/custom-call.1 | solution.py:39
  180.5 1.3 select_bitcast_fusion.5
  181.8 9.8 %custom-call.25 = f32[1,128,128]{1,2,0:T(8,128)S(1)} custom-call(f32[1,128,128]{2,1,0:T(8,128)S(1)} %get-tuple-element.401), custom_call_target="InvertDiagBlocksLowerTriangular" | custom-call | tf_op jit(solution)/shard_map/triangular_solve/custom-call.0 | solution.py:17
  191.9 1.2 convolution_dynamic-update-slice_fusion.1
  193.1 2.4 convolution_subtract_fusion.2
  195.6 12.1 %custom-call.26 = f32[128,128]{1,0:T(8,128)S(1)} custom-call(f32[128,128]{1,0:T(8,128)S(1)} %slice.962), custom_call_target="Cholesky" | custom-call | tf_op jit(solution)/shard_map/cholesky/custom-call.1 | solution.py:39
  208.4 1.3 select_bitcast_fusion.4
  209.7 9.8 %custom-call.27 = f32[1,128,128]{1,2,0:T(8,128)S(1)} custom-call(f32[1,128,128]{2,1,0:T(8,128)S(1)} %get-tuple-element.399), custom_call_target="InvertDiagBlocksLowerTriangular" | custom-call | tf_op jit(solution)/shard_map/triangular_solve/custom-call.0 | solution.py:17
  220.9 2.4 convolution_subtract_fusion.3
  223.3 11.7 %custom-call.28 = f32[128,128]{1,0:T(8,128)S(1)} custom-call(f32[128,128]{1,0:T(8,128)S(1)} %slice.967), custom_call_target="Cholesky" | custom-call | tf_op jit(solution)/shard_map/cholesky/custom-call.1 | solution.py:39
  235.7 1.3 select_bitcast_fusion.3
  237.0 9.9 %custom-call.29 = f32[1,128,128]{1,2,0:T(8,128)S(1)} custom-call(f32[1,128,128]{2,1,0:T(8,128)S(1)} %get-tuple-element.397), custom_call_target="InvertDiagBlocksLowerTriangular" | custom-call | tf_op jit(solution)/shard_map/triangular_solve/custom-call.0 | solution.py:17
  248.4 2.4 fusion.30
  250.9 5.0 %sort.48 = (s32[2048]{0:T(1024)}, s32[2048]{0:T(1024)S(1)}) sort(s32[2048]{0:T(1024)S(1)} %fusion.111, s32[2048]{0:T(1024)S(1)} %iota.307), dimensions={0}, to_apply=%region_5.8 | sort | flops 22528 | bytes 32768 | tf_op jit(solution)/shard_map/sort | solution.py:94
  257.6 8.4 %slice.969 = f32[2048,1024]{1,0:T(8,128)} slice(f32[2048,1152]{1,0:T(8,128)} %all-gather.6.cloned.1.call-done), slice={[0:2048], [0:1024]} | slice | bytes 16777216 | tf_op jit(solution)/shard_map/slice | solution.py:91
  265.9 4.1 gather_fusion.4
  271.3 2.5 collective-permute-start.1
  274.9 2.3 convolution_subtract_fusion.4
  277.3 11.7 %custom-call.30 = f32[128,128]{1,0:T(8,128)S(1)} custom-call(f32[128,128]{1,0:T(8,128)S(1)} %slice.973), custom_call_target="Cholesky" | custom-call | tf_op jit(solution)/shard_map/cholesky/custom-call.1 | solution.py:39
  289.7 1.3 select_bitcast_fusion.2
  290.9 9.8 %custom-call.31 = f32[1,128,128]{1,2,0:T(8,128)S(1)} custom-call(f32[1,128,128]{2,1,0:T(8,128)S(1)} %get-tuple-element.395), custom_call_target="InvertDiagBlocksLowerTriangular" | custom-call | tf_op jit(solution)/shard_map/triangular_solve/custom-call.0 | solution.py:17
  302.0 2.1 convolution_subtract_fusion.5
  304.1 11.7 %custom-call.32 = f32[128,128]{1,0:T(8,128)S(1)} custom-call(f32[128,128]{1,0:T(8,128)S(1)} %slice.978), custom_call_target="Cholesky" | custom-call | tf_op jit(solution)/shard_map/cholesky/custom-call.1 | solution.py:39
  316.5 1.3 select_bitcast_fusion.1
  317.8 10.2 %custom-call.33 = f32[1,128,128]{1,2,0:T(8,128)S(1)} custom-call(f32[1,128,128]{2,1,0:T(8,128)S(1)} %get-tuple-element.393), custom_call_target="InvertDiagBlocksLowerTriangular" | custom-call | tf_op jit(solution)/shard_map/triangular_solve/custom-call.0 | solution.py:17
  329.2 1.8 convolution_subtract_fusion.6
  331.0 11.7 %custom-call.34 = f32[128,128]{1,0:T(8,128)S(1)} custom-call(f32[128,128]{1,0:T(8,128)S(1)} %convolution_subtract_fusion.6), custom_call_target="Cholesky" | custom-call | tf_op jit(solution)/shard_map/cholesky/custom-call.1 | solution.py:39
  343.4 1.3 select_bitcast_fusion
  347.2 1.3 fusion.65
  350.1 1.7 fusion.41
  353.5 2.0 fusion.31
  357.2 2.8 fusion.20
  361.8 3.4 fusion.17
  365.2 1.2 fusion.23
  367.1 4.2 %fusion.6 = f32[128,896]{1,0:T(8,128)S(1)} fusion(f32[1024,1024]{1,0:T(8,128)} %constant_dynamic-update-slice_fusion.5, f32[1024,1024]{1,0:T(8,128)} %get-tuple-element.392), kind=kOutput, calls=%fused_computation.15 | convolution fusion | flops 1233125376 | bytes 4128768 | tf_op jit(solution)/shard_map/dot_general | solution.py:25
  371.3 9.8 %custom-call.35 = f32[1,128,128]{1,2,0:T(8,128)S(1)} custom-call(f32[1,128,128]{2,1,0:T(8,128)S(1)} %get-tuple-element.391), custom_call_target="InvertDiagBlocksLowerTriangular" | custom-call | tf_op jit(solution)/shard_map/triangular_solve/custom-call.0 | solution.py:17
  381.4 1.3 fusion.22
  383.5 1.5 constant_dynamic-slice_fusion
  385.1 6.6 %fusion.115 = f32[128,1024]{1,0:T(8,128)S(1)} fusion(f32[128,1024]{1,0:T(8,128)S(1)} %constant_dynamic-update-slice_fusion, f32[1024,1024]{1,0:T(8,128)} %constant_dynamic-update-slice_fusion.9), kind=kOutput, calls=%fused_computation.235 | convolution fusion | flops 1610612736 | bytes 5242880 | tf_op jit(solution)/shard_map/dot_general | solution.py:21
  391.7 2.4 fusion.116
  394.8 4.2 %fusion.14 = f32[2048,128]{1,0:T(8,128)S(1)} fusion(f32[2048,1152]{1,0:T(8,128)} %all-gather.6.cloned.1.call-done, f32[2048]{0:T(1024)S(1)} %convert_element_type.60, f32[128,1024]{1,0:T(8,128)S(1)} %fusion.116), kind=kOutput, calls=%fused_computation.19 | convolution fusion | flops 805568512 | bytes 5513216 | tf_op jit(solution)/shard_map/dot_general | solution.py:125
  399.0 4.0 fusion.11
  403.1 5.5 %gather_fusion.7 = f32[2048,128]{1,0:T(8,128)S(1)} fusion(f32[2048,128]{1,0:T(8,128)S(1)} %fusion.11, s32[2048]{0:T(1024)S(1)} %fusion.112), kind=kCustom, calls=%fused_computation.7 | custom fusion | bytes 2105344 | tf_op jit(solution)/shard_map/gather | solution.py:128
  (105 shorter events, 33.7 us)
Async XLA Ops:
  7.2 4.1 copy-start
  7.2 84.2 %all-gather.4.cloned.1.call-start = ((), (), s32[]{:S(2)}) async-start(), calls=%async_computation | async-start | bytes 5013504 | tf_op jit(solution)/shard_map/all_gather | solution.py:78
  34.9 213.6 %all-gather.6.cloned.1.call-start = ((), (), s32[]{:S(2)}) async-start(), calls=%async_computation.1 | async-start | bytes 9584640 | tf_op jit(solution)/shard_map/all_gather | solution.py:89
  92.6 8.5 %copy-start.3 = (s32[2,32]{1,0:T(2,128)S(1)}, s32[2,32]{1,0:T(2,128)}, u32[]{:S(2)}) copy-start(s32[2,32]{1,0:T(2,128)} %param.69) | copy-start | bytes 772
  270.1 114.9 %collective-permute-start = (f32[32,1024]{1,0:T(8,128)S(1)}, f32[32,1024]{1,0:T(8,128)S(1)}, u32[]{:S(2)}, u32[]{:S(2)}) collective-permute-start(f32[32,1024]{1,0:T(8,128)S(1)} %select_multiply_fusion), channel_id=1, source_target_pairs={{0,1},{1,2},{2,3},{3,0},{4,5},{5,6},{6,7},{7,4},{8,9},{9,10},{10,1... | collective-permute-start | bytes 393224 | tf_op jit(solution)/shard_map/ppermute | solution.py:113
  271.3 113.8 %collective-permute-start.1 = (f32[32,1024]{1,0:T(8,128)S(1)}, f32[32,1024]{1,0:T(8,128)S(1)}, u32[]{:S(2)}, u32[]{:S(2)}) collective-permute-start(f32[32,1024]{1,0:T(8,128)S(1)} %select_multiply_fusion), channel_id=1, source_target_pairs={{0,2},{1,3},{2,0},{3,1},{4,6},{5,7},{6,4},{7,5},{8,10},{9,11},{10,... | collective-permute-start | bytes 393224 | tf_op jit(solution)/shard_map/ppermute | solution.py:113
  273.7 111.3 %collective-permute-start.2 = (f32[32,1024]{1,0:T(8,128)S(1)}, f32[32,1024]{1,0:T(8,128)S(1)}, u32[]{:S(2)}, u32[]{:S(2)}) collective-permute-start(f32[32,1024]{1,0:T(8,128)S(1)} %select_multiply_fusion), channel_id=1, source_target_pairs={{0,3},{1,0},{2,1},{3,2},{4,7},{5,4},{6,5},{7,6},{8,11},{9,8},{10,9... | collective-permute-start | bytes 393224 | tf_op jit(solution)/shard_map/ppermute | solution.py:113
  383.5 8.2 %copy-start.1 = (f32[1024,1024]{1,0:T(8,128)S(1)}, f32[1024,1024]{1,0:T(8,128)}, u32[]{:S(2)}) copy-start(f32[1024,1024]{1,0:T(8,128)} %constant_dynamic-update-slice_fusion.9) | copy-start | bytes 12582916
  403.0 5.5 %copy-start.2 = (f32[64,1,32,128]{3,2,1,0:T(8,128)S(1)}, f32[64,1,32,128]{3,2,1,0:T(8,128)}, u32[]{:S(2)}) copy-start(f32[64,1,32,128]{3,2,1,0:T(8,128)} %param.70) | copy-start | bytes 3145732
Sparse Core Ops, SparseCore 0:
  35.0 56.3 all-gather.3
  101.2 85.1 all-gather.5

commit v8 on v7

--- a/solution.py
+++ b/solution.py
@@ -119,7 +119,7 @@
     masked_range, first_keep, second_keep, trail_src = tied
     range_panel = contract_rows(masked_range, inverse)
     panel = lax.dynamic_slice_in_dim(range_panel, col_index * trail_rows, trail_rows, 0)
-    range_back = matmul(range_panel, inverse)
+    range_back = lax.dot_general(range_panel, inverse, (((1,), (0,)), ((), ())), precision=lax.Precision.HIGH)
     first_part = lax.dot_general(gathered[:, :half_width], range_back[:, :half_width],
                                  (((1,), (1,)), ((), ())), precision=lax.Precision.HIGH)
     second_part = lax.dot_general(gathered[:, half_width:], range_back[:, half_width:],

time: 421 us -> 421 us (level)
    dot_general x15 -> x14, matrix products: 26.4 us -> 24 us  [matmul(): lax.dot_general(left, right, (((1,), (0,)), ((), ())), precision=highest)]
where the time goes in v8:
time: 421 us; the launch traced here: 416 us
  other arithmetic  205 us (49%)
  matrix products  65.9 us (16%)
  waiting for transfers between devices  51.7 us (12%)
  local copies, waits for them, and re-layouts  51.2 us (12%)
  blocking collectives  22.1 us (5%)
  between operations  14.9 us (4%)
  starting transfers between devices  4.91 us (1%)
    another operation x24, other arithmetic, factor_and_inverse(): block = jnp.tril(lax.linalg.cholesky(column[:size], symmetrize_input=False))  99.5 us
    another operation x16, other arithmetic, lower_inverse(): lax.linalg.triangular_solve(lower_factor, identity, left_side=True, lower...  88.9 us
    all_gather x1, waiting for transfers between devices, local(): diag_pack = lax.all_gather(diag_pack, axis, axis=0, tiled=True)  51.6 us
    dot_general x15, matrix products, contract_rows(): lax.dot_general(left_rows, right_rows, (((1,), (1,)), ((), ())), precisio...  29.6 us
    dot_general x14, matrix products, matmul(): lax.dot_general(left, right, (((1,), (0,)), ((), ())), precision=highest)  24 us
    all_gather x1, blocking collectives, local(): diag_pack = lax.all_gather(diag_pack, axis, axis=0, tiled=True)  22.1 us
  transfers between devices with their start and end apart: 5, of which 1 were waited for; matrix products, arithmetic and copies ran while one was open for 63% of the time, Pallas kernels for 0%

profile of v8, /device:TPU:1, one launch (start us, length us, event | category | flops | bytes accessed | tf_op | source)
XLA Modules:
  0.0 416.0 jit_solution(18146462031352234577)
XLA Ops:
  7.9 2.0 sort.47
  10.0 1.3 gather_fusion.3
  11.9 22.1 %all-gather = f32[16,4,1152]{2,1,0:T(4,128)S(1)} all-gather(f32[1,4,1152]{2,1,0:T(4,128)S(1)} %maximum_bitcast_fusion), channel_id=1, replica_groups=mesh['y'=4,'z'=8,'core'=2,'col'=4] {'z','core'}, dimensions={0}, use_global_device_ids=true | all-gather | bytes 313344 | tf_op jit(solution)/shard_map/all_gather | solution.py:78
  34.9 2.0 sort.46
  37.6 1.4 gather_fusion.1
  39.7 51.6 %all-gather.4.cloned.1.call-done = f32[1024,1152]{1,0:T(8,128)} async-done(((f32[64,1152]{1,0:T(8,128)}), f32[1024,1152]{1,0:T(8,128)}) %all-gather.4.cloned.1.call-update) | async-done | bytes 4718608 | tf_op jit(solution)/shard_map/all_gather | solution.py:78
  91.3 1.3 fusion.43
  92.6 8.4 %scatter_custom_fusion = f32[1024,1024]{1,0:T(8,128)} fusion(s32[1024]{0:T(1024)S(1)} %fusion.43, f32[1024,1152]{1,0:T(8,128)} %all-gather.4.cloned.1.call-done, f32[]{:T(128)} %constant.853.clone.1), kind=kCustom, calls=%fused_computation.13 | custom fusion | bytes 8389120 | tf_op jit(solution)/shard_map/scatter | solution.py:80
  101.1 5.9 %copy.47 = f32[1024,1024]{0,1:T(8,128)} copy(f32[1024,1024]{1,0:T(8,128)} %scatter_custom_fusion) | data formatting | bytes 8388608 | tf_op jit(solution)/shard_map/optimization_barrier | solution.py:88
  107.9 1.3 fusion.45
  109.2 11.7 %custom-call.20 = f32[128,128]{1,0:T(8,128)S(1)} custom-call(f32[128,128]{1,0:T(8,128)S(1)} %slice.948), custom_call_target="Cholesky" | custom-call | tf_op jit(solution)/shard_map/cholesky/custom-call.1 | solution.py:39
  122.3 9.8 %custom-call.21 = f32[1,128,128]{1,2,0:T(8,128)S(1)} custom-call(f32[1,128,128]{2,1,0:T(8,128)S(1)} %get-tuple-element.389), custom_call_target="InvertDiagBlocksLowerTriangular" | custom-call | tf_op jit(solution)/shard_map/triangular_solve/custom-call.0 | solution.py:17
  132.1 2.5 scatter.109
  134.9 2.5 scatter.125
  137.4 1.3 constant_dynamic-update-slice_fusion.4
  138.7 1.7 convolution_subtract_fusion
  140.4 11.7 %custom-call.22 = f32[128,128]{1,0:T(8,128)S(1)} custom-call(f32[128,128]{1,0:T(8,128)S(1)} %slice.952), custom_call_target="Cholesky" | custom-call | tf_op jit(solution)/shard_map/cholesky/custom-call.1 | solution.py:39
  152.8 1.3 select_bitcast_fusion.6
  154.1 10.0 %custom-call.23 = f32[1,128,128]{1,2,0:T(8,128)S(1)} custom-call(f32[1,128,128]{2,1,0:T(8,128)S(1)} %get-tuple-element.403), custom_call_target="InvertDiagBlocksLowerTriangular" | custom-call | tf_op jit(solution)/shard_map/triangular_solve/custom-call.0 | solution.py:17
  164.4 1.3 convolution_dynamic-update-slice_fusion
  165.6 2.5 convolution_subtract_fusion.1
  168.1 11.7 %custom-call.24 = f32[128,128]{1,0:T(8,128)S(1)} custom-call(f32[128,128]{1,0:T(8,128)S(1)} %slice.957), custom_call_target="Cholesky" | custom-call | tf_op jit(solution)/shard_map/cholesky/custom-call.1 | solution.py:39
  180.5 1.3 select_bitcast_fusion.5
  181.8 9.8 %custom-call.25 = f32[1,128,128]{1,2,0:T(8,128)S(1)} custom-call(f32[1,128,128]{2,1,0:T(8,128)S(1)} %get-tuple-element.401), custom_call_target="InvertDiagBlocksLowerTriangular" | custom-call | tf_op jit(solution)/shard_map/triangular_solve/custom-call.0 | solution.py:17
  191.9 1.2 convolution_dynamic-update-slice_fusion.1
  193.1 2.4 convolution_subtract_fusion.2
  195.6 12.1 %custom-call.26 = f32[128,128]{1,0:T(8,128)S(1)} custom-call(f32[128,128]{1,0:T(8,128)S(1)} %slice.962), custom_call_target="Cholesky" | custom-call | tf_op jit(solution)/shard_map/cholesky/custom-call.1 | solution.py:39
  208.4 1.3 select_bitcast_fusion.4
  209.7 9.8 %custom-call.27 = f32[1,128,128]{1,2,0:T(8,128)S(1)} custom-call(f32[1,128,128]{2,1,0:T(8,128)S(1)} %get-tuple-element.399), custom_call_target="InvertDiagBlocksLowerTriangular" | custom-call | tf_op jit(solution)/shard_map/triangular_solve/custom-call.0 | solution.py:17
  220.9 2.4 convolution_subtract_fusion.3
  223.3 11.7 %custom-call.28 = f32[128,128]{1,0:T(8,128)S(1)} custom-call(f32[128,128]{1,0:T(8,128)S(1)} %slice.967), custom_call_target="Cholesky" | custom-call | tf_op jit(solution)/shard_map/cholesky/custom-call.1 | solution.py:39
  235.7 1.3 select_bitcast_fusion.3
  237.0 9.9 %custom-call.29 = f32[1,128,128]{1,2,0:T(8,128)S(1)} custom-call(f32[1,128,128]{2,1,0:T(8,128)S(1)} %get-tuple-element.397), custom_call_target="InvertDiagBlocksLowerTriangular" | custom-call | tf_op jit(solution)/shard_map/triangular_solve/custom-call.0 | solution.py:17
  248.4 2.4 fusion.30
  250.9 5.0 %sort.48 = (s32[2048]{0:T(1024)}, s32[2048]{0:T(1024)S(1)}) sort(s32[2048]{0:T(1024)S(1)} %fusion.111, s32[2048]{0:T(1024)S(1)} %iota.307), dimensions={0}, to_apply=%region_5.8 | sort | flops 22528 | bytes 32768 | tf_op jit(solution)/shard_map/sort | solution.py:94
  257.6 8.4 %slice.969 = f32[2048,1024]{1,0:T(8,128)} slice(f32[2048,1152]{1,0:T(8,128)} %all-gather.6.cloned.1.call-done), slice={[0:2048], [0:1024]} | slice | bytes 16777216 | tf_op jit(solution)/shard_map/slice | solution.py:91
  265.9 4.1 gather_fusion.4
  271.3 2.5 collective-permute-start.1
  274.9 2.3 convolution_subtract_fusion.4
  277.3 11.7 %custom-call.30 = f32[128,128]{1,0:T(8,128)S(1)} custom-call(f32[128,128]{1,0:T(8,128)S(1)} %slice.973), custom_call_target="Cholesky" | custom-call | tf_op jit(solution)/shard_map/cholesky/custom-call.1 | solution.py:39
  289.7 1.3 select_bitcast_fusion.2
  290.9 9.8 %custom-call.31 = f32[1,128,128]{1,2,0:T(8,128)S(1)} custom-call(f32[1,128,128]{2,1,0:T(8,128)S(1)} %get-tuple-element.395), custom_call_target="InvertDiagBlocksLowerTriangular" | custom-call | tf_op jit(solution)/shard_map/triangular_solve/custom-call.0 | solution.py:17
  302.0 2.1 convolution_subtract_fusion.5
  304.1 11.7 %custom-call.32 = f32[128,128]{1,0:T(8,128)S(1)} custom-call(f32[128,128]{1,0:T(8,128)S(1)} %slice.978), custom_call_target="Cholesky" | custom-call | tf_op jit(solution)/shard_map/cholesky/custom-call.1 | solution.py:39
  316.5 1.3 select_bitcast_fusion.1
  317.8 10.2 %custom-call.33 = f32[1,128,128]{1,2,0:T(8,128)S(1)} custom-call(f32[1,128,128]{2,1,0:T(8,128)S(1)} %get-tuple-element.393), custom_call_target="InvertDiagBlocksLowerTriangular" | custom-call | tf_op jit(solution)/shard_map/triangular_solve/custom-call.0 | solution.py:17
  329.2 1.8 convolution_subtract_fusion.6
  331.0 11.7 %custom-call.34 = f32[128,128]{1,0:T(8,128)S(1)} custom-call(f32[128,128]{1,0:T(8,128)S(1)} %convolution_subtract_fusion.6), custom_call_target="Cholesky" | custom-call | tf_op jit(solution)/shard_map/cholesky/custom-call.1 | solution.py:39
  343.4 1.3 select_bitcast_fusion
  347.2 1.3 fusion.65
  350.1 1.7 fusion.41
  353.5 2.0 fusion.31
  357.2 2.8 fusion.20
  361.8 3.4 fusion.17
  365.2 1.2 fusion.23
  367.1 4.2 %fusion.6 = f32[128,896]{1,0:T(8,128)S(1)} fusion(f32[1024,1024]{1,0:T(8,128)} %constant_dynamic-update-slice_fusion.5, f32[1024,1024]{1,0:T(8,128)} %get-tuple-element.392), kind=kOutput, calls=%fused_computation.15 | convolution fusion | flops 1233125376 | bytes 4128768 | tf_op jit(solution)/shard_map/dot_general | solution.py:25
  371.3 9.8 %custom-call.35 = f32[1,128,128]{1,2,0:T(8,128)S(1)} custom-call(f32[1,128,128]{2,1,0:T(8,128)S(1)} %get-tuple-element.391), custom_call_target="InvertDiagBlocksLowerTriangular" | custom-call | tf_op jit(solution)/shard_map/triangular_solve/custom-call.0 | solution.py:17
  381.4 1.3 fusion.22
  383.5 1.5 constant_dynamic-slice_fusion
  385.1 6.6 %fusion.115 = f32[128,1024]{1,0:T(8,128)S(1)} fusion(f32[128,1024]{1,0:T(8,128)S(1)} %constant_dynamic-update-slice_fusion, f32[1024,1024]{1,0:T(8,128)} %constant_dynamic-update-slice_fusion.9), kind=kOutput, calls=%fused_computation.235 | convolution fusion | flops 1610612736 | bytes 5242880 | tf_op jit(solution)/shard_map/dot_general | solution.py:21
  391.7 1.6 fusion.116
  394.0 4.2 %fusion.14 = f32[2048,128]{1,0:T(8,128)S(1)} fusion(f32[2048,1152]{1,0:T(8,128)} %all-gather.6.cloned.1.call-done, f32[2048]{0:T(1024)S(1)} %convert_element_type.60, f32[128,1024]{1,0:T(8,128)S(1)} %fusion.116), kind=kOutput, calls=%fused_computation.19 | convolution fusion | flops 805568512 | bytes 5513216 | tf_op jit(solution)/shard_map/dot_general | solution.py:125
  398.2 4.0 fusion.11
  402.3 5.5 %gather_fusion.7 = f32[2048,128]{1,0:T(8,128)S(1)} fusion(f32[2048,128]{1,0:T(8,128)S(1)} %fusion.11, s32[2048]{0:T(1024)S(1)} %fusion.112), kind=kCustom, calls=%fused_computation.7 | custom fusion | bytes 2105344 | tf_op jit(solution)/shard_map/gather | solution.py:128
  (105 shorter events, 33.7 us)
Async XLA Ops:
  7.2 4.1 copy-start
  7.2 84.2 %all-gather.4.cloned.1.call-start = ((), (), s32[]{:S(2)}) async-start(), calls=%async_computation | async-start | bytes 5013504 | tf_op jit(solution)/shard_map/all_gather | solution.py:78
  34.9 213.6 %all-gather.6.cloned.1.call-start = ((), (), s32[]{:S(2)}) async-start(), calls=%async_computation.1 | async-start | bytes 9584640 | tf_op jit(solution)/shard_map/all_gather | solution.py:89
  92.6 8.5 %copy-start.3 = (s32[2,32]{1,0:T(2,128)S(1)}, s32[2,32]{1,0:T(2,128)}, u32[]{:S(2)}) copy-start(s32[2,32]{1,0:T(2,128)} %param.69) | copy-start | bytes 772
  270.1 114.9 %collective-permute-start = (f32[32,1024]{1,0:T(8,128)S(1)}, f32[32,1024]{1,0:T(8,128)S(1)}, u32[]{:S(2)}, u32[]{:S(2)}) collective-permute-start(f32[32,1024]{1,0:T(8,128)S(1)} %select_multiply_fusion), channel_id=1, source_target_pairs={{0,1},{1,2},{2,3},{3,0},{4,5},{5,6},{6,7},{7,4},{8,9},{9,10},{10,1... | collective-permute-start | bytes 393224 | tf_op jit(solution)/shard_map/ppermute | solution.py:113
  271.3 113.8 %collective-permute-start.1 = (f32[32,1024]{1,0:T(8,128)S(1)}, f32[32,1024]{1,0:T(8,128)S(1)}, u32[]{:S(2)}, u32[]{:S(2)}) collective-permute-start(f32[32,1024]{1,0:T(8,128)S(1)} %select_multiply_fusion), channel_id=1, source_target_pairs={{0,2},{1,3},{2,0},{3,1},{4,6},{5,7},{6,4},{7,5},{8,10},{9,11},{10,... | collective-permute-start | bytes 393224 | tf_op jit(solution)/shard_map/ppermute | solution.py:113
  273.7 111.3 %collective-permute-start.2 = (f32[32,1024]{1,0:T(8,128)S(1)}, f32[32,1024]{1,0:T(8,128)S(1)}, u32[]{:S(2)}, u32[]{:S(2)}) collective-permute-start(f32[32,1024]{1,0:T(8,128)S(1)} %select_multiply_fusion), channel_id=1, source_target_pairs={{0,3},{1,0},{2,1},{3,2},{4,7},{5,4},{6,5},{7,6},{8,11},{9,8},{10,9... | collective-permute-start | bytes 393224 | tf_op jit(solution)/shard_map/ppermute | solution.py:113
  383.5 8.2 %copy-start.1 = (f32[1024,1024]{1,0:T(8,128)S(1)}, f32[1024,1024]{1,0:T(8,128)}, u32[]{:S(2)}) copy-start(f32[1024,1024]{1,0:T(8,128)} %constant_dynamic-update-slice_fusion.9) | copy-start | bytes 12582916
  402.3 5.5 %copy-start.2 = (f32[64,1,32,128]{3,2,1,0:T(8,128)S(1)}, f32[64,1,32,128]{3,2,1,0:T(8,128)}, u32[]{:S(2)}) copy-start(f32[64,1,32,128]{3,2,1,0:T(8,128)} %param.70) | copy-start | bytes 3145732
Sparse Core Ops, SparseCore 0:
  35.0 56.3 all-gather.3
  101.2 85.1 all-gather.5

commit v9 on v8

--- a/solution.py
+++ b/solution.py
@@ -33,14 +33,18 @@
     diag_inverses = []
     for k in range(count):
         start = k * size
-        column = (gathered[start:, start:start + size] + gathered[start:start + size, start:].T) * 0.5
+        end = start + size
+        top = (gathered[start:end, start:end] + gathered[start:end, start:end].T) * 0.5
         if k > 0:
-            column = column - contract_rows(factor[start:, :start], factor[start:start + size, :start])
-        block = jnp.tril(lax.linalg.cholesky(column[:size], symmetrize_input=False))
+            top = top - contract_rows(factor[start:end, :start], factor[start:end, :start])
+        block = jnp.tril(lax.linalg.cholesky(top, symmetrize_input=False))
         block_inverse = jnp.tril(lower_inverse(block))
-        factor = factor.at[start:start + size, start:start + size].set(block)
+        factor = factor.at[start:end, start:end].set(block)
         if k < count - 1:
-            factor = factor.at[start + size:, start:start + size].set(contract_rows(column[size:], block_inverse))
+            below = (gathered[end:, start:end] + gathered[start:end, end:].T) * 0.5
+            if k > 0:
+                below = below - contract_rows(factor[end:, :start], factor[start:end, :start])
+            factor = factor.at[end:, start:end].set(contract_rows(below, block_inverse))
         diag_inverses.append(block_inverse)
         if k == count // 2:
             factor, tied = lax.optimization_barrier((factor, tied))

time: 421 us -> 430 us (1.021)
  matrix products: 65.9 us -> 74.3 us
    dot_general x15 -> x21, matrix products: 29.6 us -> 37.8 us  [contract_rows(): lax.dot_general(left_rows, right_rows, (((1,), (1,)), ((), ())), precisio...]
  transfers between devices with their start and end apart: 5 -> 5, of which waited for: 1 -> 1; matrix products, arithmetic and copies ran while one was open for 63% -> 64% of each run, Pallas kernels for 0% -> 0%
where the time goes in v9:
time: 430 us; the launch traced here: 425 us
  other arithmetic  205 us (48%)
  matrix products  74.3 us (17%)
  local copies, waits for them, and re-layouts  52 us (12%)
  waiting for transfers between devices  51.7 us (12%)
  blocking collectives  22.1 us (5%)
  between operations  14.9 us (3%)
  starting transfers between devices  5.03 us (1%)
    another operation x24, other arithmetic, factor_and_inverse(): block = jnp.tril(lax.linalg.cholesky(top, symmetrize_input=False))  99.3 us
    another operation x16, other arithmetic, lower_inverse(): lax.linalg.triangular_solve(lower_factor, identity, left_side=True, lower...  88.9 us
    all_gather x1, waiting for transfers between devices, local(): diag_pack = lax.all_gather(diag_pack, axis, axis=0, tiled=True)  51.6 us
    dot_general x21, matrix products, contract_rows(): lax.dot_general(left_rows, right_rows, (((1,), (1,)), ((), ())), precisio...  37.8 us
    dot_general x14, matrix products, matmul(): lax.dot_general(left, right, (((1,), (0,)), ((), ())), precision=highest)  24.3 us
    all_gather x1, blocking collectives, local(): diag_pack = lax.all_gather(diag_pack, axis, axis=0, tiled=True)  22.1 us
  transfers between devices with their start and end apart: 5, of which 1 were waited for; matrix products, arithmetic and copies ran while one was open for 64% of the time, Pallas kernels for 0%

profile of v9, /device:TPU:1, one launch (start us, length us, event | category | flops | bytes accessed | tf_op | source)
XLA Modules:
  0.0 424.8 jit_solution(13147684697021274179)
XLA Ops:
  7.9 2.0 sort.47
  10.0 1.3 gather_fusion.3
  11.9 22.1 %all-gather = f32[16,4,1152]{2,1,0:T(4,128)S(1)} all-gather(f32[1,4,1152]{2,1,0:T(4,128)S(1)} %maximum_bitcast_fusion), channel_id=1, replica_groups=mesh['y'=4,'z'=8,'core'=2,'col'=4] {'z','core'}, dimensions={0}, use_global_device_ids=true | all-gather | bytes 313344 | tf_op jit(solution)/shard_map/all_gather | solution.py:82
  34.9 2.0 sort.46
  37.6 1.4 gather_fusion.1
  39.7 51.6 %all-gather.4.cloned.1.call-done = f32[1024,1152]{1,0:T(8,128)} async-done(((f32[64,1152]{1,0:T(8,128)}), f32[1024,1152]{1,0:T(8,128)}) %all-gather.4.cloned.1.call-update) | async-done | bytes 4718608 | tf_op jit(solution)/shard_map/all_gather | solution.py:82
  92.6 8.3 %scatter_custom_fusion = f32[1024,1024]{1,0:T(8,128)} fusion(s32[1024]{0:T(1024)S(1)} %fusion.42, f32[1024,1152]{1,0:T(8,128)} %all-gather.4.cloned.1.call-done, f32[]{:T(128)} %constant.852.clone.1), kind=kCustom, calls=%fused_computation.13 | custom fusion | bytes 8389120 | tf_op jit(solution)/shard_map/scatter | solution.py:84
  101.1 5.9 %copy.117 = f32[1024,1024]{0,1:T(8,128)} copy(f32[1024,1024]{1,0:T(8,128)} %scatter_custom_fusion) | data formatting | bytes 8388608 | tf_op jit(solution)/shard_map/optimization_barrier | solution.py:92
  109.1 11.7 %custom-call.20 = f32[128,128]{1,0:T(8,128)S(1)} custom-call(f32[128,128]{1,0:T(8,128)S(1)} %fusion.111), custom_call_target="Cholesky" | custom-call | tf_op jit(solution)/shard_map/cholesky/custom-call.1 | solution.py:40
  122.1 9.8 %custom-call.21 = f32[1,128,128]{1,2,0:T(8,128)S(1)} custom-call(f32[1,128,128]{2,1,0:T(8,128)S(1)} %get-tuple-element.389), custom_call_target="InvertDiagBlocksLowerTriangular" | custom-call | tf_op jit(solution)/shard_map/triangular_solve/custom-call.0 | solution.py:17
  131.9 2.5 scatter.109
  134.8 2.5 scatter.125
  137.3 2.9 constant_dynamic-update-slice_fusion.4
  141.3 11.7 %custom-call.22 = f32[128,128]{1,0:T(8,128)S(1)} custom-call(f32[128,128]{1,0:T(8,128)S(1)} %convolution_subtract_fusion.10), custom_call_target="Cholesky" | custom-call | tf_op jit(solution)/shard_map/cholesky/custom-call.1 | solution.py:40
  153.7 1.3 select_bitcast_fusion.6
  155.0 10.0 %custom-call.23 = f32[1,128,128]{1,2,0:T(8,128)S(1)} custom-call(f32[1,128,128]{2,1,0:T(8,128)S(1)} %get-tuple-element.411), custom_call_target="InvertDiagBlocksLowerTriangular" | custom-call | tf_op jit(solution)/shard_map/triangular_solve/custom-call.0 | solution.py:17
  165.3 1.8 convolution_subtract_fusion
  169.7 11.7 %custom-call.24 = f32[128,128]{1,0:T(8,128)S(1)} custom-call(f32[128,128]{1,0:T(8,128)S(1)} %convolution_subtract_fusion.9), custom_call_target="Cholesky" | custom-call | tf_op jit(solution)/shard_map/cholesky/custom-call.1 | solution.py:40
  182.1 1.3 select_bitcast_fusion.5
  183.4 9.8 %custom-call.25 = f32[1,128,128]{1,2,0:T(8,128)S(1)} custom-call(f32[1,128,128]{2,1,0:T(8,128)S(1)} %get-tuple-element.409), custom_call_target="InvertDiagBlocksLowerTriangular" | custom-call | tf_op jit(solution)/shard_map/triangular_solve/custom-call.0 | solution.py:17
  193.6 2.1 convolution_subtract_fusion.1
  196.9 1.4 convolution_subtract_fusion.12
  198.3 11.9 %custom-call.26 = f32[128,128]{1,0:T(8,128)S(1)} custom-call(f32[128,128]{1,0:T(8,128)S(1)} %convolution_subtract_fusion.12), custom_call_target="Cholesky" | custom-call | tf_op jit(solution)/shard_map/cholesky/custom-call.1 | solution.py:40
  210.9 1.3 select_bitcast_fusion.4
  212.2 9.8 %custom-call.27 = f32[1,128,128]{1,2,0:T(8,128)S(1)} custom-call(f32[1,128,128]{2,1,0:T(8,128)S(1)} %get-tuple-element.407), custom_call_target="InvertDiagBlocksLowerTriangular" | custom-call | tf_op jit(solution)/shard_map/triangular_solve/custom-call.0 | solution.py:17
  222.4 2.2 convolution_subtract_fusion.2
  225.7 1.4 convolution_subtract_fusion.11
  227.1 11.7 %custom-call.28 = f32[128,128]{1,0:T(8,128)S(1)} custom-call(f32[128,128]{1,0:T(8,128)S(1)} %convolution_subtract_fusion.11), custom_call_target="Cholesky" | custom-call | tf_op jit(solution)/shard_map/cholesky/custom-call.1 | solution.py:40
  239.5 1.3 select_bitcast_fusion.3
  240.8 10.2 %custom-call.29 = f32[1,128,128]{1,2,0:T(8,128)S(1)} custom-call(f32[1,128,128]{2,1,0:T(8,128)S(1)} %get-tuple-element.405), custom_call_target="InvertDiagBlocksLowerTriangular" | custom-call | tf_op jit(solution)/shard_map/triangular_solve/custom-call.0 | solution.py:17
  251.6 2.1 convolution_subtract_fusion.3
  254.8 2.4 fusion.30
  257.2 5.0 %sort.48 = (s32[2048]{0:T(1024)}, s32[2048]{0:T(1024)S(1)}) sort(s32[2048]{0:T(1024)S(1)} %fusion.121, s32[2048]{0:T(1024)S(1)} %iota.307), dimensions={0}, to_apply=%region_5.8 | sort | flops 22528 | bytes 32768 | tf_op jit(solution)/shard_map/sort | solution.py:98
  263.9 8.4 %slice.981 = f32[2048,1024]{1,0:T(8,128)} slice(f32[2048,1152]{1,0:T(8,128)} %all-gather.6.cloned.1.call-done), slice={[0:2048], [0:1024]} | slice | bytes 16777216 | tf_op jit(solution)/shard_map/slice | solution.py:95
  272.3 4.1 gather_fusion.4
  277.7 2.4 collective-permute-start.1
  280.0 1.3 collective-permute-start.2
  281.4 1.6 convolution_subtract_fusion.8
  283.0 11.7 %custom-call.30 = f32[128,128]{1,0:T(8,128)S(1)} custom-call(f32[128,128]{1,0:T(8,128)S(1)} %convolution_subtract_fusion.8), custom_call_target="Cholesky" | custom-call | tf_op jit(solution)/shard_map/cholesky/custom-call.1 | solution.py:40
  295.4 1.3 select_bitcast_fusion.2
  296.6 9.8 %custom-call.31 = f32[1,128,128]{1,2,0:T(8,128)S(1)} custom-call(f32[1,128,128]{2,1,0:T(8,128)S(1)} %get-tuple-element.403), custom_call_target="InvertDiagBlocksLowerTriangular" | custom-call | tf_op jit(solution)/shard_map/triangular_solve/custom-call.0 | solution.py:17
  306.8 1.9 convolution_subtract_fusion.4
  309.6 1.6 convolution_subtract_fusion.7
  311.3 11.7 %custom-call.32 = f32[128,128]{1,0:T(8,128)S(1)} custom-call(f32[128,128]{1,0:T(8,128)S(1)} %convolution_subtract_fusion.7), custom_call_target="Cholesky" | custom-call | tf_op jit(solution)/shard_map/cholesky/custom-call.1 | solution.py:40
  323.7 1.3 select_bitcast_fusion.1
  325.0 10.0 %custom-call.33 = f32[1,128,128]{1,2,0:T(8,128)S(1)} custom-call(f32[1,128,128]{2,1,0:T(8,128)S(1)} %get-tuple-element.401), custom_call_target="InvertDiagBlocksLowerTriangular" | custom-call | tf_op jit(solution)/shard_map/triangular_solve/custom-call.0 | solution.py:17
  335.3 1.6 convolution_subtract_fusion.6
  337.8 1.8 convolution_subtract_fusion.5
  339.5 11.7 %custom-call.34 = f32[128,128]{1,0:T(8,128)S(1)} custom-call(f32[128,128]{1,0:T(8,128)S(1)} %convolution_subtract_fusion.5), custom_call_target="Cholesky" | custom-call | tf_op jit(solution)/shard_map/cholesky/custom-call.1 | solution.py:40
  351.9 1.3 select_bitcast_fusion
  355.8 1.3 fusion.65
  358.7 1.7 fusion.40
  362.0 2.0 fusion.31
  365.8 2.8 fusion.20
  370.4 3.6 fusion.17
  376.0 4.2 fusion.6
  380.1 9.8 %custom-call.35 = f32[1,128,128]{1,2,0:T(8,128)S(1)} custom-call(f32[1,128,128]{2,1,0:T(8,128)S(1)} %get-tuple-element.399), custom_call_target="InvertDiagBlocksLowerTriangular" | custom-call | tf_op jit(solution)/shard_map/triangular_solve/custom-call.0 | solution.py:17
  390.3 1.3 fusion.22
  392.3 1.5 constant_dynamic-slice_fusion
  393.9 6.6 %fusion.127 = f32[128,1024]{1,0:T(8,128)S(1)} fusion(f32[128,1024]{1,0:T(8,128)S(1)} %constant_dynamic-update-slice_fusion, f32[1024,1024]{1,0:T(8,128)} %constant_dynamic-update-slice_fusion.9), kind=kOutput, calls=%fused_computation.259 | convolution fusion | flops 1610612736 | bytes 5242880 | tf_op jit(solution)/shard_map/dot_general | solution.py:21
  400.5 1.6 fusion.128
  402.8 4.2 fusion.14
  407.0 4.0 fusion.11
  411.1 5.5 %gather_fusion.7 = f32[2048,128]{1,0:T(8,128)S(1)} fusion(f32[2048,128]{1,0:T(8,128)S(1)} %fusion.11, s32[2048]{0:T(1024)S(1)} %fusion.122), kind=kCustom, calls=%fused_computation.7 | custom fusion | bytes 2105344 | tf_op jit(solution)/shard_map/gather | solution.py:132
  (111 shorter events, 41.7 us)
Async XLA Ops:
  7.2 4.1 copy-start
  7.2 84.2 %all-gather.4.cloned.1.call-start = ((), (), s32[]{:S(2)}) async-start(), calls=%async_computation | async-start | bytes 5013504 | tf_op jit(solution)/shard_map/all_gather | solution.py:82
  34.9 219.9 %all-gather.6.cloned.1.call-start = ((), (), s32[]{:S(2)}) async-start(), calls=%async_computation.1 | async-start | bytes 9584640 | tf_op jit(solution)/shard_map/all_gather | solution.py:93
  92.6 8.5 %copy-start.3 = (s32[2,32]{1,0:T(2,128)S(1)}, s32[2,32]{1,0:T(2,128)}, u32[]{:S(2)}) copy-start(s32[2,32]{1,0:T(2,128)} %param.69) | copy-start | bytes 772
  276.4 117.4 %collective-permute-start = (f32[32,1024]{1,0:T(8,128)S(1)}, f32[32,1024]{1,0:T(8,128)S(1)}, u32[]{:S(2)}, u32[]{:S(2)}) collective-permute-start(f32[32,1024]{1,0:T(8,128)S(1)} %select_multiply_fusion), channel_id=1, source_target_pairs={{0,1},{1,2},{2,3},{3,0},{4,5},{5,6},{6,7},{7,4},{8,9},{9,10},{10,1... | collective-permute-start | bytes 393224 | tf_op jit(solution)/shard_map/ppermute | solution.py:117
  277.7 116.2 %collective-permute-start.1 = (f32[32,1024]{1,0:T(8,128)S(1)}, f32[32,1024]{1,0:T(8,128)S(1)}, u32[]{:S(2)}, u32[]{:S(2)}) collective-permute-start(f32[32,1024]{1,0:T(8,128)S(1)} %select_multiply_fusion), channel_id=1, source_target_pairs={{0,2},{1,3},{2,0},{3,1},{4,6},{5,7},{6,4},{7,5},{8,10},{9,11},{10,... | collective-permute-start | bytes 393224 | tf_op jit(solution)/shard_map/ppermute | solution.py:117
  280.0 113.8 %collective-permute-start.2 = (f32[32,1024]{1,0:T(8,128)S(1)}, f32[32,1024]{1,0:T(8,128)S(1)}, u32[]{:S(2)}, u32[]{:S(2)}) collective-permute-start(f32[32,1024]{1,0:T(8,128)S(1)} %select_multiply_fusion), channel_id=1, source_target_pairs={{0,3},{1,0},{2,1},{3,2},{4,7},{5,4},{6,5},{7,6},{8,11},{9,8},{10,9... | collective-permute-start | bytes 393224 | tf_op jit(solution)/shard_map/ppermute | solution.py:117
  392.3 8.2 %copy-start.1 = (f32[1024,1024]{1,0:T(8,128)S(1)}, f32[1024,1024]{1,0:T(8,128)}, u32[]{:S(2)}) copy-start(f32[1024,1024]{1,0:T(8,128)} %constant_dynamic-update-slice_fusion.9) | copy-start | bytes 12582916
  411.1 5.5 %copy-start.2 = (f32[64,1,32,128]{3,2,1,0:T(8,128)S(1)}, f32[64,1,32,128]{3,2,1,0:T(8,128)}, u32[]{:S(2)}) copy-start(f32[64,1,32,128]{3,2,1,0:T(8,128)} %param.70) | copy-start | bytes 3145732
Sparse Core Ops, SparseCore 0:
  35.0 56.3 all-gather.3
  101.1 85.2 all-gather.5

commit v10 on v8

--- a/solution.py
+++ b/solution.py
@@ -74,7 +74,7 @@
     diag_ids = row_map[order_ids].astype(jnp.float32)
     diag_pack = jnp.concatenate(
         [assembled[order_ids], jnp.broadcast_to(diag_ids[:, None], (diag_share, LANE_PAD))], axis=1)
-    for axis in (("z", "core"), ("y", "col")):
+    for axis in (("y", "col"), ("z", "core")):
         diag_pack = lax.all_gather(diag_pack, axis, axis=0, tiled=True)
     diag_slot = diag_pack[:, twice_width].astype(jnp.int32)
     full = jnp.zeros((twice_width, twice_width), jnp.float32).at[diag_slot].set(

time: 421 us -> 411 us (0.976)
  waiting for transfers between devices: 51.7 us -> 43.9 us
    all_gather x1, waiting for transfers between devices: 51.6 us -> 43.9 us  [local(): diag_pack = lax.all_gather(diag_pack, axis, axis=0, tiled=True)]
  transfers between devices with their start and end apart: 5 -> 5, of which waited for: 1 -> 1; matrix products, arithmetic and copies ran while one was open for 63% -> 64% of each run, Pallas kernels for 0% -> 0%
where the time goes in v10:
time: 411 us; the launch traced here: 406 us
  other arithmetic  205 us (50%)
  matrix products  65.7 us (16%)
  local copies, waits for them, and re-layouts  51.2 us (12%)
  waiting for transfers between devices  43.9 us (11%)
  blocking collectives  19.8 us (5%)
  between operations  14.9 us (4%)
  starting transfers between devices  4.92 us (1%)
    another operation x24, other arithmetic, factor_and_inverse(): block = jnp.tril(lax.linalg.cholesky(column[:size], symmetrize_input=False))  99.5 us
    another operation x16, other arithmetic, lower_inverse(): lax.linalg.triangular_solve(lower_factor, identity, left_side=True, lower...  88.9 us
    all_gather x1, waiting for transfers between devices, local(): diag_pack = lax.all_gather(diag_pack, axis, axis=0, tiled=True)  43.9 us
    dot_general x15, matrix products, contract_rows(): lax.dot_general(left_rows, right_rows, (((1,), (1,)), ((), ())), precisio...  29.5 us
    dot_general x14, matrix products, matmul(): lax.dot_general(left, right, (((1,), (0,)), ((), ())), precision=highest)  24 us
    all_gather x1, blocking collectives, local(): diag_pack = lax.all_gather(diag_pack, axis, axis=0, tiled=True)  19.8 us
    scatter x1, local copies, waits for them, and re-layouts, local(): jnp.zeros((twice_width, twice_width), jnp.float32).at[diag_slot]  8.4 us
    slice x1, local copies, waits for them, and re-layouts, local(): gathered = gathered[:, :twice_width]  8.35 us
  transfers between devices with their start and end apart: 5, of which 1 were waited for; matrix products, arithmetic and copies ran while one was open for 64% of the time, Pallas kernels for 0%

profile of v10, /device:TPU:1, one launch (start us, length us, event | category | flops | bytes accessed | tf_op | source)
XLA Modules:
  0.0 405.9 jit_solution(16506895643595651147)
XLA Ops:
  7.9 2.0 sort.47
  10.0 1.3 gather_fusion.3
  11.9 19.8 %all-gather = f32[16,4,1152]{2,1,0:T(4,128)S(1)} all-gather(f32[1,4,1152]{2,1,0:T(4,128)S(1)} %maximum_bitcast_fusion), channel_id=1, replica_groups=mesh['y'=4,'z'=8,'core'=2,'col'=4] {'y','col'}, dimensions={0}, use_global_device_ids=true | all-gather | bytes 313344 | tf_op jit(solution)/shard_map/all_gather | solution.py:78
  32.6 2.0 sort.46
  35.3 1.4 gather_fusion.1
  37.4 43.9 %all-gather.4.cloned.1.call-done = f32[1024,1152]{1,0:T(8,128)} async-done(((f32[64,1152]{1,0:T(8,128)}), f32[1024,1152]{1,0:T(8,128)}) %all-gather.4.cloned.1.call-update) | async-done | bytes 4718608 | tf_op jit(solution)/shard_map/all_gather | solution.py:78
  81.3 1.3 fusion.43
  82.6 8.4 %scatter_custom_fusion = f32[1024,1024]{1,0:T(8,128)} fusion(s32[1024]{0:T(1024)S(1)} %fusion.43, f32[1024,1152]{1,0:T(8,128)} %all-gather.4.cloned.1.call-done, f32[]{:T(128)} %constant.853.clone.1), kind=kCustom, calls=%fused_computation.13 | custom fusion | bytes 8389120 | tf_op jit(solution)/shard_map/scatter | solution.py:80
  91.1 5.9 %copy.47 = f32[1024,1024]{0,1:T(8,128)} copy(f32[1024,1024]{1,0:T(8,128)} %scatter_custom_fusion) | data formatting | bytes 8388608 | tf_op jit(solution)/shard_map/optimization_barrier | solution.py:88
  97.9 1.3 fusion.45
  99.2 11.7 %custom-call.20 = f32[128,128]{1,0:T(8,128)S(1)} custom-call(f32[128,128]{1,0:T(8,128)S(1)} %slice.948), custom_call_target="Cholesky" | custom-call | tf_op jit(solution)/shard_map/cholesky/custom-call.1 | solution.py:39
  112.3 9.8 %custom-call.21 = f32[1,128,128]{1,2,0:T(8,128)S(1)} custom-call(f32[1,128,128]{2,1,0:T(8,128)S(1)} %get-tuple-element.389), custom_call_target="InvertDiagBlocksLowerTriangular" | custom-call | tf_op jit(solution)/shard_map/triangular_solve/custom-call.0 | solution.py:17
  122.1 2.5 scatter.109
  124.8 2.5 scatter.125
  127.4 1.3 constant_dynamic-update-slice_fusion.4
  128.7 1.7 convolution_subtract_fusion
  130.4 11.7 %custom-call.22 = f32[128,128]{1,0:T(8,128)S(1)} custom-call(f32[128,128]{1,0:T(8,128)S(1)} %slice.952), custom_call_target="Cholesky" | custom-call | tf_op jit(solution)/shard_map/cholesky/custom-call.1 | solution.py:39
  142.8 1.3 select_bitcast_fusion.6
  144.1 10.0 %custom-call.23 = f32[1,128,128]{1,2,0:T(8,128)S(1)} custom-call(f32[1,128,128]{2,1,0:T(8,128)S(1)} %get-tuple-element.403), custom_call_target="InvertDiagBlocksLowerTriangular" | custom-call | tf_op jit(solution)/shard_map/triangular_solve/custom-call.0 | solution.py:17
  154.3 1.3 convolution_dynamic-update-slice_fusion
  155.6 2.3 convolution_subtract_fusion.1
  158.0 11.7 %custom-call.24 = f32[128,128]{1,0:T(8,128)S(1)} custom-call(f32[128,128]{1,0:T(8,128)S(1)} %slice.957), custom_call_target="Cholesky" | custom-call | tf_op jit(solution)/shard_map/cholesky/custom-call.1 | solution.py:39
  170.4 1.3 select_bitcast_fusion.5
  171.7 9.8 %custom-call.25 = f32[1,128,128]{1,2,0:T(8,128)S(1)} custom-call(f32[1,128,128]{2,1,0:T(8,128)S(1)} %get-tuple-element.401), custom_call_target="InvertDiagBlocksLowerTriangular" | custom-call | tf_op jit(solution)/shard_map/triangular_solve/custom-call.0 | solution.py:17
  183.0 2.4 convolution_subtract_fusion.2
  185.5 12.1 %custom-call.26 = f32[128,128]{1,0:T(8,128)S(1)} custom-call(f32[128,128]{1,0:T(8,128)S(1)} %slice.962), custom_call_target="Cholesky" | custom-call | tf_op jit(solution)/shard_map/cholesky/custom-call.1 | solution.py:39
  198.2 1.3 select_bitcast_fusion.4
  199.5 9.8 %custom-call.27 = f32[1,128,128]{1,2,0:T(8,128)S(1)} custom-call(f32[1,128,128]{2,1,0:T(8,128)S(1)} %get-tuple-element.399), custom_call_target="InvertDiagBlocksLowerTriangular" | custom-call | tf_op jit(solution)/shard_map/triangular_solve/custom-call.0 | solution.py:17
  210.8 2.4 convolution_subtract_fusion.3
  213.2 11.7 %custom-call.28 = f32[128,128]{1,0:T(8,128)S(1)} custom-call(f32[128,128]{1,0:T(8,128)S(1)} %slice.967), custom_call_target="Cholesky" | custom-call | tf_op jit(solution)/shard_map/cholesky/custom-call.1 | solution.py:39
  225.6 1.3 select_bitcast_fusion.3
  226.9 9.9 %custom-call.29 = f32[1,128,128]{1,2,0:T(8,128)S(1)} custom-call(f32[1,128,128]{2,1,0:T(8,128)S(1)} %get-tuple-element.397), custom_call_target="InvertDiagBlocksLowerTriangular" | custom-call | tf_op jit(solution)/shard_map/triangular_solve/custom-call.0 | solution.py:17
  238.3 2.4 fusion.30
  240.7 5.0 %sort.48 = (s32[2048]{0:T(1024)}, s32[2048]{0:T(1024)S(1)}) sort(s32[2048]{0:T(1024)S(1)} %fusion.111, s32[2048]{0:T(1024)S(1)} %iota.307), dimensions={0}, to_apply=%region_5.8 | sort | flops 22528 | bytes 32768 | tf_op jit(solution)/shard_map/sort | solution.py:94
  247.4 8.4 %slice.969 = f32[2048,1024]{1,0:T(8,128)} slice(f32[2048,1152]{1,0:T(8,128)} %all-gather.6.cloned.1.call-done), slice={[0:2048], [0:1024]} | slice | bytes 16777216 | tf_op jit(solution)/shard_map/slice | solution.py:91
  255.8 4.1 gather_fusion.4
  259.9 1.3 collective-permute-start
  261.2 2.4 collective-permute-start.1
  264.8 2.3 convolution_subtract_fusion.4
  267.1 11.7 %custom-call.30 = f32[128,128]{1,0:T(8,128)S(1)} custom-call(f32[128,128]{1,0:T(8,128)S(1)} %slice.973), custom_call_target="Cholesky" | custom-call | tf_op jit(solution)/shard_map/cholesky/custom-call.1 | solution.py:39
  279.5 1.3 select_bitcast_fusion.2
  280.8 9.8 %custom-call.31 = f32[1,128,128]{1,2,0:T(8,128)S(1)} custom-call(f32[1,128,128]{2,1,0:T(8,128)S(1)} %get-tuple-element.395), custom_call_target="InvertDiagBlocksLowerTriangular" | custom-call | tf_op jit(solution)/shard_map/triangular_solve/custom-call.0 | solution.py:17
  291.9 2.1 convolution_subtract_fusion.5
  294.0 11.7 %custom-call.32 = f32[128,128]{1,0:T(8,128)S(1)} custom-call(f32[128,128]{1,0:T(8,128)S(1)} %slice.978), custom_call_target="Cholesky" | custom-call | tf_op jit(solution)/shard_map/cholesky/custom-call.1 | solution.py:39
  306.4 1.3 select_bitcast_fusion.1
  307.7 10.2 %custom-call.33 = f32[1,128,128]{1,2,0:T(8,128)S(1)} custom-call(f32[1,128,128]{2,1,0:T(8,128)S(1)} %get-tuple-element.393), custom_call_target="InvertDiagBlocksLowerTriangular" | custom-call | tf_op jit(solution)/shard_map/triangular_solve/custom-call.0 | solution.py:17
  319.0 1.8 convolution_subtract_fusion.6
  320.8 11.7 %custom-call.34 = f32[128,128]{1,0:T(8,128)S(1)} custom-call(f32[128,128]{1,0:T(8,128)S(1)} %convolution_subtract_fusion.6), custom_call_target="Cholesky" | custom-call | tf_op jit(solution)/shard_map/cholesky/custom-call.1 | solution.py:39
  333.2 1.3 select_bitcast_fusion
  337.0 1.3 fusion.65
  339.9 1.7 fusion.41
  343.3 2.0 fusion.31
  347.1 2.8 fusion.20
  351.7 3.4 fusion.17
  355.1 1.2 fusion.23
  357.0 4.2 %fusion.6 = f32[128,896]{1,0:T(8,128)S(1)} fusion(f32[1024,1024]{1,0:T(8,128)} %constant_dynamic-update-slice_fusion.5, f32[1024,1024]{1,0:T(8,128)} %get-tuple-element.392), kind=kOutput, calls=%fused_computation.15 | convolution fusion | flops 1233125376 | bytes 4128768 | tf_op jit(solution)/shard_map/dot_general | solution.py:25
  361.2 9.8 %custom-call.35 = f32[1,128,128]{1,2,0:T(8,128)S(1)} custom-call(f32[1,128,128]{2,1,0:T(8,128)S(1)} %get-tuple-element.391), custom_call_target="InvertDiagBlocksLowerTriangular" | custom-call | tf_op jit(solution)/shard_map/triangular_solve/custom-call.0 | solution.py:17
  371.3 1.3 fusion.22
  373.3 1.5 constant_dynamic-slice_fusion
  375.0 6.6 %fusion.115 = f32[128,1024]{1,0:T(8,128)S(1)} fusion(f32[128,1024]{1,0:T(8,128)S(1)} %constant_dynamic-update-slice_fusion, f32[1024,1024]{1,0:T(8,128)} %constant_dynamic-update-slice_fusion.9), kind=kOutput, calls=%fused_computation.235 | convolution fusion | flops 1610612736 | bytes 5242880 | tf_op jit(solution)/shard_map/dot_general | solution.py:21
  381.5 1.6 fusion.116
  383.9 4.2 %fusion.14 = f32[2048,128]{1,0:T(8,128)S(1)} fusion(f32[2048,1152]{1,0:T(8,128)} %all-gather.6.cloned.1.call-done, f32[2048]{0:T(1024)S(1)} %convert_element_type.60, f32[128,1024]{1,0:T(8,128)S(1)} %fusion.116), kind=kOutput, calls=%fused_computation.19 | convolution fusion | flops 805568512 | bytes 5513216 | tf_op jit(solution)/shard_map/dot_general | solution.py:125
  388.1 4.0 fusion.11
  392.1 5.5 %gather_fusion.7 = f32[2048,128]{1,0:T(8,128)S(1)} fusion(f32[2048,128]{1,0:T(8,128)S(1)} %fusion.11, s32[2048]{0:T(1024)S(1)} %fusion.112), kind=kCustom, calls=%fused_computation.7 | custom fusion | bytes 2105344 | tf_op jit(solution)/shard_map/gather | solution.py:128
  (105 shorter events, 33.8 us)
Async XLA Ops:
  7.2 4.1 %copy-start = (f32[36,1024]{1,0:T(8,128)S(1)}, f32[36,1024]{1,0:T(8,128)}, u32[]{:S(2)}) copy-start(f32[36,1024]{1,0:T(8,128)} %param.67) | copy-start | bytes 442372
  7.2 74.1 %all-gather.4.cloned.1.call-start = ((), (), s32[]{:S(2)}) async-start(), calls=%async_computation | async-start | bytes 5013504 | tf_op jit(solution)/shard_map/all_gather | solution.py:78
  32.6 205.7 %all-gather.6.cloned.1.call-start = ((), (), s32[]{:S(2)}) async-start(), calls=%async_computation.1 | async-start | bytes 9584640 | tf_op jit(solution)/shard_map/all_gather | solution.py:89
  82.6 8.5 %copy-start.3 = (s32[2,32]{1,0:T(2,128)S(1)}, s32[2,32]{1,0:T(2,128)}, u32[]{:S(2)}) copy-start(s32[2,32]{1,0:T(2,128)} %param.69) | copy-start | bytes 772
  259.9 114.9 %collective-permute-start = (f32[32,1024]{1,0:T(8,128)S(1)}, f32[32,1024]{1,0:T(8,128)S(1)}, u32[]{:S(2)}, u32[]{:S(2)}) collective-permute-start(f32[32,1024]{1,0:T(8,128)S(1)} %select_multiply_fusion), channel_id=1, source_target_pairs={{0,1},{1,2},{2,3},{3,0},{4,5},{5,6},{6,7},{7,4},{8,9},{9,10},{10,1... | collective-permute-start | bytes 393224 | tf_op jit(solution)/shard_map/ppermute | solution.py:113
  261.2 113.7 %collective-permute-start.1 = (f32[32,1024]{1,0:T(8,128)S(1)}, f32[32,1024]{1,0:T(8,128)S(1)}, u32[]{:S(2)}, u32[]{:S(2)}) collective-permute-start(f32[32,1024]{1,0:T(8,128)S(1)} %select_multiply_fusion), channel_id=1, source_target_pairs={{0,2},{1,3},{2,0},{3,1},{4,6},{5,7},{6,4},{7,5},{8,10},{9,11},{10,... | collective-permute-start | bytes 393224 | tf_op jit(solution)/shard_map/ppermute | solution.py:113
  263.6 111.3 %collective-permute-start.2 = (f32[32,1024]{1,0:T(8,128)S(1)}, f32[32,1024]{1,0:T(8,128)S(1)}, u32[]{:S(2)}, u32[]{:S(2)}) collective-permute-start(f32[32,1024]{1,0:T(8,128)S(1)} %select_multiply_fusion), channel_id=1, source_target_pairs={{0,3},{1,0},{2,1},{3,2},{4,7},{5,4},{6,5},{7,6},{8,11},{9,8},{10,9... | collective-permute-start | bytes 393224 | tf_op jit(solution)/shard_map/ppermute | solution.py:113
  373.3 8.2 %copy-start.1 = (f32[1024,1024]{1,0:T(8,128)S(1)}, f32[1024,1024]{1,0:T(8,128)}, u32[]{:S(2)}) copy-start(f32[1024,1024]{1,0:T(8,128)} %constant_dynamic-update-slice_fusion.9) | copy-start | bytes 12582916
  392.1 5.5 %copy-start.2 = (f32[64,1,32,128]{3,2,1,0:T(8,128)S(1)}, f32[64,1,32,128]{3,2,1,0:T(8,128)}, u32[]{:S(2)}) copy-start(f32[64,1,32,128]{3,2,1,0:T(8,128)} %param.70) | copy-start | bytes 3145732
Sparse Core Ops, SparseCore 0:
  32.7 48.5 all-gather.3
  91.1 83.4 all-gather.5

commit v11 on v10

--- a/solution.py
+++ b/solution.py
@@ -106,13 +106,16 @@
     def exchange(tied):
         own, first, second, source = tied
         rows = own.shape[0]
+        held = own
+        shift = 1
+        while shift < col_count:
+            pairs = [(c, (c + shift) % col_count) for c in range(col_count)]
+            held = jnp.concatenate([held, lax.ppermute(held, "col", pairs)], axis=0)
+            shift *= 2
         owners = jnp.zeros((col_count * rows, own.shape[1]), jnp.float32)
-        owners = lax.dynamic_update_slice_in_dim(owners, own, col_index * rows, 0)
-        for shift in range(1, col_count):
-            pairs = [(c, (c + shift) % col_count) for c in range(col_count)]
-            arrived = lax.ppermute(own, "col", pairs)
+        for back in range(col_count):
             owners = lax.dynamic_update_slice_in_dim(
-                owners, arrived, ((col_index - shift) % col_count) * rows, 0)
+                owners, held[back * rows:(back + 1) * rows], ((col_index - back) % col_count) * rows, 0)
         return (owners, first, second, source)
 
     factor, inverse, tied = factor_and_inverse(full, (masked_own, first_keep, second_keep, trail_src), exchange)

time: 411 us -> 417 us (1.015)
  waiting for transfers between devices: 43.9 us -> 52.2 us
    ppermute x3 -> x2, waiting for transfers between devices: 0.01 us -> 8.24 us  [exchange(): held = jnp.concatenate([held, lax.ppermute(held, 'col', pairs)], axis=0)]
  transfers between devices with their start and end apart: 5 -> 4, of which waited for: 1 -> 3; matrix products, arithmetic and copies ran while one was open for 64% -> 38% of each run, Pallas kernels for 0% -> 0%
where the time goes in v11:
time: 417 us; the launch traced here: 412 us
  other arithmetic  205 us (49%)
  matrix products  65.7 us (16%)
  waiting for transfers between devices  52.2 us (13%)
  local copies, waits for them, and re-layouts  51 us (12%)
  blocking collectives  19.8 us (5%)
  between operations  15.1 us (4%)
    another operation x24, other arithmetic, factor_and_inverse(): block = jnp.tril(lax.linalg.cholesky(column[:size], symmetrize_input=False))  99.3 us
    another operation x16, other arithmetic, lower_inverse(): lax.linalg.triangular_solve(lower_factor, identity, left_side=True, lower...  88.7 us
    all_gather x1, waiting for transfers between devices, local(): diag_pack = lax.all_gather(diag_pack, axis, axis=0, tiled=True)  43.9 us
    dot_general x15, matrix products, contract_rows(): lax.dot_general(left_rows, right_rows, (((1,), (1,)), ((), ())), precisio...  29.7 us
    dot_general x14, matrix products, matmul(): lax.dot_general(left, right, (((1,), (0,)), ((), ())), precision=highest)  24.1 us
    all_gather x1, blocking collectives, local(): diag_pack = lax.all_gather(diag_pack, axis, axis=0, tiled=True)  19.8 us
    scatter x1, local copies, waits for them, and re-layouts, local(): jnp.zeros((twice_width, twice_width), jnp.float32).at[diag_slot]  8.4 us
    slice x1, local copies, waits for them, and re-layouts, local(): gathered = gathered[:, :twice_width]  8.35 us
  transfers between devices with their start and end apart: 4, of which 3 were waited for; matrix products, arithmetic and copies ran while one was open for 38% of the time, Pallas kernels for 0%

profile of v11, /device:TPU:1, one launch (start us, length us, event | category | flops | bytes accessed | tf_op | source)
XLA Modules:
  0.0 412.0 jit_solution(16975953806784582505)
XLA Ops:
  7.9 2.0 sort.47
  10.0 1.3 gather_fusion.3
  11.9 19.8 %all-gather = f32[16,4,1152]{2,1,0:T(4,128)S(1)} all-gather(f32[1,4,1152]{2,1,0:T(4,128)S(1)} %maximum_bitcast_fusion), channel_id=1, replica_groups=mesh['y'=4,'z'=8,'core'=2,'col'=4] {'y','col'}, dimensions={0}, use_global_device_ids=true | all-gather | bytes 313344 | tf_op jit(solution)/shard_map/all_gather | solution.py:78
  32.6 2.0 sort.46
  35.3 1.4 gather_fusion.1
  37.4 43.9 %all-gather.4.cloned.1.call-done = f32[1024,1152]{1,0:T(8,128)} async-done(((f32[64,1152]{1,0:T(8,128)}), f32[1024,1152]{1,0:T(8,128)}) %all-gather.4.cloned.1.call-update) | async-done | bytes 4718608 | tf_op jit(solution)/shard_map/all_gather | solution.py:78
  81.3 1.3 fusion.43
  82.6 8.4 %scatter_custom_fusion = f32[1024,1024]{1,0:T(8,128)} fusion(s32[1024]{0:T(1024)S(1)} %fusion.43, f32[1024,1152]{1,0:T(8,128)} %all-gather.4.cloned.1.call-done, f32[]{:T(128)} %constant.857.clone.1), kind=kCustom, calls=%fused_computation.13 | custom fusion | bytes 8389120 | tf_op jit(solution)/shard_map/scatter | solution.py:80
  91.1 5.9 %copy.47 = f32[1024,1024]{0,1:T(8,128)} copy(f32[1024,1024]{1,0:T(8,128)} %scatter_custom_fusion) | data formatting | bytes 8388608 | tf_op jit(solution)/shard_map/optimization_barrier | solution.py:88
  97.9 1.3 fusion.45
  99.2 11.7 %custom-call.20 = f32[128,128]{1,0:T(8,128)S(1)} custom-call(f32[128,128]{1,0:T(8,128)S(1)} %slice.956), custom_call_target="Cholesky" | custom-call | tf_op jit(solution)/shard_map/cholesky/custom-call.1 | solution.py:39
  112.2 9.8 %custom-call.21 = f32[1,128,128]{1,2,0:T(8,128)S(1)} custom-call(f32[1,128,128]{2,1,0:T(8,128)S(1)} %get-tuple-element.389), custom_call_target="InvertDiagBlocksLowerTriangular" | custom-call | tf_op jit(solution)/shard_map/triangular_solve/custom-call.0 | solution.py:17
  122.0 2.5 scatter.109
  124.8 2.5 scatter.125
  127.3 1.3 constant_dynamic-update-slice_fusion.2
  128.6 1.7 convolution_subtract_fusion
  130.4 11.7 %custom-call.22 = f32[128,128]{1,0:T(8,128)S(1)} custom-call(f32[128,128]{1,0:T(8,128)S(1)} %slice.960), custom_call_target="Cholesky" | custom-call | tf_op jit(solution)/shard_map/cholesky/custom-call.1 | solution.py:39
  142.8 1.3 select_bitcast_fusion.6
  144.0 9.9 %custom-call.23 = f32[1,128,128]{1,2,0:T(8,128)S(1)} custom-call(f32[1,128,128]{2,1,0:T(8,128)S(1)} %get-tuple-element.403), custom_call_target="InvertDiagBlocksLowerTriangular" | custom-call | tf_op jit(solution)/shard_map/triangular_solve/custom-call.0 | solution.py:17
  154.3 1.3 convolution_dynamic-update-slice_fusion
  155.6 2.4 convolution_subtract_fusion.1
  157.9 11.7 %custom-call.24 = f32[128,128]{1,0:T(8,128)S(1)} custom-call(f32[128,128]{1,0:T(8,128)S(1)} %slice.965), custom_call_target="Cholesky" | custom-call | tf_op jit(solution)/shard_map/cholesky/custom-call.1 | solution.py:39
  170.3 1.3 select_bitcast_fusion.5
  171.6 9.8 %custom-call.25 = f32[1,128,128]{1,2,0:T(8,128)S(1)} custom-call(f32[1,128,128]{2,1,0:T(8,128)S(1)} %get-tuple-element.401), custom_call_target="InvertDiagBlocksLowerTriangular" | custom-call | tf_op jit(solution)/shard_map/triangular_solve/custom-call.0 | solution.py:17
  183.0 2.4 convolution_subtract_fusion.2
  185.4 11.9 %custom-call.26 = f32[128,128]{1,0:T(8,128)S(1)} custom-call(f32[128,128]{1,0:T(8,128)S(1)} %slice.970), custom_call_target="Cholesky" | custom-call | tf_op jit(solution)/shard_map/cholesky/custom-call.1 | solution.py:39
  198.0 1.3 select_bitcast_fusion.4
  199.3 9.8 %custom-call.27 = f32[1,128,128]{1,2,0:T(8,128)S(1)} custom-call(f32[1,128,128]{2,1,0:T(8,128)S(1)} %get-tuple-element.399), custom_call_target="InvertDiagBlocksLowerTriangular" | custom-call | tf_op jit(solution)/shard_map/triangular_solve/custom-call.0 | solution.py:17
  210.5 2.4 convolution_subtract_fusion.3
  212.9 11.7 %custom-call.28 = f32[128,128]{1,0:T(8,128)S(1)} custom-call(f32[128,128]{1,0:T(8,128)S(1)} %slice.975), custom_call_target="Cholesky" | custom-call | tf_op jit(solution)/shard_map/cholesky/custom-call.1 | solution.py:39
  225.3 1.3 select_bitcast_fusion.3
  226.6 10.2 %custom-call.29 = f32[1,128,128]{1,2,0:T(8,128)S(1)} custom-call(f32[1,128,128]{2,1,0:T(8,128)S(1)} %get-tuple-element.397), custom_call_target="InvertDiagBlocksLowerTriangular" | custom-call | tf_op jit(solution)/shard_map/triangular_solve/custom-call.0 | solution.py:17
  238.3 2.4 fusion.30
  240.7 5.0 %sort.48 = (s32[2048]{0:T(1024)}, s32[2048]{0:T(1024)S(1)}) sort(s32[2048]{0:T(1024)S(1)} %fusion.111, s32[2048]{0:T(1024)S(1)} %iota.307), dimensions={0}, to_apply=%region_5.8 | sort | flops 22528 | bytes 32768 | tf_op jit(solution)/shard_map/sort | solution.py:94
  247.4 8.4 %slice.977 = f32[2048,1024]{1,0:T(8,128)} slice(f32[2048,1152]{1,0:T(8,128)} %all-gather.6.cloned.1.call-done), slice={[0:2048], [0:1024]} | slice | bytes 16777216 | tf_op jit(solution)/shard_map/slice | solution.py:91
  255.8 4.1 gather_fusion.4
  259.9 2.3 convolution_subtract_fusion.4
  262.3 11.7 %custom-call.30 = f32[128,128]{1,0:T(8,128)S(1)} custom-call(f32[128,128]{1,0:T(8,128)S(1)} %slice.983), custom_call_target="Cholesky" | custom-call | tf_op jit(solution)/shard_map/cholesky/custom-call.1 | solution.py:39
  274.7 1.3 select_bitcast_fusion.2
  276.0 9.8 %custom-call.31 = f32[1,128,128]{1,2,0:T(8,128)S(1)} custom-call(f32[1,128,128]{2,1,0:T(8,128)S(1)} %get-tuple-element.395), custom_call_target="InvertDiagBlocksLowerTriangular" | custom-call | tf_op jit(solution)/shard_map/triangular_solve/custom-call.0 | solution.py:17
  287.0 2.3 convolution_subtract_fusion.5
  289.3 11.7 %custom-call.32 = f32[128,128]{1,0:T(8,128)S(1)} custom-call(f32[128,128]{1,0:T(8,128)S(1)} %slice.988), custom_call_target="Cholesky" | custom-call | tf_op jit(solution)/shard_map/cholesky/custom-call.1 | solution.py:39
  301.7 1.3 select_bitcast_fusion.1
  303.0 9.8 %custom-call.33 = f32[1,128,128]{1,2,0:T(8,128)S(1)} custom-call(f32[1,128,128]{2,1,0:T(8,128)S(1)} %get-tuple-element.393), custom_call_target="InvertDiagBlocksLowerTriangular" | custom-call | tf_op jit(solution)/shard_map/triangular_solve/custom-call.0 | solution.py:17
  314.0 1.8 convolution_subtract_fusion.6
  315.8 11.7 %custom-call.34 = f32[128,128]{1,0:T(8,128)S(1)} custom-call(f32[128,128]{1,0:T(8,128)S(1)} %convolution_subtract_fusion.6), custom_call_target="Cholesky" | custom-call | tf_op jit(solution)/shard_map/cholesky/custom-call.1 | solution.py:39
  328.2 1.3 select_bitcast_fusion
  332.0 1.3 fusion.65
  335.1 1.7 fusion.41
  338.5 2.0 fusion.31
  342.2 2.8 fusion.20
  346.9 3.2 fusion.17
  352.0 4.2 %fusion.6 = f32[128,896]{1,0:T(8,128)S(1)} fusion(f32[1024,1024]{1,0:T(8,128)} %constant_dynamic-update-slice_fusion.3, f32[1024,1024]{1,0:T(8,128)} %get-tuple-element.392), kind=kOutput, calls=%fused_computation.15 | convolution fusion | flops 1233125376 | bytes 4128768 | tf_op jit(solution)/shard_map/dot_general | solution.py:25
  356.2 9.8 %custom-call.35 = f32[1,128,128]{1,2,0:T(8,128)S(1)} custom-call(f32[1,128,128]{2,1,0:T(8,128)S(1)} %get-tuple-element.391), custom_call_target="InvertDiagBlocksLowerTriangular" | custom-call | tf_op jit(solution)/shard_map/triangular_solve/custom-call.0 | solution.py:17
  367.5 1.3 fusion.22
  369.5 2.9 collective-permute-done
  372.4 1.8 collective-permute-start.1
  374.2 1.4 constant_dynamic-slice_fusion
  375.7 5.3 %collective-permute-done.1 = f32[64,1024]{1,0:T(8,128)S(1)} collective-permute-done((f32[64,1024]{1,0:T(8,128)S(1)}, f32[64,1024]{1,0:T(8,128)S(1)}, u32[]{:S(2)}, u32[]{:S(2)}) %collective-permute-start.1) | collective-permute-done | bytes 262176 | tf_op jit(solution)/shard_map/ppermute | solution.py:113
  381.1 6.6 %fusion.115 = f32[128,1024]{1,0:T(8,128)S(1)} fusion(f32[128,1024]{1,0:T(8,128)S(1)} %slice_dynamic-update-slice_fusion, f32[1024,1024]{1,0:T(8,128)} %constant_dynamic-update-slice_fusion.7), kind=kOutput, calls=%fused_computation.236 | convolution fusion | flops 1610612736 | bytes 5242880 | tf_op jit(solution)/shard_map/dot_general | solution.py:21
  387.6 1.6 fusion.116
  390.0 4.0 fusion.14
  394.0 4.0 fusion.11
  398.0 5.5 %gather_fusion.7 = f32[2048,128]{1,0:T(8,128)S(1)} fusion(f32[2048,128]{1,0:T(8,128)S(1)} %fusion.11, s32[2048]{0:T(1024)S(1)} %fusion.112), kind=kCustom, calls=%fused_computation.7 | custom fusion | bytes 2105344 | tf_op jit(solution)/shard_map/gather | solution.py:131
  (104 shorter events, 35.3 us)
Async XLA Ops:
  7.2 4.1 copy-start
  7.2 74.1 %all-gather.4.cloned.1.call-start = ((), (), s32[]{:S(2)}) async-start(), calls=%async_computation | async-start | bytes 5013504 | tf_op jit(solution)/shard_map/all_gather | solution.py:78
  32.6 205.7 %all-gather.6.cloned.1.call-start = ((), (), s32[]{:S(2)}) async-start(), calls=%async_computation.1 | async-start | bytes 9584640 | tf_op jit(solution)/shard_map/all_gather | solution.py:89
  82.6 8.5 %copy-start.3 = (s32[2,32]{1,0:T(2,128)S(1)}, s32[2,32]{1,0:T(2,128)}, u32[]{:S(2)}) copy-start(s32[2,32]{1,0:T(2,128)} %param.69) | copy-start | bytes 772
  366.3 6.1 %collective-permute-start = (f32[32,1024]{1,0:T(8,128)S(1)}, f32[32,1024]{1,0:T(8,128)S(1)}, u32[]{:S(2)}, u32[]{:S(2)}) collective-permute-start(f32[32,1024]{1,0:T(8,128)S(1)} %select_multiply_fusion), channel_id=1, source_target_pairs={{0,1},{1,2},{2,3},{3,0},{4,5},{5,6},{6,7},{7,4},{8,9},{9,10},{10,1... | collective-permute-start | bytes 393224 | tf_op jit(solution)/shard_map/ppermute | solution.py:113
  369.5 18.2 %copy-start.1 = (f32[1024,1024]{1,0:T(8,128)S(1)}, f32[1024,1024]{1,0:T(8,128)}, u32[]{:S(2)}) copy-start(f32[1024,1024]{1,0:T(8,128)} %constant_dynamic-update-slice_fusion.7) | copy-start | bytes 12582916
  372.4 8.6 %collective-permute-start.1 = (f32[64,1024]{1,0:T(8,128)S(1)}, f32[64,1024]{1,0:T(8,128)S(1)}, u32[]{:S(2)}, u32[]{:S(2)}) collective-permute-start(f32[64,1024]{1,0:T(8,128)S(1)} %pad_maximum_fusion), channel_id=1, source_target_pairs={{0,2},{1,3},{2,0},{3,1},{4,6},{5,7},{6,4},{7,5},{8,10},{9,11},{10,... | collective-permute-start | bytes 786440 | tf_op jit(solution)/shard_map/ppermute | solution.py:113
  398.0 5.5 %copy-start.2 = (f32[64,1,32,128]{3,2,1,0:T(8,128)S(1)}, f32[64,1,32,128]{3,2,1,0:T(8,128)}, u32[]{:S(2)}) copy-start(f32[64,1,32,128]{3,2,1,0:T(8,128)} %param.70) | copy-start | bytes 3145732
Sparse Core Ops, SparseCore 0:
  32.7 48.5 all-gather.3
  91.1 83.6 all-gather.5

commit v12 on v10

--- a/solution.py
+++ b/solution.py
@@ -74,7 +74,7 @@
     diag_ids = row_map[order_ids].astype(jnp.float32)
     diag_pack = jnp.concatenate(
         [assembled[order_ids], jnp.broadcast_to(diag_ids[:, None], (diag_share, LANE_PAD))], axis=1)
-    for axis in (("y", "col"), ("z", "core")):
+    for axis in (("y", "col", "core"), ("z",)):
         diag_pack = lax.all_gather(diag_pack, axis, axis=0, tiled=True)
     diag_slot = diag_pack[:, twice_width].astype(jnp.int32)
     full = jnp.zeros((twice_width, twice_width), jnp.float32).at[diag_slot].set(

time: 411 us -> 430 us (1.046)
  waiting for transfers between devices: 43.9 us -> 55.8 us
  blocking collectives: 19.8 us -> 26.5 us
    all_gather x1, waiting for transfers between devices: 43.9 us -> 55.8 us  [local(): diag_pack = lax.all_gather(diag_pack, axis, axis=0, tiled=True)]
    all_gather x1, blocking collectives: 19.8 us -> 26.5 us  [local(): diag_pack = lax.all_gather(diag_pack, axis, axis=0, tiled=True)]
  transfers between devices with their start and end apart: 5 -> 5, of which waited for: 1 -> 1; matrix products, arithmetic and copies ran while one was open for 64% -> 62% of each run, Pallas kernels for 0% -> 0%
where the time goes in v12:
time: 430 us; the launch traced here: 424 us
  other arithmetic  205 us (48%)
  matrix products  65.6 us (15%)
  waiting for transfers between devices  55.8 us (13%)
  local copies, waits for them, and re-layouts  50.8 us (12%)
  blocking collectives  26.5 us (6%)
  between operations  14.9 us (3%)
  starting transfers between devices  4.93 us (1%)
    another operation x24, other arithmetic, factor_and_inverse(): block = jnp.tril(lax.linalg.cholesky(column[:size], symmetrize_input=False))  99.5 us
    another operation x16, other arithmetic, lower_inverse(): lax.linalg.triangular_solve(lower_factor, identity, left_side=True, lower...  88.9 us
    all_gather x1, waiting for transfers between devices, local(): diag_pack = lax.all_gather(diag_pack, axis, axis=0, tiled=True)  55.8 us
    dot_general x15, matrix products, contract_rows(): lax.dot_general(left_rows, right_rows, (((1,), (1,)), ((), ())), precisio...  29.4 us
    all_gather x1, blocking collectives, local(): diag_pack = lax.all_gather(diag_pack, axis, axis=0, tiled=True)  26.5 us
    dot_general x14, matrix products, matmul(): lax.dot_general(left, right, (((1,), (0,)), ((), ())), precision=highest)  24 us
  transfers between devices with their start and end apart: 5, of which 1 were waited for; matrix products, arithmetic and copies ran while one was open for 62% of the time, Pallas kernels for 0%

profile of v12, /device:TPU:1, one launch (start us, length us, event | category | flops | bytes accessed | tf_op | source)
XLA Modules:
  0.0 423.9 jit_solution(11428317784304633874)
XLA Ops:
  7.9 2.0 sort.47
  10.0 1.3 gather_fusion.3
  11.9 26.5 %all-gather = f32[32,4,1152]{2,1,0:T(4,128)S(1)} all-gather(f32[1,4,1152]{2,1,0:T(4,128)S(1)} %maximum_bitcast_fusion), channel_id=1, replica_groups=mesh['y'=4,'z'=8,'core'=2,'col'=4] {'y','col','core'}, dimensions={0}, use_global_device_ids=true | all-gather | bytes 608256 | tf_op jit(solution)/shard_map/all_gather | solution.py:78
  39.5 2.0 sort.46
  43.7 55.8 %all-gather.4.cloned.1.call-done = f32[1024,1152]{1,0:T(8,128)} async-done(((f32[128,1152]{1,0:T(8,128)}), f32[1024,1152]{1,0:T(8,128)}) %all-gather.4.cloned.1.call-update) | async-done | bytes 4718608 | tf_op jit(solution)/shard_map/all_gather | solution.py:78
  99.5 1.3 fusion.43
  100.7 8.4 %scatter_custom_fusion = f32[1024,1024]{1,0:T(8,128)} fusion(s32[1024]{0:T(1024)S(1)} %fusion.43, f32[1024,1152]{1,0:T(8,128)} %all-gather.4.cloned.1.call-done, f32[]{:T(128)} %constant.853.clone.1), kind=kCustom, calls=%fused_computation.13 | custom fusion | bytes 8389120 | tf_op jit(solution)/shard_map/scatter | solution.py:80
  109.3 5.9 %copy.47 = f32[1024,1024]{0,1:T(8,128)} copy(f32[1024,1024]{1,0:T(8,128)} %scatter_custom_fusion) | data formatting | bytes 8388608 | tf_op jit(solution)/shard_map/optimization_barrier | solution.py:88
  116.1 1.3 fusion.45
  117.3 11.7 %custom-call.20 = f32[128,128]{1,0:T(8,128)S(1)} custom-call(f32[128,128]{1,0:T(8,128)S(1)} %slice.948), custom_call_target="Cholesky" | custom-call | tf_op jit(solution)/shard_map/cholesky/custom-call.1 | solution.py:39
  130.4 9.8 %custom-call.21 = f32[1,128,128]{1,2,0:T(8,128)S(1)} custom-call(f32[1,128,128]{2,1,0:T(8,128)S(1)} %get-tuple-element.389), custom_call_target="InvertDiagBlocksLowerTriangular" | custom-call | tf_op jit(solution)/shard_map/triangular_solve/custom-call.0 | solution.py:17
  140.2 2.5 scatter.109
  143.0 2.5 scatter.125
  145.5 1.3 constant_dynamic-update-slice_fusion.4
  146.8 1.7 convolution_subtract_fusion
  148.5 11.7 %custom-call.22 = f32[128,128]{1,0:T(8,128)S(1)} custom-call(f32[128,128]{1,0:T(8,128)S(1)} %slice.952), custom_call_target="Cholesky" | custom-call | tf_op jit(solution)/shard_map/cholesky/custom-call.1 | solution.py:39
  160.9 1.3 select_bitcast_fusion.6
  162.2 9.9 %custom-call.23 = f32[1,128,128]{1,2,0:T(8,128)S(1)} custom-call(f32[1,128,128]{2,1,0:T(8,128)S(1)} %get-tuple-element.403), custom_call_target="InvertDiagBlocksLowerTriangular" | custom-call | tf_op jit(solution)/shard_map/triangular_solve/custom-call.0 | solution.py:17
  172.5 1.3 convolution_dynamic-update-slice_fusion
  173.7 2.2 convolution_subtract_fusion.1
  176.0 11.7 %custom-call.24 = f32[128,128]{1,0:T(8,128)S(1)} custom-call(f32[128,128]{1,0:T(8,128)S(1)} %slice.957), custom_call_target="Cholesky" | custom-call | tf_op jit(solution)/shard_map/cholesky/custom-call.1 | solution.py:39
  188.4 1.3 select_bitcast_fusion.5
  189.7 9.8 %custom-call.25 = f32[1,128,128]{1,2,0:T(8,128)S(1)} custom-call(f32[1,128,128]{2,1,0:T(8,128)S(1)} %get-tuple-element.401), custom_call_target="InvertDiagBlocksLowerTriangular" | custom-call | tf_op jit(solution)/shard_map/triangular_solve/custom-call.0 | solution.py:17
  199.8 1.2 convolution_dynamic-update-slice_fusion.1
  201.0 2.4 convolution_subtract_fusion.2
  203.5 12.1 %custom-call.26 = f32[128,128]{1,0:T(8,128)S(1)} custom-call(f32[128,128]{1,0:T(8,128)S(1)} %slice.962), custom_call_target="Cholesky" | custom-call | tf_op jit(solution)/shard_map/cholesky/custom-call.1 | solution.py:39
  216.3 1.3 select_bitcast_fusion.4
  217.6 9.8 %custom-call.27 = f32[1,128,128]{1,2,0:T(8,128)S(1)} custom-call(f32[1,128,128]{2,1,0:T(8,128)S(1)} %get-tuple-element.399), custom_call_target="InvertDiagBlocksLowerTriangular" | custom-call | tf_op jit(solution)/shard_map/triangular_solve/custom-call.0 | solution.py:17
  228.8 2.4 convolution_subtract_fusion.3
  231.2 11.7 %custom-call.28 = f32[128,128]{1,0:T(8,128)S(1)} custom-call(f32[128,128]{1,0:T(8,128)S(1)} %slice.967), custom_call_target="Cholesky" | custom-call | tf_op jit(solution)/shard_map/cholesky/custom-call.1 | solution.py:39
  243.6 1.3 select_bitcast_fusion.3
  244.9 9.9 %custom-call.29 = f32[1,128,128]{1,2,0:T(8,128)S(1)} custom-call(f32[1,128,128]{2,1,0:T(8,128)S(1)} %get-tuple-element.397), custom_call_target="InvertDiagBlocksLowerTriangular" | custom-call | tf_op jit(solution)/shard_map/triangular_solve/custom-call.0 | solution.py:17
  256.3 2.4 fusion.30
  258.8 5.0 %sort.48 = (s32[2048]{0:T(1024)}, s32[2048]{0:T(1024)S(1)}) sort(s32[2048]{0:T(1024)S(1)} %fusion.111, s32[2048]{0:T(1024)S(1)} %iota.307), dimensions={0}, to_apply=%region_5.8 | sort | flops 22528 | bytes 32768 | tf_op jit(solution)/shard_map/sort | solution.py:94
  265.5 8.4 %slice.969 = f32[2048,1024]{1,0:T(8,128)} slice(f32[2048,1152]{1,0:T(8,128)} %all-gather.6.cloned.1.call-done), slice={[0:2048], [0:1024]} | slice | bytes 16777216 | tf_op jit(solution)/shard_map/slice | solution.py:91
  273.8 4.1 gather_fusion.4
  278.0 1.3 collective-permute-start
  279.2 2.4 collective-permute-start.1
  282.8 2.3 convolution_subtract_fusion.4
  285.2 11.7 %custom-call.30 = f32[128,128]{1,0:T(8,128)S(1)} custom-call(f32[128,128]{1,0:T(8,128)S(1)} %slice.973), custom_call_target="Cholesky" | custom-call | tf_op jit(solution)/shard_map/cholesky/custom-call.1 | solution.py:39
  297.6 1.3 select_bitcast_fusion.2
  298.8 9.8 %custom-call.31 = f32[1,128,128]{1,2,0:T(8,128)S(1)} custom-call(f32[1,128,128]{2,1,0:T(8,128)S(1)} %get-tuple-element.395), custom_call_target="InvertDiagBlocksLowerTriangular" | custom-call | tf_op jit(solution)/shard_map/triangular_solve/custom-call.0 | solution.py:17
  309.9 2.1 convolution_subtract_fusion.5
  312.0 11.7 %custom-call.32 = f32[128,128]{1,0:T(8,128)S(1)} custom-call(f32[128,128]{1,0:T(8,128)S(1)} %slice.978), custom_call_target="Cholesky" | custom-call | tf_op jit(solution)/shard_map/cholesky/custom-call.1 | solution.py:39
  324.4 1.3 select_bitcast_fusion.1
  325.7 10.2 %custom-call.33 = f32[1,128,128]{1,2,0:T(8,128)S(1)} custom-call(f32[1,128,128]{2,1,0:T(8,128)S(1)} %get-tuple-element.393), custom_call_target="InvertDiagBlocksLowerTriangular" | custom-call | tf_op jit(solution)/shard_map/triangular_solve/custom-call.0 | solution.py:17
  337.1 1.8 convolution_subtract_fusion.6
  338.9 11.7 %custom-call.34 = f32[128,128]{1,0:T(8,128)S(1)} custom-call(f32[128,128]{1,0:T(8,128)S(1)} %convolution_subtract_fusion.6), custom_call_target="Cholesky" | custom-call | tf_op jit(solution)/shard_map/cholesky/custom-call.1 | solution.py:39
  351.3 1.3 select_bitcast_fusion
  355.1 1.3 fusion.65
  358.0 1.7 fusion.41
  361.4 2.0 fusion.31
  365.1 2.8 fusion.20
  369.7 3.4 fusion.17
  373.2 1.2 fusion.23
  375.0 4.2 fusion.6
  379.2 9.8 %custom-call.35 = f32[1,128,128]{1,2,0:T(8,128)S(1)} custom-call(f32[1,128,128]{2,1,0:T(8,128)S(1)} %get-tuple-element.391), custom_call_target="InvertDiagBlocksLowerTriangular" | custom-call | tf_op jit(solution)/shard_map/triangular_solve/custom-call.0 | solution.py:17
  389.4 1.3 fusion.22
  391.4 1.5 constant_dynamic-slice_fusion
  393.0 6.6 %fusion.115 = f32[128,1024]{1,0:T(8,128)S(1)} fusion(f32[128,1024]{1,0:T(8,128)S(1)} %constant_dynamic-update-slice_fusion, f32[1024,1024]{1,0:T(8,128)} %constant_dynamic-update-slice_fusion.9), kind=kOutput, calls=%fused_computation.235 | convolution fusion | flops 1610612736 | bytes 5242880 | tf_op jit(solution)/shard_map/dot_general | solution.py:21
  399.6 1.6 fusion.116
  401.9 4.2 fusion.14
  406.1 4.0 fusion.11
  410.2 5.5 %gather_fusion.7 = f32[2048,128]{1,0:T(8,128)S(1)} fusion(f32[2048,128]{1,0:T(8,128)S(1)} %fusion.11, s32[2048]{0:T(1024)S(1)} %fusion.112), kind=kCustom, calls=%fused_computation.7 | custom fusion | bytes 2105344 | tf_op jit(solution)/shard_map/gather | solution.py:128
  (107 shorter events, 33.5 us)
Async XLA Ops:
  7.2 4.1 copy-start
  7.2 35.0 %copy-start.1 = (s32[36]{0:T(128)S(1)}, s32[36]{0:T(128)}, u32[]{:S(2)}) copy-start(s32[36]{0:T(128)} %param.68) | copy-start | bytes 436
  7.2 92.3 %all-gather.4.cloned.1.call-start = ((), (), s32[]{:S(2)}) async-start(), calls=%async_computation | async-start | bytes 5308416 | tf_op jit(solution)/shard_map/all_gather | solution.py:78
  39.4 216.9 %all-gather.6.cloned.1.call-start = ((), (), s32[]{:S(2)}) async-start(), calls=%async_computation.1 | async-start | bytes 9584640 | tf_op jit(solution)/shard_map/all_gather | solution.py:89
  100.7 8.5 %copy-start.4 = (s32[2,32]{1,0:T(2,128)S(1)}, s32[2,32]{1,0:T(2,128)}, u32[]{:S(2)}) copy-start(s32[2,32]{1,0:T(2,128)} %param.69) | copy-start | bytes 772
  278.0 114.9 %collective-permute-start = (f32[32,1024]{1,0:T(8,128)S(1)}, f32[32,1024]{1,0:T(8,128)S(1)}, u32[]{:S(2)}, u32[]{:S(2)}) collective-permute-start(f32[32,1024]{1,0:T(8,128)S(1)} %select_multiply_fusion), channel_id=1, source_target_pairs={{0,1},{1,2},{2,3},{3,0},{4,5},{5,6},{6,7},{7,4},{8,9},{9,10},{10,1... | collective-permute-start | bytes 393224 | tf_op jit(solution)/shard_map/ppermute | solution.py:113
  279.2 113.7 %collective-permute-start.1 = (f32[32,1024]{1,0:T(8,128)S(1)}, f32[32,1024]{1,0:T(8,128)S(1)}, u32[]{:S(2)}, u32[]{:S(2)}) collective-permute-start(f32[32,1024]{1,0:T(8,128)S(1)} %select_multiply_fusion), channel_id=1, source_target_pairs={{0,2},{1,3},{2,0},{3,1},{4,6},{5,7},{6,4},{7,5},{8,10},{9,11},{10,... | collective-permute-start | bytes 393224 | tf_op jit(solution)/shard_map/ppermute | solution.py:113
  281.6 111.3 %collective-permute-start.2 = (f32[32,1024]{1,0:T(8,128)S(1)}, f32[32,1024]{1,0:T(8,128)S(1)}, u32[]{:S(2)}, u32[]{:S(2)}) collective-permute-start(f32[32,1024]{1,0:T(8,128)S(1)} %select_multiply_fusion), channel_id=1, source_target_pairs={{0,3},{1,0},{2,1},{3,2},{4,7},{5,4},{6,5},{7,6},{8,11},{9,8},{10,9... | collective-permute-start | bytes 393224 | tf_op jit(solution)/shard_map/ppermute | solution.py:113
  391.4 8.2 %copy-start.2 = (f32[1024,1024]{1,0:T(8,128)S(1)}, f32[1024,1024]{1,0:T(8,128)}, u32[]{:S(2)}) copy-start(f32[1024,1024]{1,0:T(8,128)} %constant_dynamic-update-slice_fusion.9) | copy-start | bytes 12582916
  410.2 5.5 %copy-start.3 = (f32[64,1,32,128]{3,2,1,0:T(8,128)S(1)}, f32[64,1,32,128]{3,2,1,0:T(8,128)}, u32[]{:S(2)}) copy-start(f32[64,1,32,128]{3,2,1,0:T(8,128)} %param.70) | copy-start | bytes 3145732
Sparse Core Ops, SparseCore 0:
  39.6 59.8 all-gather.3
  109.3 83.8 all-gather.5
